TPU v7x, 32 devices: a whole 2x2x4 slice. The times are simulated.
32 devices in a mesh: ctx: 8 (over y, x, core), tp: 4 (over z).
Axes of the slice: x: 2, y: 2, z: 4, core: 2. Of those that a mesh axis runs over, the one named last changes fastest.
Arguments:
- queries: bfloat16 [1024, 4096], P('ctx', 'tp'), may hold values from -128 to 128
- key_rows: bfloat16 [1024, 4096], P('ctx', 'tp'), may hold values from -6 to 6
- value_rows: bfloat16 [1024, 4096], P('ctx', 'tp'), may hold values from -6 to 6
- view_mask: int32 [8, 3], replicated, may hold values from 0 to 1, as said below
- norm_gain: float32 [4096], replicated, may hold values from 0.5 to 1.5
- normed_grad: bfloat16 [1024, 4096], P(('ctx', 'tp')), may hold values from -6 to 6
Outputs:
- normed: bfloat16 [1024, 4096], P(('ctx', 'tp'))
- query_grad: bfloat16 [1024, 4096], P('ctx', 'tp')
- key_grad: bfloat16 [1024, 4096], P('ctx', 'tp')
- value_grad: bfloat16 [1024, 4096], P('ctx', 'tp')
Inputs may be any that keep to these rules, and one draw needn't show every extreme that they name: `view_mask`: the blocks form views of consecutive blocks. Block 0 begins a view; otherwise a view begins only at blocks b with b % 4 equal to 2 or 3, and in every group of 4 blocks at least one of these two begins a view. A column is 1 exactly where its key block lies inside the grid of blocks and either is not later than the query block or lies in the query block's view.
All inputs are finite; a program needn't handle non-finite values.
Results may differ from a plain program's by a relative error of at most 0.012.
Values may be sent and summed in bfloat16 or wider, within the bound.
No kernel may reach another device: no remote copies, remote signals or barrier semaphores. Data moves between devices by JAX's collectives and lax.ppermute only.
A program may use at most 64 MiB of HBM per device.

v0:
```python
import jax
import jax.numpy as jnp
from jax import lax
from jax.sharding import PartitionSpec as P

HSZ = 128
REACH = 2


NEGATIVE = -1e30
EPSILON = 1e-06


def with_halo(cells, sides, width):
    for axis, dim in sides:
        count = lax.axis_size(axis)
        ends = count - 1
        head = lax.slice_in_dim(cells, 0, width, axis=dim)
        tail = lax.slice_in_dim(cells, cells.shape[dim] - width, cells.shape[dim], axis=dim)
        cells = jnp.concatenate(
            [
                lax.ppermute(tail, axis, [(i, (i + 1) % count) for i in range(ends)]),
                cells,
                lax.ppermute(head, axis, [((i + 1) % count, i) for i in range(ends)]),
            ],
            axis=dim,
        )
    return cells


def passed_along(x, axis, by):
    peers = lax.axis_size(axis)
    pairs = [(i, i + by) for i in range(peers) if 0 <= i + by < peers]
    return lax.ppermute(x, axis, pairs)


def split_heads(values):
    return values.reshape(values.shape[0], -1, HSZ)


def per_device(queries, key_rows, value_rows, view_mask, norm_gain, normed_grad):
    length = queries.shape[0]
    span_blocks = 2 * REACH - 1
    rim_rows = (REACH - 1) * length
    score_scale = HSZ ** (-0.5)
    position = lax.axis_index("ctx")
    key_ext, value_ext = (
        with_halo(key_rows, (("ctx", 0),), rim_rows),
        with_halo(value_rows, (("ctx", 0),), rim_rows),
    )
    mask_row = lax.dynamic_slice_in_dim(view_mask, position, 1, 0)[0]
    key_live = jnp.repeat(mask_row, length) > 0
    q_heads = split_heads(queries)
    k_heads = split_heads(key_ext)
    v_heads = split_heads(value_ext)
    scores = (
        jnp.einsum("thd,shd->hts", q_heads, k_heads, preferred_element_type=jnp.float32)
        * score_scale
    )
    scores = jnp.where(key_live[None, None, :], scores, NEGATIVE)
    peak = jnp.max(scores, -1, keepdims=True)
    log_total = peak + jnp.log(jnp.sum(jnp.exp(scores - peak), -1, keepdims=True))
    probs = jnp.exp(scores - log_total)
    probs_low = probs.astype(jnp.bfloat16)
    out_heads = jnp.einsum(
        "hts,shd->thd", probs_low, v_heads, preferred_element_type=jnp.float32
    ).astype(jnp.bfloat16)
    attended = out_heads.reshape(length, -1)
    tiles = lax.all_to_all(attended, "tp", split_axis=0, concat_axis=1, tiled=True)
    values_f = tiles.astype(jnp.float32)
    inverse = lax.rsqrt(jnp.mean(values_f * values_f, -1, keepdims=True) + EPSILON)
    normed = (values_f * inverse * norm_gain).astype(jnp.bfloat16)
    upstream = normed_grad.astype(jnp.float32) * norm_gain
    inner_mean = jnp.mean(upstream * values_f, -1, keepdims=True)
    tile_grad = (inverse * upstream - values_f * inverse * inverse * inverse * inner_mean).astype(
        jnp.bfloat16
    )
    attended_grad = lax.all_to_all(tile_grad, "tp", split_axis=1, concat_axis=0, tiled=True)
    grad_heads = split_heads(attended_grad)
    delta = jnp.sum(grad_heads.astype(jnp.float32) * out_heads.astype(jnp.float32), -1)
    prob_grad = jnp.einsum("thd,shd->hts", grad_heads, v_heads, preferred_element_type=jnp.float32)
    score_grad = (probs * (prob_grad - delta.T[:, :, None])).astype(jnp.bfloat16)
    query_grad = (
        (
            jnp.einsum("hts,shd->thd", score_grad, k_heads, preferred_element_type=jnp.float32)
            * score_scale
        )
        .astype(jnp.bfloat16)
        .reshape(length, -1)
    )
    key_terms = (
        jnp.einsum("hts,thd->shd", score_grad, q_heads, preferred_element_type=jnp.float32)
        * score_scale
    ).reshape(span_blocks * length, -1)
    value_terms = jnp.einsum(
        "hts,thd->shd", probs_low, grad_heads, preferred_element_type=jnp.float32
    ).reshape(span_blocks * length, -1)
    key_total = key_terms[rim_rows : rim_rows + length]
    value_total = value_terms[rim_rows : rim_rows + length]
    for column in range(span_blocks):
        if column != REACH - 1:
            offset = column - (REACH - 1)
            received = passed_along(
                (
                    key_terms[column * length : (column + 1) * length],
                    value_terms[column * length : (column + 1) * length],
                ),
                "ctx",
                offset,
            )
            key_total = key_total + received[0]
            value_total = value_total + received[1]
    return (normed, query_grad, key_total.astype(jnp.bfloat16), value_total.astype(jnp.bfloat16))


def solution(mesh):
    placed = (P("ctx", "tp"), P("ctx", "tp"), P("ctx", "tp"), P(), P(), P(("ctx", "tp"), None))
    return jax.shard_map(
        per_device,
        mesh=mesh,
        in_specs=placed,
        out_specs=(P(("ctx", "tp"), None), P("ctx", "tp"), P("ctx", "tp"), P("ctx", "tp")),
        check_vma=False,
    )
```

profile of v0, /device:TPU:1, one launch (start us, length us, event | category | flops | bytes accessed | tf_op | source)
XLA Modules:
  0.0 84.3 jit_solution(13889925027430745565)
XLA Ops:
  0.6 4.5 %collective-permute-start = (bf16[128,1024]{1,0:T(8,128)(2,1)}, bf16[128,1024]{1,0:T(8,128)(2,1)S(1)}, u32[]{:S(2)}, u32[]{:S(2)}) collective-permute-start(bf16[128,1024]{1,0:T(8,128)(2,1)} %param.8), channel_id=1, source_target_pairs={{0,4},{4,8},{8,12},{12,16},{16,20},{20,24},{24,28},{1,5},{5,9},{9,... | collective-permute-start | bytes 786440 | tf_op jit(solution)/shard_map/ppermute | solution.py:22
  5.1 1.9 %collective-permute-start.1 = (bf16[128,1024]{1,0:T(8,128)(2,1)}, bf16[128,1024]{1,0:T(8,128)(2,1)S(1)}, u32[]{:S(2)}, u32[]{:S(2)}) collective-permute-start(bf16[128,1024]{1,0:T(8,128)(2,1)} %param.8), channel_id=1, source_target_pairs={{4,0},{8,4},{12,8},{16,12},{20,16},{24,20},{28,24},{5,1},{9,5},{13... | collective-permute-start | bytes 786440 | tf_op jit(solution)/shard_map/ppermute | solution.py:24
  7.1 1.1 %copy.56 = bf16[128,1024]{0,1:T(8,128)(2,1)S(1)} copy(bf16[128,1024]{1,0:T(8,128)(2,1)} %param.7) | data formatting | bytes 524288 | tf_op args[1]
  8.2 1.9 %collective-permute-start.3 = (bf16[128,1024]{0,1:T(8,128)(2,1)S(1)}, bf16[128,1024]{0,1:T(8,128)(2,1)S(1)}, u32[]{:S(2)}, u32[]{:S(2)}) collective-permute-start(bf16[128,1024]{0,1:T(8,128)(2,1)S(1)} %copy.56), channel_id=1, source_target_pairs={{4,0},{8,4},{12,8},{16,12},{20,16},{24,20},{28,24},{5,1},{9,5},{13... | collective-permute-start | bytes 786440 | tf_op jit(solution)/shard_map/ppermute | solution.py:24
  10.1 3.6 %collective-permute-start.2 = (bf16[128,1024]{0,1:T(8,128)(2,1)S(1)}, bf16[128,1024]{0,1:T(8,128)(2,1)S(1)}, u32[]{:S(2)}, u32[]{:S(2)}) collective-permute-start(bf16[128,1024]{0,1:T(8,128)(2,1)S(1)} %copy.56), channel_id=1, source_target_pairs={{0,4},{4,8},{8,12},{12,16},{16,20},{20,24},{24,28},{1,5},{5,9},{9,... | collective-permute-start | bytes 786440 | tf_op jit(solution)/shard_map/ppermute | solution.py:22
  13.8 1.1 %copy.91 = bf16[128,1024]{0,1:T(8,128)(2,1)S(1)} copy(bf16[128,1024]{1,0:T(8,128)(2,1)} %param.6) | data formatting | bytes 524288 | tf_op jit(solution)/shard_map/reshape | solution.py:38
  15.9 1.0 %pad_maximum_fusion = bf16[384,1024]{1,0:T(8,128)(2,1)S(1)} fusion(bf16[128,1024]{1,0:T(8,128)(2,1)S(1)} %collective-permute-done.1, bf16[128,1024]{1,0:T(8,128)(2,1)} %param.8, bf16[128,1024]{1,0:T(8,128)(2,1)S(1)} %collective-permute-done), kind=kLoop, calls=%fused_computation.15 | loop fusion | flops 2359296 | bytes 1572864 | tf_op jit(solution)/shard_map/concatenate | solution.py:20
  19.0 13.1 %all_to_all.29 = bf16[4,32,1024]{2,1,0:T(8,128)(2,1)S(1)} all-to-all(bf16[4,32,1024]{2,1,0:T(8,128)(2,1)S(1)} %all_to_all.22), channel_id=1, replica_groups=mesh['ctx'=8,'tp'=4] {'tp'}, dimensions={0} | all-to-all | bytes 524288 | tf_op jit(solution)/shard_map/all_to_all | solution.py:69
  32.5 0.9 %subtract_convert_fusion = (bf16[32,4096]{1,0:T(8,128)(2,1)S(1)}, bf16[32,4096]{1,0:T(8,128)(2,1)}) fusion(bf16[32,4096]{1,0:T(8,128)(2,1)S(1)} %copy-done.9, f32[32,4096]{1,0:T(8,128)S(1)} %bitcast.69, f32[32]{0:T(128)S(1)} %get-tuple-element.27, f32[4096]{0:T(1024)S(1)} %copy-done.10, f32[32]{0:T(128)S(1)} %get-tuple-element.26), kind=kLoop, calls=%fused_computation.25 | loop fusion | flops 1441792 | bytes 1327360 | tf_op jit(solution)/shard_map/convert_element_type | solution.py:75
  33.5 9.6 %all_to_all.30 = bf16[32,4,1024]{2,0,1:T(8,128)(2,1)S(1)} all-to-all(bf16[32,4,1024]{2,0,1:T(8,128)(2,1)S(1)} %bitcast.76), channel_id=1, replica_groups=mesh['ctx'=8,'tp'=4] {'tp'}, dimensions={1} | all-to-all | bytes 524288 | tf_op jit(solution)/shard_map/all_to_all | solution.py:78
  43.5 1.6 %convolution_bitcast_fusion = f32[384,8,128]{0,2,1:T(8,128)} fusion(bf16[128,8,128]{0,2,1:T(8,128)(2,1)S(1)} %copy.67, f32[8,384,128]{2,1,0:T(8,128)S(1)} %get-tuple-element.25, f32[8,128]{1,0:T(8,128)S(1)} %log_add_fusion), kind=kOutput, calls=%fused_computation.9 | convolution fusion | flops 101449728 | bytes 3411968 | tf_op jit(solution)/shard_map/hts,thd->shd/dot_general | solution.py:95
  46.4 1.2 %fusion.13 = (f32[128,8,128]{2,0,1:T(8,128)}, f32[128,8,128]{2,0,1:T(8,128)}, f32[128,8,128]{2,0,1:T(8,128)}) fusion(f32[384,8,128]{2,0,1:T(8,128)S(1)} %multiply_bitcast_fusion), kind=kLoop, calls=%fused_computation.37 | loop fusion | bytes 3145728 | tf_op jit(solution)/shard_map/slice | solution.py:98
  47.6 2.2 %copy.75 = f32[128,8,128]{0,2,1:T(8,128)} copy(f32[128,8,128]{2,0,1:T(8,128)} %get-tuple-element.20) | data formatting | bytes 1048576 | tf_op jit(solution)/shard_map/slice | solution.py:105
  49.8 2.0 %copy.74 = f32[128,8,128]{0,2,1:T(8,128)} copy(f32[128,8,128]{2,0,1:T(8,128)} %get-tuple-element.21) | data formatting | bytes 1048576 | tf_op jit(solution)/shard_map/slice | solution.py:105
  51.8 4.5 %collective-permute-start.4 = (f32[128,1024]{0,1:T(8,128)}, f32[128,1024]{0,1:T(8,128)}, u32[]{:S(2)}, u32[]{:S(2)}) collective-permute-start(f32[128,1024]{0,1:T(8,128)} %bitcast.81), channel_id=1, source_target_pairs={{4,0},{8,4},{12,8},{16,12},{20,16},{24,20},{28,24},{5,1},{9,5},{13... | collective-permute-start | bytes 1572872 | tf_op jit(solution)/shard_map/ppermute | solution.py:34
  56.4 3.9 %collective-permute-start.5 = (f32[128,1024]{0,1:T(8,128)}, f32[128,1024]{0,1:T(8,128)}, u32[]{:S(2)}, u32[]{:S(2)}) collective-permute-start(f32[128,1024]{0,1:T(8,128)} %bitcast.80), channel_id=1, source_target_pairs={{0,4},{4,8},{8,12},{12,16},{16,20},{20,24},{24,28},{1,5},{5,9},{9,... | collective-permute-start | bytes 1572872 | tf_op jit(solution)/shard_map/ppermute | solution.py:34
  60.3 1.2 %fusion.12 = (f32[128,8,128]{0,2,1:T(8,128)}, f32[128,8,128]{0,2,1:T(8,128)}, f32[128,8,128]{0,2,1:T(8,128)}) fusion(f32[384,8,128]{0,2,1:T(8,128)S(1)} %copy-done.2), kind=kLoop, calls=%fused_computation.36 | loop fusion | bytes 3145728 | tf_op jit(solution)/shard_map/slice | solution.py:106
  61.4 2.0 %copy.78 = f32[128,1024]{1,0:T(8,128)} copy(f32[128,1024]{0,1:T(8,128)} %bitcast.74) | data formatting | bytes 1048576 | tf_op jit(solution)/shard_map/slice | solution.py:106
  63.5 2.1 %copy.80 = f32[128,1024]{1,0:T(8,128)} copy(f32[128,1024]{0,1:T(8,128)} %bitcast.73) | data formatting | bytes 1048576 | tf_op jit(solution)/shard_map/slice | solution.py:106
  65.6 2.5 %collective-permute-start.7 = (f32[128,1024]{1,0:T(8,128)}, f32[128,1024]{1,0:T(8,128)}, u32[]{:S(2)}, u32[]{:S(2)}) collective-permute-start(f32[128,1024]{1,0:T(8,128)} %copy.80), channel_id=1, source_target_pairs={{0,4},{4,8},{8,12},{12,16},{16,20},{20,24},{24,28},{1,5},{5,9},{9,... | collective-permute-start | bytes 1572872 | tf_op jit(solution)/shard_map/ppermute | solution.py:34
  68.1 2.7 %collective-permute-start.6 = (f32[128,1024]{1,0:T(8,128)}, f32[128,1024]{1,0:T(8,128)}, u32[]{:S(2)}, u32[]{:S(2)}) collective-permute-start(f32[128,1024]{1,0:T(8,128)} %copy.78), channel_id=1, source_target_pairs={{4,0},{8,4},{12,8},{16,12},{20,16},{24,20},{28,24},{5,1},{9,5},{13... | collective-permute-start | bytes 1572872 | tf_op jit(solution)/shard_map/ppermute | solution.py:34
  72.5 1.3 %fusion.8 = bf16[128,1024]{0,1:T(8,128)(2,1)S(1)} fusion(f32[128,1024]{0,1:T(8,128)} %collective-permute-done.5, f32[128,1024]{0,1:T(8,128)} %collective-permute-done.4, f32[128,8,128]{0,2,1:T(8,128)S(1)} %copy.73), kind=kLoop, calls=%fused_computation.22 | loop fusion | flops 393216 | bytes 1835008 | tf_op jit(solution)/shard_map/convert_element_type | solution.py:113
  74.6 7.7 %collective-permute-done.6 = f32[128,1024]{1,0:T(8,128)} collective-permute-done((f32[128,1024]{1,0:T(8,128)}, f32[128,1024]{1,0:T(8,128)}, u32[]{:S(2)}, u32[]{:S(2)}) %collective-permute-start.6) | collective-permute-done | bytes 524320 | tf_op jit(solution)/shard_map/ppermute | solution.py:34
  82.3 2.0 %add_convert_fusion = bf16[128,1024]{1,0:T(8,128)(2,1)} fusion(f32[128,1024]{1,0:T(8,128)} %collective-permute-done.7, f32[128,1024]{1,0:T(8,128)S(1)} %copy.79, f32[128,1024]{1,0:T(8,128)} %collective-permute-done.6), kind=kLoop, calls=%fused_computation.23 | loop fusion | flops 393216 | bytes 1835008 | tf_op jit(solution)/shard_map/convert_element_type | solution.py:113
  (55 shorter events, 7.6 us)
Async XLA Ops:
  0.6 15.3 %collective-permute-start = (bf16[128,1024]{1,0:T(8,128)(2,1)}, bf16[128,1024]{1,0:T(8,128)(2,1)S(1)}, u32[]{:S(2)}, u32[]{:S(2)}) collective-permute-start(bf16[128,1024]{1,0:T(8,128)(2,1)} %param.8), channel_id=1, source_target_pairs={{0,4},{4,8},{8,12},{12,16},{16,20},{20,24},{24,28},{1,5},{5,9},{9,... | collective-permute-start | bytes 786440 | tf_op jit(solution)/shard_map/ppermute | solution.py:22
  5.1 10.8 %collective-permute-start.1 = (bf16[128,1024]{1,0:T(8,128)(2,1)}, bf16[128,1024]{1,0:T(8,128)(2,1)S(1)}, u32[]{:S(2)}, u32[]{:S(2)}) collective-permute-start(bf16[128,1024]{1,0:T(8,128)(2,1)} %param.8), channel_id=1, source_target_pairs={{4,0},{8,4},{12,8},{16,12},{20,16},{24,20},{28,24},{5,1},{9,5},{13... | collective-permute-start | bytes 786440 | tf_op jit(solution)/shard_map/ppermute | solution.py:24
  8.2 9.1 %collective-permute-start.3 = (bf16[128,1024]{0,1:T(8,128)(2,1)S(1)}, bf16[128,1024]{0,1:T(8,128)(2,1)S(1)}, u32[]{:S(2)}, u32[]{:S(2)}) collective-permute-start(bf16[128,1024]{0,1:T(8,128)(2,1)S(1)} %copy.56), channel_id=1, source_target_pairs={{4,0},{8,4},{12,8},{16,12},{20,16},{24,20},{28,24},{5,1},{9,5},{13... | collective-permute-start | bytes 786440 | tf_op jit(solution)/shard_map/ppermute | solution.py:24
  10.1 7.2 %collective-permute-start.2 = (bf16[128,1024]{0,1:T(8,128)(2,1)S(1)}, bf16[128,1024]{0,1:T(8,128)(2,1)S(1)}, u32[]{:S(2)}, u32[]{:S(2)}) collective-permute-start(bf16[128,1024]{0,1:T(8,128)(2,1)S(1)} %copy.56), channel_id=1, source_target_pairs={{0,4},{4,8},{8,12},{12,16},{16,20},{20,24},{24,28},{1,5},{5,9},{9,... | collective-permute-start | bytes 786440 | tf_op jit(solution)/shard_map/ppermute | solution.py:22
  14.9 2.5 %copy-start.3 = (bf16[128,1024]{0,1:T(8,128)(2,1)}, bf16[128,1024]{0,1:T(8,128)(2,1)S(1)}, u32[]{:S(2)}) copy-start(bf16[128,1024]{0,1:T(8,128)(2,1)S(1)} %copy.91) | copy-start | bytes 786436
  17.3 0.9 %copy-start = (bf16[384,1024]{0,1:T(8,128)(2,1)}, bf16[384,1024]{0,1:T(8,128)(2,1)S(1)}, u32[]{:S(2)}) copy-start(bf16[384,1024]{0,1:T(8,128)(2,1)S(1)} %copy.55) | copy-start | bytes 2359300
  18.6 13.5 %copy-start.5 = (bf16[128,8,128]{0,2,1:T(8,128)(2,1)}, bf16[128,8,128]{0,2,1:T(8,128)(2,1)S(1)}, u32[]{:S(2)}) copy-start(bf16[128,8,128]{0,2,1:T(8,128)(2,1)S(1)} %fusion.5) | copy-start | bytes 786436
  18.8 13.3 %copy-start.9 = (bf16[32,4096]{1,0:T(8,128)(2,1)S(1)}, bf16[32,4096]{1,0:T(8,128)(2,1)}, u32[]{:S(2)}) copy-start(bf16[32,4096]{1,0:T(8,128)(2,1)} %param.11) | copy-start | bytes 786436
  18.8 13.3 %copy-start.10 = (f32[4096]{0:T(1024)S(1)}, f32[4096]{0:T(1024)}, u32[]{:S(2)}) copy-start(f32[4096]{0:T(1024)} %param.10) | copy-start | bytes 49156
  32.5 10.8 %copy-start.6 = (bf16[128,8,128]{0,2,1:T(8,128)(2,1)S(1)}, bf16[128,8,128]{0,2,1:T(8,128)(2,1)}, u32[]{:S(2)}) copy-start(bf16[128,8,128]{0,2,1:T(8,128)(2,1)} %copy-done.5) | copy-start | bytes 786436
  43.5 1.6 %copy-start.1 = (bf16[384,1024]{0,1:T(8,128)(2,1)S(1)}, bf16[384,1024]{0,1:T(8,128)(2,1)}, u32[]{:S(2)}) copy-start(bf16[384,1024]{0,1:T(8,128)(2,1)} %copy-done) | copy-start | bytes 2359300
  45.1 1.0 %copy-start.4 = (bf16[128,1024]{0,1:T(8,128)(2,1)S(1)}, bf16[128,1024]{0,1:T(8,128)(2,1)}, u32[]{:S(2)}) copy-start(bf16[128,1024]{0,1:T(8,128)(2,1)} %copy-done.3) | copy-start | bytes 786436
  47.6 12.6 %copy-start.2 = (f32[384,8,128]{0,2,1:T(8,128)S(1)}, f32[384,8,128]{0,2,1:T(8,128)}, u32[]{:S(2)}) copy-start(f32[384,8,128]{0,2,1:T(8,128)} %convolution_bitcast_fusion) | copy-start | bytes 4718596
  51.8 20.6 %collective-permute-start.4 = (f32[128,1024]{0,1:T(8,128)}, f32[128,1024]{0,1:T(8,128)}, u32[]{:S(2)}, u32[]{:S(2)}) collective-permute-start(f32[128,1024]{0,1:T(8,128)} %bitcast.81), channel_id=1, source_target_pairs={{4,0},{8,4},{12,8},{16,12},{20,16},{24,20},{28,24},{5,1},{9,5},{13... | collective-permute-start | bytes 1572872 | tf_op jit(solution)/shard_map/ppermute | solution.py:34
  56.4 16.1 %collective-permute-start.5 = (f32[128,1024]{0,1:T(8,128)}, f32[128,1024]{0,1:T(8,128)}, u32[]{:S(2)}, u32[]{:S(2)}) collective-permute-start(f32[128,1024]{0,1:T(8,128)} %bitcast.80), channel_id=1, source_target_pairs={{0,4},{4,8},{8,12},{12,16},{16,20},{20,24},{24,28},{1,5},{5,9},{9,... | collective-permute-start | bytes 1572872 | tf_op jit(solution)/shard_map/ppermute | solution.py:34
  63.5 8.6 %copy-start.8 = (f32[128,8,128]{0,2,1:T(8,128)S(1)}, f32[128,8,128]{0,2,1:T(8,128)}, u32[]{:S(2)}) copy-start(f32[128,8,128]{0,2,1:T(8,128)} %get-tuple-element.18) | copy-start | bytes 1572868
  65.6 6.7 %copy-start.7 = (f32[128,8,128]{2,0,1:T(8,128)S(1)}, f32[128,8,128]{2,0,1:T(8,128)}, u32[]{:S(2)}) copy-start(f32[128,8,128]{2,0,1:T(8,128)} %get-tuple-element.19) | copy-start | bytes 1572868
  65.6 9.1 %collective-permute-start.7 = (f32[128,1024]{1,0:T(8,128)}, f32[128,1024]{1,0:T(8,128)}, u32[]{:S(2)}, u32[]{:S(2)}) collective-permute-start(f32[128,1024]{1,0:T(8,128)} %copy.80), channel_id=1, source_target_pairs={{0,4},{4,8},{8,12},{12,16},{16,20},{20,24},{24,28},{1,5},{5,9},{9,... | collective-permute-start | bytes 1572872 | tf_op jit(solution)/shard_map/ppermute | solution.py:34
  68.1 14.2 %collective-permute-start.6 = (f32[128,1024]{1,0:T(8,128)}, f32[128,1024]{1,0:T(8,128)}, u32[]{:S(2)}, u32[]{:S(2)}) collective-permute-start(f32[128,1024]{1,0:T(8,128)} %copy.78), channel_id=1, source_target_pairs={{4,0},{8,4},{12,8},{16,12},{20,16},{24,20},{28,24},{5,1},{9,5},{13... | collective-permute-start | bytes 1572872 | tf_op jit(solution)/shard_map/ppermute | solution.py:34
where the time goes:
time: 85.1 us; the launch traced here: 84.3 us
  starting transfers between devices  25.6 us (30%)
  blocking collectives  22.7 us (27%)
  local copies, waits for them, and re-layouts  16.6 us (20%)
  waiting for transfers between devices  7.74 us (9%)
  other arithmetic  6.92 us (8%)
  matrix products  3.83 us (5%)
  between operations  1.01 us (1%)
    ppermute x4, starting transfers between devices, passed_along(): return lax.ppermute(x, axis, pairs)  13.6 us
    all_to_all x1, blocking collectives, per_device(): lax.all_to_all(attended, 'tp', split_axis=0, concat_axis=1, tiled=True)  13.1 us
    all_to_all x1, blocking collectives, per_device(): lax.all_to_all(tile_grad, 'tp', split_axis=1, concat_axis=0, tiled=True)  9.59 us
    ppermute x2, starting transfers between devices, with_halo(): lax.ppermute(tail, axis, [(i, (i + 1) % count) for i in range(ends)])  8.15 us
    ppermute x4, waiting for transfers between devices, passed_along(): return lax.ppermute(x, axis, pairs)  7.73 us
    slice x3, local copies, waits for them, and re-layouts, per_device(): value_terms[column * length:(column + 1) * length]  5.3 us
    slice x2, local copies, waits for them, and re-layouts, per_device(): key_terms[column * length:(column + 1) * length]  4.2 us
    ppermute x2, starting transfers between devices, with_halo(): lax.ppermute(head, axis, [((i + 1) % count, i) for i in range(ends)])  3.84 us
  transfers between devices with their start and end apart: 8, of which 1 were waited for; matrix products, arithmetic and copies ran while one was open for 16% of the time, Pallas kernels for 0%

commit v1 on v0

v1 whole, which is shorter than its diff:
```python
import jax
import jax.numpy as jnp
from jax import lax
from jax.sharding import PartitionSpec as P

HSZ = 128
REACH = 2


NEGATIVE = -1e30
EPSILON = 1e-06
STATS_SUM = "a2a"


def passed_along(x, axis, by):
    peers = lax.axis_size(axis)
    pairs = [(i, i + by) for i in range(peers) if 0 <= i + by < peers]
    return lax.ppermute(x, axis, pairs)


def split_heads(values):
    return values.reshape(values.shape[0], -1, HSZ)


def tp_sum(stats):
    if STATS_SUM == "psum":
        return lax.psum(stats, "tp")
    peers = lax.axis_size("tp")
    if STATS_SUM == "a2a":
        spread = jnp.broadcast_to(stats[None], (peers,) + stats.shape)
        gathered = lax.all_to_all(spread, "tp", split_axis=0, concat_axis=0, tiled=True)
        return jnp.sum(gathered, 0)
    total = stats
    for shift in range(1, peers):
        total = total + lax.ppermute(stats, "tp", [(i, (i + shift) % peers) for i in range(peers)])
    return total


def per_device(queries, key_rows, value_rows, view_mask, norm_gain, normed_grad):
    length = queries.shape[0]
    width = queries.shape[1]
    features = norm_gain.shape[0]
    span_blocks = 2 * REACH - 1
    score_scale = HSZ ** (-0.5)
    position = lax.axis_index("ctx")
    part = lax.axis_index("tp")

    grad_tiles = lax.all_to_all(normed_grad, "tp", split_axis=1, concat_axis=0, tiled=True)
    gain_local = lax.dynamic_slice_in_dim(norm_gain, part * width, width, 0)

    both = jnp.concatenate([key_rows, value_rows], axis=1)
    from_prev = passed_along(both, "ctx", 1)
    from_next = passed_along(both, "ctx", -1)
    key_ext = jnp.concatenate([from_prev[:, :width], key_rows, from_next[:, :width]], axis=0)
    value_ext = jnp.concatenate([from_prev[:, width:], value_rows, from_next[:, width:]], axis=0)

    mask_row = lax.dynamic_slice_in_dim(view_mask, position, 1, 0)[0]
    key_live = jnp.repeat(mask_row, length) > 0
    q_heads = split_heads(queries)
    k_heads = split_heads(key_ext)
    v_heads = split_heads(value_ext)
    scores = (
        jnp.einsum("thd,shd->hts", q_heads, k_heads, preferred_element_type=jnp.float32)
        * score_scale
    )
    scores = jnp.where(key_live[None, None, :], scores, NEGATIVE)
    peak = jnp.max(scores, -1, keepdims=True)
    log_total = peak + jnp.log(jnp.sum(jnp.exp(scores - peak), -1, keepdims=True))
    probs = jnp.exp(scores - log_total)
    probs_low = probs.astype(jnp.bfloat16)
    out_heads = jnp.einsum(
        "hts,shd->thd", probs_low, v_heads, preferred_element_type=jnp.float32
    ).astype(jnp.bfloat16)
    attended = out_heads.reshape(length, -1)

    values_f = attended.astype(jnp.float32)
    upstream = grad_tiles.astype(jnp.float32) * gain_local
    partial = jnp.stack(
        [jnp.sum(values_f * values_f, -1), jnp.sum(upstream * values_f, -1)], axis=-1
    )
    totals = tp_sum(partial)
    inverse = lax.rsqrt(totals[:, 0:1] / features + EPSILON)
    inner_mean = totals[:, 1:2] / features
    normed_heads = (values_f * inverse * gain_local).astype(jnp.bfloat16)
    normed = lax.all_to_all(normed_heads, "tp", split_axis=0, concat_axis=1, tiled=True)
    attended_grad = (
        inverse * upstream - values_f * inverse * inverse * inverse * inner_mean
    ).astype(jnp.bfloat16)

    grad_heads = split_heads(attended_grad)
    delta = jnp.sum(grad_heads.astype(jnp.float32) * out_heads.astype(jnp.float32), -1)
    prob_grad = jnp.einsum("thd,shd->hts", grad_heads, v_heads, preferred_element_type=jnp.float32)
    score_grad = (probs * (prob_grad - delta.T[:, :, None])).astype(jnp.bfloat16)
    query_grad = (
        (
            jnp.einsum("hts,shd->thd", score_grad, k_heads, preferred_element_type=jnp.float32)
            * score_scale
        )
        .astype(jnp.bfloat16)
        .reshape(length, -1)
    )
    key_terms = (
        jnp.einsum("hts,thd->shd", score_grad, q_heads, preferred_element_type=jnp.float32)
        * score_scale
    ).reshape(span_blocks * length, -1)
    value_terms = jnp.einsum(
        "hts,thd->shd", probs_low, grad_heads, preferred_element_type=jnp.float32
    ).reshape(span_blocks * length, -1)
    terms = jnp.concatenate([key_terms, value_terms], axis=1)
    total = terms[length : 2 * length]
    to_prev = terms[:length].astype(jnp.bfloat16)
    to_next = terms[2 * length :].astype(jnp.bfloat16)
    total = total + passed_along(to_prev, "ctx", -1).astype(jnp.float32)
    total = total + passed_along(to_next, "ctx", 1).astype(jnp.float32)
    total = total.astype(jnp.bfloat16)
    return (normed, query_grad, total[:, :width], total[:, width:])


def solution(mesh):
    placed = (P("ctx", "tp"), P("ctx", "tp"), P("ctx", "tp"), P(), P(), P(("ctx", "tp"), None))
    return jax.shard_map(
        per_device,
        mesh=mesh,
        in_specs=placed,
        out_specs=(P(("ctx", "tp"), None), P("ctx", "tp"), P("ctx", "tp"), P("ctx", "tp")),
        check_vma=False,
    )
```

time: 85.1 us -> 68.4 us (0.80)
  the two profiles are of different devices: /device:TPU:1 before, /device:TPU:4 now
where the time goes in v1:
time: 68.4 us; the launch traced here: 67.4 us
  starting transfers between devices  22.8 us (33%)
  local copies, waits for them, and re-layouts  16.6 us (24%)
  waiting for transfers between devices  16.3 us (24%)
  matrix products  7.25 us (11%)
  other arithmetic  3.49 us (5%)
  between operations  0.93 us (1%)
    ppermute x4, starting transfers between devices, passed_along(): return lax.ppermute(x, axis, pairs)  9.02 us
    all_to_all x1, waiting for transfers between devices, per_device(): lax.all_to_all(normed_heads, 'tp', split_axis=0, concat_axis=1, tiled=True)  7.64 us
    unnamed x24, local copies, waits for them, and re-layouts  6.8 us
    ppermute x4, waiting for transfers between devices, passed_along(): return lax.ppermute(x, axis, pairs)  5.27 us
    all_to_all x1, starting transfers between devices, per_device(): lax.all_to_all(normed_grad, 'tp', split_axis=1, concat_axis=0, tiled=True)  4.87 us
    all_to_all x1, starting transfers between devices, tp_sum(): lax.all_to_all(spread, 'tp', split_axis=0, concat_axis=0, tiled=True)  4.87 us
    all_to_all x1, starting transfers between devices, per_device(): lax.all_to_all(normed_heads, 'tp', split_axis=0, concat_axis=1, tiled=True)  4.05 us
    all_to_all x1, waiting for transfers between devices, tp_sum(): lax.all_to_all(spread, 'tp', split_axis=0, concat_axis=0, tiled=True)  3.38 us
  transfers between devices with their start and end apart: 7, of which 4 were waited for; matrix products, arithmetic and copies ran while one was open for 18% of the time, Pallas kernels for 0%

profile of v1, /device:TPU:4, one launch (start us, length us, event | category | flops | bytes accessed | tf_op | source)
XLA Modules:
  0.0 67.4 jit_solution(5957752640084259469)
XLA Ops:
  0.7 1.2 %copy.73 = bf16[128,1024]{0,1:T(8,128)(2,1)S(1)} copy(bf16[128,1024]{1,0:T(8,128)(2,1)} %param.7) | data formatting | bytes 524288 | tf_op args[1]
  1.9 1.1 %copy.74 = bf16[128,1024]{0,1:T(8,128)(2,1)S(1)} copy(bf16[128,1024]{1,0:T(8,128)(2,1)} %param.8) | data formatting | bytes 524288 | tf_op args[2]
  3.0 2.8 %collective-permute-start.1 = (bf16[128,2048]{0,1:T(8,128)(2,1)S(1)}, bf16[128,2048]{0,1:T(8,128)(2,1)S(1)}, u32[]{:S(2)}, u32[]{:S(2)}) collective-permute-start(bf16[128,2048]{0,1:T(8,128)(2,1)S(1)} %pad_maximum_fusion.3), channel_id=1, source_target_pairs={{4,0},{8,4},{12,8},{16,12},{20,16},{24,20},{28,24},{5,1},{9,5},{13... | collective-permute-start | bytes 1572872 | tf_op jit(solution)/shard_map/ppermute | solution.py:18
  5.8 1.9 %collective-permute-start = (bf16[128,2048]{0,1:T(8,128)(2,1)S(1)}, bf16[128,2048]{0,1:T(8,128)(2,1)S(1)}, u32[]{:S(2)}, u32[]{:S(2)}) collective-permute-start(bf16[128,2048]{0,1:T(8,128)(2,1)S(1)} %pad_maximum_fusion.3), channel_id=1, source_target_pairs={{0,4},{4,8},{8,12},{12,16},{16,20},{20,24},{24,28},{1,5},{5,9},{9,... | collective-permute-start | bytes 1572872 | tf_op jit(solution)/shard_map/ppermute | solution.py:18
  8.5 4.9 %all-to-all-start = ((bf16[32,4,1024]{2,0,1:T(8,128)(2,1)}), bf16[32,4,1024]{2,0,1:T(8,128)(2,1)S(1)}, u32[]{:S(2)}, u32[]{:S(2)}) async-start(bf16[32,4,1024]{2,0,1:T(8,128)(2,1)} %bitcast.66), calls=%async_computation | async-start | bytes 524288 | tf_op jit(solution)/shard_map/all_to_all | solution.py:48
  13.8 2.2 %collective-permute-done.1 = bf16[128,2048]{0,1:T(8,128)(2,1)S(1)} collective-permute-done((bf16[128,2048]{0,1:T(8,128)(2,1)S(1)}, bf16[128,2048]{0,1:T(8,128)(2,1)S(1)}, u32[]{:S(2)}, u32[]{:S(2)}) %collective-permute-start.1) | collective-permute-done | bytes 524320 | tf_op jit(solution)/shard_map/ppermute | solution.py:18
  16.1 3.0 %collective-permute-done = bf16[128,2048]{0,1:T(8,128)(2,1)S(1)} collective-permute-done((bf16[128,2048]{0,1:T(8,128)(2,1)S(1)}, bf16[128,2048]{0,1:T(8,128)(2,1)S(1)}, u32[]{:S(2)}, u32[]{:S(2)}) %collective-permute-start) | collective-permute-done | bytes 524320 | tf_op jit(solution)/shard_map/ppermute | solution.py:18
  21.0 1.0 %copy.80 = f32[128,8,128]{2,1,0:T(8,128)} copy(f32[128,8,128]{0,2,1:T(8,128)S(1)} %get-tuple-element.36) | data formatting | bytes 1048576 | tf_op jit(solution)/shard_map/convert_element_type | solution.py:76
  22.0 1.1 %reshape.114 = f32[4,32,1024]{2,1,0:T(8,128)S(1)} reshape(f32[128,8,128]{2,1,0:T(8,128)} %copy.80) | data formatting | bytes 1048576 | tf_op jit(solution)/shard_map/convert_element_type | solution.py:76
  24.0 4.9 %all-to-all-start.1 = ((f32[4,128,2]{1,2,0:T(2,128)}), f32[4,128,2]{1,2,0:T(2,128)S(1)}, u32[]{:S(2)}, u32[]{:S(2)}) async-start(f32[4,128,2]{1,2,0:T(2,128)} %broadcast_in_dim.30), calls=%async_computation.1 | async-start | bytes 8192 | tf_op jit(solution)/shard_map/all_to_all | solution.py:31
  28.9 0.9 %copy.108 = f32[16,8,8,128]{3,2,1,0:T(8,128)} copy(f32[16,8,8,128]{3,1,2,0:T(8,128)S(1)} %bitcast.77) | data formatting | bytes 1048576
  29.8 1.2 %copy.83 = f32[128,8,128]{0,2,1:T(8,128)S(1)} copy(f32[128,8,128]{2,1,0:T(8,128)} %bitcast.78) | data formatting | bytes 1048576 | tf_op jit(solution)/shard_map/convert_element_type | solution.py:77
  31.1 3.4 %all-to-all-done.1 = f32[4,128,2]{1,2,0:T(2,128)S(1)} async-done(((f32[4,128,2]{1,2,0:T(2,128)}), f32[4,128,2]{1,2,0:T(2,128)S(1)}, u32[]{:S(2)}, u32[]{:S(2)}) %all-to-all-start.1) | async-done | bytes 4128 | tf_op jit(solution)/shard_map/all_to_all | solution.py:31
  35.9 1.4 %multiply_convert_fusion = bf16[8,128,384]{1,2,0:T(8,128)(2,1)} fusion(bf16[128,8,128]{0,2,1:T(8,128)(2,1)S(1)} %get-tuple-element.21, bf16[384,8,128]{0,2,1:T(8,128)(2,1)S(1)} %bitcast.74, f32[8,384,128]{2,1,0:T(8,128)S(1)} %get-tuple-element.34, f32[8,128]{1,0:T(8,128)S(1)} %bitcast.82, f32[8,128]{1,0:T(8,128)S(1)} %log_add_fusion), kind=kOutput, calls=%fused_computation.11 | convolution fusion | flops 102236160 | bytes 3416064 | tf_op jit(solution)/shard_map/thd,shd->hts/dot_general | solution.py:92
  37.3 2.7 %multiply_bitcast_fusion = f32[384,8,128]{2,0,1:T(8,128)} fusion(bf16[8,128,384]{1,2,0:T(8,128)(2,1)} %multiply_convert_fusion, bf16[128,8,128]{0,2,1:T(8,128)(2,1)S(1)} %bitcast.76), kind=kOutput, calls=%fused_computation.10 | convolution fusion | flops 101056512 | bytes 2621440 | tf_op jit(solution)/shard_map/hts,thd->shd/dot_general | solution.py:103
  40.0 1.9 %copy.91 = f32[384,8,128]{0,2,1:T(8,128)S(1)} copy(f32[384,8,128]{2,0,1:T(8,128)} %multiply_bitcast_fusion) | data formatting | bytes 3145728 | tf_op jit(solution)/shard_map/mul | solution.py:103
  42.1 1.0 %fusion.19 = (bf16[128,2048]{0,1:T(8,128)(2,1)}, bf16[128,2048]{0,1:T(8,128)(2,1)}) fusion(bf16[384,2048]{0,1:T(8,128)(2,1)S(1)} %fusion), kind=kLoop, calls=%fused_computation.43 | loop fusion | bytes 2097152 | tf_op jit(solution)/shard_map/slice | solution.py:111
  43.1 1.9 %collective-permute-start.2 = (bf16[128,2048]{0,1:T(8,128)(2,1)}, bf16[128,2048]{0,1:T(8,128)(2,1)}, u32[]{:S(2)}, u32[]{:S(2)}) collective-permute-start(bf16[128,2048]{0,1:T(8,128)(2,1)} %get-tuple-element.22), channel_id=1, source_target_pairs={{4,0},{8,4},{12,8},{16,12},{20,16},{24,20},{28,24},{5,1},{9,5},{13... | collective-permute-start | bytes 1572872 | tf_op jit(solution)/shard_map/ppermute | solution.py:18
  45.0 2.4 %collective-permute-start.3 = (bf16[128,2048]{0,1:T(8,128)(2,1)}, bf16[128,2048]{0,1:T(8,128)(2,1)}, u32[]{:S(2)}, u32[]{:S(2)}) collective-permute-start(bf16[128,2048]{0,1:T(8,128)(2,1)} %get-tuple-element.23), channel_id=1, source_target_pairs={{0,4},{4,8},{8,12},{12,16},{16,20},{20,24},{24,28},{1,5},{5,9},{9,... | collective-permute-start | bytes 1572872 | tf_op jit(solution)/shard_map/ppermute | solution.py:18
  48.3 4.1 %all-to-all-start.2 = ((bf16[4,32,1024]{2,1,0:T(8,128)(2,1)}), bf16[4,32,1024]{2,1,0:T(8,128)(2,1)}, u32[]{:S(2)}, u32[]{:S(2)}) async-start(bf16[4,32,1024]{2,1,0:T(8,128)(2,1)} %multiply_convert_fusion.1), calls=%async_computation.2 | async-start | bytes 524288 | tf_op jit(solution)/shard_map/all_to_all | solution.py:85
  52.3 1.7 %fusion.5 = bf16[8,128,128]{2,1,0:T(8,128)(2,1)S(1)} fusion(bf16[384,8,128]{0,2,1:T(8,128)(2,1)} %bitcast.72, bf16[8,128,384]{1,2,0:T(8,128)(2,1)} %multiply_convert_fusion), kind=kOutput, calls=%fused_computation.15 | convolution fusion | flops 100925440 | bytes 1835008 | tf_op jit(solution)/shard_map/hts,shd->thd/dot_general | solution.py:96
  54.9 7.6 %all-to-all-done.2 = bf16[4,32,1024]{2,1,0:T(8,128)(2,1)} async-done(((bf16[4,32,1024]{2,1,0:T(8,128)(2,1)}), bf16[4,32,1024]{2,1,0:T(8,128)(2,1)}, u32[]{:S(2)}, u32[]{:S(2)}) %all-to-all-start.2) | async-done | bytes 262176 | tf_op jit(solution)/shard_map/all_to_all | solution.py:85
  62.6 1.7 %copy.107 = bf16[4,4,8,1024]{3,2,0,1:T(8,128)(2,1)} copy(bf16[4,4,8,1024]{3,2,1,0:T(8,128)(2,1)} %bitcast.24) | data formatting | bytes 524288 | tf_op jit(solution)/shard_map/all_to_all | solution.py:85
  64.3 1.4 %fusion.11 = bf16[128,2048]{0,1:T(8,128)(2,1)S(1)} fusion(f32[384,1024]{0,1:T(8,128)S(1)} %bitcast.68, f32[384,1024]{0,1:T(8,128)S(1)} %bitcast.70, bf16[128,2048]{0,1:T(8,128)(2,1)} %collective-permute-done.3, bf16[128,2048]{0,1:T(8,128)(2,1)} %collective-permute-done.2), kind=kLoop, calls=%fused_computation.22 | loop fusion | flops 1572864 | bytes 4718592 | tf_op jit(solution)/shard_map/convert_element_type | solution.py:115
  (51 shorter events, 9.0 us)
Async XLA Ops:
  0.6 7.1 %copy-start.5 = (bf16[32,4096]{1,0:T(8,128)(2,1)S(1)}, bf16[32,4096]{1,0:T(8,128)(2,1)}, u32[]{:S(2)}) copy-start(bf16[32,4096]{1,0:T(8,128)(2,1)} %param.11) | copy-start | bytes 786436
  0.6 12.7 %copy-start.6 = (bf16[128,1024]{1,0:T(8,128)(2,1)S(1)}, bf16[128,1024]{1,0:T(8,128)(2,1)}, u32[]{:S(2)}) copy-start(bf16[128,1024]{1,0:T(8,128)(2,1)} %param.6) | copy-start | bytes 786436
  1.8 11.7 %copy-start.7 = (f32[4096]{0:T(1024)S(1)}, f32[4096]{0:T(1024)}, u32[]{:S(2)}) copy-start(f32[4096]{0:T(1024)} %param.10) | copy-start | bytes 49156
  1.8 11.7 %copy-start.8 = (s32[8,3]{0,1:T(4,128)S(1)}, s32[8,3]{0,1:T(4,128)}, u32[]{:S(2)}) copy-start(s32[8,3]{0,1:T(4,128)} %param.9) | copy-start | bytes 292
  3.0 13.0 %collective-permute-start.1 = (bf16[128,2048]{0,1:T(8,128)(2,1)S(1)}, bf16[128,2048]{0,1:T(8,128)(2,1)S(1)}, u32[]{:S(2)}, u32[]{:S(2)}) collective-permute-start(bf16[128,2048]{0,1:T(8,128)(2,1)S(1)} %pad_maximum_fusion.3), channel_id=1, source_target_pairs={{4,0},{8,4},{12,8},{16,12},{20,16},{24,20},{28,24},{5,1},{9,5},{13... | collective-permute-start | bytes 1572872 | tf_op jit(solution)/shard_map/ppermute | solution.py:18
  5.8 13.3 %collective-permute-start = (bf16[128,2048]{0,1:T(8,128)(2,1)S(1)}, bf16[128,2048]{0,1:T(8,128)(2,1)S(1)}, u32[]{:S(2)}, u32[]{:S(2)}) collective-permute-start(bf16[128,2048]{0,1:T(8,128)(2,1)S(1)} %pad_maximum_fusion.3), channel_id=1, source_target_pairs={{0,4},{4,8},{8,12},{12,16},{16,20},{20,24},{24,28},{1,5},{5,9},{9,... | collective-permute-start | bytes 1572872 | tf_op jit(solution)/shard_map/ppermute | solution.py:18
  8.5 14.6 %all-to-all-start = ((bf16[32,4,1024]{2,0,1:T(8,128)(2,1)}), bf16[32,4,1024]{2,0,1:T(8,128)(2,1)S(1)}, u32[]{:S(2)}, u32[]{:S(2)}) async-start(bf16[32,4,1024]{2,0,1:T(8,128)(2,1)} %bitcast.66), calls=%async_computation | async-start | bytes 524288 | tf_op jit(solution)/shard_map/all_to_all | solution.py:48
  19.4 0.9 %copy-start = (bf16[384,1024]{0,1:T(8,128)(2,1)}, bf16[384,1024]{0,1:T(8,128)(2,1)S(1)}, u32[]{:S(2)}) copy-start(bf16[384,1024]{0,1:T(8,128)(2,1)S(1)} %get-tuple-element.38) | copy-start | bytes 2359300
  19.4 1.2 %copy-start.1 = (bf16[384,1024]{0,1:T(8,128)(2,1)}, bf16[384,1024]{0,1:T(8,128)(2,1)S(1)}, u32[]{:S(2)}) copy-start(bf16[384,1024]{0,1:T(8,128)(2,1)S(1)} %get-tuple-element.37) | copy-start | bytes 2359300
  23.1 7.9 %copy-start.3 = (f32[4,32,1024]{2,1,0:T(8,128)}, f32[4,32,1024]{2,1,0:T(8,128)S(1)}, u32[]{:S(2)}) copy-start(f32[4,32,1024]{2,1,0:T(8,128)S(1)} %reshape.114) | copy-start | bytes 1572868
  24.0 10.4 %all-to-all-start.1 = ((f32[4,128,2]{1,2,0:T(2,128)}), f32[4,128,2]{1,2,0:T(2,128)S(1)}, u32[]{:S(2)}, u32[]{:S(2)}) async-start(f32[4,128,2]{1,2,0:T(2,128)} %broadcast_in_dim.30), calls=%async_computation.1 | async-start | bytes 8192 | tf_op jit(solution)/shard_map/all_to_all | solution.py:31
  34.7 1.1 %copy-start.2 = (bf16[384,1024]{0,1:T(8,128)(2,1)S(1)}, bf16[384,1024]{0,1:T(8,128)(2,1)}, u32[]{:S(2)}) copy-start(bf16[384,1024]{0,1:T(8,128)(2,1)} %copy-done.1) | copy-start | bytes 2359300
  42.1 5.4 %copy-start.4 = (f32[4,32,1024]{2,1,0:T(8,128)S(1)}, f32[4,32,1024]{2,1,0:T(8,128)}, u32[]{:S(2)}) copy-start(f32[4,32,1024]{2,1,0:T(8,128)} %copy-done.3) | copy-start | bytes 1572868
  43.1 21.1 %collective-permute-start.2 = (bf16[128,2048]{0,1:T(8,128)(2,1)}, bf16[128,2048]{0,1:T(8,128)(2,1)}, u32[]{:S(2)}, u32[]{:S(2)}) collective-permute-start(bf16[128,2048]{0,1:T(8,128)(2,1)} %get-tuple-element.22), channel_id=1, source_target_pairs={{4,0},{8,4},{12,8},{16,12},{20,16},{24,20},{28,24},{5,1},{9,5},{13... | collective-permute-start | bytes 1572872 | tf_op jit(solution)/shard_map/ppermute | solution.py:18
  45.0 19.2 %collective-permute-start.3 = (bf16[128,2048]{0,1:T(8,128)(2,1)}, bf16[128,2048]{0,1:T(8,128)(2,1)}, u32[]{:S(2)}, u32[]{:S(2)}) collective-permute-start(bf16[128,2048]{0,1:T(8,128)(2,1)} %get-tuple-element.23), channel_id=1, source_target_pairs={{0,4},{4,8},{8,12},{12,16},{16,20},{20,24},{24,28},{1,5},{5,9},{9,... | collective-permute-start | bytes 1572872 | tf_op jit(solution)/shard_map/ppermute | solution.py:18
  48.3 14.3 %all-to-all-start.2 = ((bf16[4,32,1024]{2,1,0:T(8,128)(2,1)}), bf16[4,32,1024]{2,1,0:T(8,128)(2,1)}, u32[]{:S(2)}, u32[]{:S(2)}) async-start(bf16[4,32,1024]{2,1,0:T(8,128)(2,1)} %multiply_convert_fusion.1), calls=%async_computation.2 | async-start | bytes 524288 | tf_op jit(solution)/shard_map/all_to_all | solution.py:85

commit v2 on v1

--- a/solution.py
+++ b/solution.py
@@ -9,7 +9,9 @@
 
 NEGATIVE = -1e30
 EPSILON = 1e-06
-STATS_SUM = "a2a"
+STATS_SUM = "perm"
+NG_MODE = "perm"
+OUT_MODE = "perm"
 
 
 def passed_along(x, axis, by):
@@ -36,6 +38,43 @@
     return total
 
 
+def rolled(pieces, part):
+    n = len(pieces)
+    ordered = jnp.stack([pieces[(-j) % n] for j in range(n)], 0)
+    return jnp.roll(ordered, part, axis=0)
+
+
+def tiles_to_heads(tile, width):
+    n = lax.axis_size("tp")
+    part = lax.axis_index("tp")
+    if NG_MODE == "a2a":
+        return lax.all_to_all(tile, "tp", split_axis=1, concat_axis=0, tiled=True)
+    pieces = []
+    for shift in range(n):
+        dest = (part + shift) % n
+        chunk = lax.dynamic_slice_in_dim(tile, dest * width, width, 1)
+        if shift:
+            chunk = lax.ppermute(chunk, "tp", [(i, (i + shift) % n) for i in range(n)])
+        pieces.append(chunk)
+    return rolled(pieces, part).reshape(n * tile.shape[0], width)
+
+
+def heads_to_tiles(block, rows):
+    n = lax.axis_size("tp")
+    part = lax.axis_index("tp")
+    if OUT_MODE == "a2a":
+        return lax.all_to_all(block, "tp", split_axis=0, concat_axis=1, tiled=True)
+    pieces = []
+    for shift in range(n):
+        dest = (part + shift) % n
+        chunk = lax.dynamic_slice_in_dim(block, dest * rows, rows, 0)
+        if shift:
+            chunk = lax.ppermute(chunk, "tp", [(i, (i + shift) % n) for i in range(n)])
+        pieces.append(chunk)
+    ordered = rolled(pieces, part)
+    return jnp.moveaxis(ordered, 0, 1).reshape(rows, -1)
+
+
 def per_device(queries, key_rows, value_rows, view_mask, norm_gain, normed_grad):
     length = queries.shape[0]
     width = queries.shape[1]
@@ -45,7 +84,7 @@
     position = lax.axis_index("ctx")
     part = lax.axis_index("tp")
 
-    grad_tiles = lax.all_to_all(normed_grad, "tp", split_axis=1, concat_axis=0, tiled=True)
+    grad_tiles = tiles_to_heads(normed_grad, width)
     gain_local = lax.dynamic_slice_in_dim(norm_gain, part * width, width, 0)
 
     both = jnp.concatenate([key_rows, value_rows], axis=1)
@@ -82,7 +121,7 @@
     inverse = lax.rsqrt(totals[:, 0:1] / features + EPSILON)
     inner_mean = totals[:, 1:2] / features
     normed_heads = (values_f * inverse * gain_local).astype(jnp.bfloat16)
-    normed = lax.all_to_all(normed_heads, "tp", split_axis=0, concat_axis=1, tiled=True)
+    normed = heads_to_tiles(normed_heads, normed_grad.shape[0])
     attended_grad = (
         inverse * upstream - values_f * inverse * inverse * inverse * inner_mean
     ).astype(jnp.bfloat16)

time: 68.4 us -> 61 us (0.89)
  waiting for transfers between devices: 16.3 us -> 12.7 us
  matrix products: 7.25 us -> 4.39 us
  local copies, waits for them, and re-layouts: 16.6 us -> 13.9 us
  other arithmetic: 3.49 us -> 5.85 us
  starting transfers between devices: 22.8 us -> 22.1 us
    all_to_all x3 -> x0, starting transfers between devices: 13.8 us -> none  [the longest x1 4.87 us: per_device(): lax.all_to_all(normed_grad, 'tp', split_axis=1, concat_axis=0, tiled=True)]
    ppermute x0 -> x9, starting transfers between devices: none -> 13.1 us  [the longest x3 4.61 us: tiles_to_heads(): chunk = lax.ppermute(chunk, 'tp', [(i, (i + shift) % n) for i in range(n)])]
    all_to_all x3 -> x0, waiting for transfers between devices: 11 us -> none  [the longest x1 7.64 us: per_device(): lax.all_to_all(normed_heads, 'tp', split_axis=0, concat_axis=1, tiled=True)]
    ppermute x0 -> x9, waiting for transfers between devices: none -> 7.2 us  [the longest x3 3.84 us: heads_to_tiles(): chunk = lax.ppermute(chunk, 'tp', [(i, (i + shift) % n) for i in range(n)])]
    all_to_all x2 -> x0, local copies, waits for them, and re-layouts: 2.39 us -> none  [the longest x1 1.67 us: per_device(): lax.all_to_all(normed_heads, 'tp', split_axis=0, concat_axis=1, tiled=True)]
    dot_general x1, matrix products: 1.74 us -> 0.37 us  [per_device(): jnp.einsum('hts,shd->thd', score_grad, k_heads, preferred_element_type=jn...]
    reduce_sum x1, other arithmetic: 0.14 us -> 1.39 us  [per_device(): jnp.sum(upstream * values_f, -1)]
    unnamed x0 -> x1, other arithmetic: none -> 1.23 us
  transfers between devices with their start and end apart: 7 -> 13, of which waited for: 4 -> 6; matrix products, arithmetic and copies ran while one was open for 18% -> 15% of each run, Pallas kernels for 0% -> 0%
where the time goes in v2:
time: 61 us; the launch traced here: 59.9 us
  starting transfers between devices  22.1 us (36%)
  local copies, waits for them, and re-layouts  13.9 us (23%)
  waiting for transfers between devices  12.7 us (21%)
  other arithmetic  5.85 us (10%)
  matrix products  4.39 us (7%)
  between operations  1.06 us (2%)
    ppermute x4, starting transfers between devices, passed_along(): return lax.ppermute(x, axis, pairs)  9.02 us
    unnamed x30, local copies, waits for them, and re-layouts  6.84 us
    ppermute x4, waiting for transfers between devices, passed_along(): return lax.ppermute(x, axis, pairs)  5.48 us
    ppermute x3, starting transfers between devices, tiles_to_heads(): chunk = lax.ppermute(chunk, 'tp', [(i, (i + shift) % n) for i in range(n)])  4.61 us
    ppermute x3, starting transfers between devices, tp_sum(): lax.ppermute(stats, 'tp', [(i, (i + shift) % peers) for i in range(peers)])  4.61 us
    ppermute x3, waiting for transfers between devices, heads_to_tiles(): chunk = lax.ppermute(chunk, 'tp', [(i, (i + shift) % n) for i in range(n)])  3.84 us
    ppermute x3, starting transfers between devices, heads_to_tiles(): chunk = lax.ppermute(chunk, 'tp', [(i, (i + shift) % n) for i in range(n)])  3.83 us
    ppermute x3, waiting for transfers between devices, tp_sum(): lax.ppermute(stats, 'tp', [(i, (i + shift) % peers) for i in range(peers)])  3.35 us
  transfers between devices with their start and end apart: 13, of which 6 were waited for; matrix products, arithmetic and copies ran while one was open for 15% of the time, Pallas kernels for 0%

profile of v2, /device:TPU:4, one launch (start us, length us, event | category | flops | bytes accessed | tf_op | source)
XLA Modules:
  0.0 59.9 jit_solution(767910592433029761)
XLA Ops:
  0.7 1.2 %copy.71 = bf16[128,1024]{0,1:T(8,128)(2,1)S(1)} copy(bf16[128,1024]{1,0:T(8,128)(2,1)} %param.9) | data formatting | bytes 524288 | tf_op args[1]
  1.8 1.1 %copy.72 = bf16[128,1024]{0,1:T(8,128)(2,1)S(1)} copy(bf16[128,1024]{1,0:T(8,128)(2,1)} %param.10) | data formatting | bytes 524288 | tf_op args[2]
  3.0 2.8 %collective-permute-start.1 = (bf16[128,2048]{0,1:T(8,128)(2,1)S(1)}, bf16[128,2048]{0,1:T(8,128)(2,1)S(1)}, u32[]{:S(2)}, u32[]{:S(2)}) collective-permute-start(bf16[128,2048]{0,1:T(8,128)(2,1)S(1)} %pad_maximum_fusion.3), channel_id=1, source_target_pairs={{4,0},{8,4},{12,8},{16,12},{20,16},{24,20},{28,24},{5,1},{9,5},{13... | collective-permute-start | bytes 1572872 | tf_op jit(solution)/shard_map/ppermute | solution.py:20
  5.8 1.9 %collective-permute-start = (bf16[128,2048]{0,1:T(8,128)(2,1)S(1)}, bf16[128,2048]{0,1:T(8,128)(2,1)S(1)}, u32[]{:S(2)}, u32[]{:S(2)}) collective-permute-start(bf16[128,2048]{0,1:T(8,128)(2,1)S(1)} %pad_maximum_fusion.3), channel_id=1, source_target_pairs={{0,4},{4,8},{8,12},{12,16},{16,20},{20,24},{24,28},{1,5},{5,9},{9,... | collective-permute-start | bytes 1572872 | tf_op jit(solution)/shard_map/ppermute | solution.py:20
  8.5 3.6 %collective-permute-start.2 = (bf16[32,1024]{1,0:T(8,128)(2,1)}, bf16[32,1024]{1,0:T(8,128)(2,1)S(1)}, u32[]{:S(2)}, u32[]{:S(2)}) collective-permute-start(bf16[32,1024]{1,0:T(8,128)(2,1)} %get-tuple-element.38), channel_id=1, source_target_pairs={{0,3},{1,0},{2,1},{3,2},{4,7},{5,4},{6,5},{7,6},{8,11},{9,8},{10,9... | collective-permute-start | bytes 196616 | tf_op jit(solution)/shard_map/ppermute | solution.py:57
  12.1 1.0 %collective-permute-start.3 = (bf16[32,1024]{1,0:T(8,128)(2,1)}, bf16[32,1024]{1,0:T(8,128)(2,1)}, u32[]{:S(2)}, u32[]{:S(2)}) collective-permute-start(bf16[32,1024]{1,0:T(8,128)(2,1)} %get-tuple-element.40), channel_id=1, source_target_pairs={{0,2},{1,3},{2,0},{3,1},{4,6},{5,7},{6,4},{7,5},{8,10},{9,11},{10,... | collective-permute-start | bytes 196616 | tf_op jit(solution)/shard_map/ppermute | solution.py:57
  13.6 2.4 %collective-permute-done.1 = bf16[128,2048]{0,1:T(8,128)(2,1)S(1)} collective-permute-done((bf16[128,2048]{0,1:T(8,128)(2,1)S(1)}, bf16[128,2048]{0,1:T(8,128)(2,1)S(1)}, u32[]{:S(2)}, u32[]{:S(2)}) %collective-permute-start.1) | collective-permute-done | bytes 524320 | tf_op jit(solution)/shard_map/ppermute | solution.py:20
  16.1 3.0 %collective-permute-done = bf16[128,2048]{0,1:T(8,128)(2,1)S(1)} collective-permute-done((bf16[128,2048]{0,1:T(8,128)(2,1)S(1)}, bf16[128,2048]{0,1:T(8,128)(2,1)S(1)}, u32[]{:S(2)}, u32[]{:S(2)}) %collective-permute-start) | collective-permute-done | bytes 524320 | tf_op jit(solution)/shard_map/ppermute | solution.py:20
  20.5 0.9 %multiply_reduce_fusion.2 = (f32[128]{0:T(128)}, f32[8,128,128]{2,1,0:T(8,128)S(1)}) fusion(bf16[384,8,128]{0,2,1:T(8,128)(2,1)S(1)} %bitcast.82, f32[8,384,128]{2,1,0:T(8,128)S(1)} %get-tuple-element.44, f32[8,128]{1,0:T(8,128)S(1)} %log_add_fusion), kind=kOutput, calls=%fused_computation.45 | convolution fusion | flops 101973888 | bytes 2888192 | tf_op jit(solution)/shard_map/hts,shd->thd/dot_general | solution.py:110
  21.8 1.4 %multiply_reduce_fusion.1 = (f32[4,32]{1,0:T(4,128)S(1)}, f32[4,32,1024]{2,1,0:T(8,128)S(1)}) fusion(f32[4,32,1024]{2,1,0:T(8,128)S(1)} %reshape.105, f32[1024]{0:T(1024)S(1)} %dynamic_slice.38, s32[]{:T(128)S(6)} %select_n.92, bf16[1,32,1024]{2,1,0:T(8,128)(2,1)} %bitcast.10, bf16[1,32,1024]{2,1,0:T(8,128)(2,1)} %bitcast.9, ...), kind=kLoop, calls=%fused_computation.44 | loop fusion | flops 1441664 | bytes 1315332 | tf_op jit(solution)/shard_map/reduce_sum | solution.py:118
  24.0 2.6 %collective-permute-start.6 = (f32[128,2]{0,1:T(2,128)S(1)}, f32[128,2]{0,1:T(2,128)S(1)}, u32[]{:S(2)}, u32[]{:S(2)}) collective-permute-start(f32[128,2]{0,1:T(2,128)S(1)} %pad_maximum_fusion.4), channel_id=1, source_target_pairs={{0,2},{1,3},{2,0},{3,1},{4,6},{5,7},{6,4},{7,5},{8,10},{9,11},{10,... | collective-permute-start | bytes 3080 | tf_op jit(solution)/shard_map/ppermute | solution.py:37
  26.5 1.3 %collective-permute-start.7 = (f32[128,2]{0,1:T(2,128)S(1)}, f32[128,2]{0,1:T(2,128)S(1)}, u32[]{:S(2)}, u32[]{:S(2)}) collective-permute-start(f32[128,2]{0,1:T(2,128)S(1)} %pad_maximum_fusion.4), channel_id=1, source_target_pairs={{0,3},{1,0},{2,1},{3,2},{4,7},{5,4},{6,5},{7,6},{8,11},{9,8},{10,9... | collective-permute-start | bytes 3080 | tf_op jit(solution)/shard_map/ppermute | solution.py:37
  28.9 1.0 %copy.79 = f32[128,1024]{1,0:T(8,128)} copy(f32[128,1024]{0,1:T(8,128)S(1)} %bitcast.79) | data formatting | bytes 1048576 | tf_op jit(solution)/shard_map/convert_element_type | solution.py:115
  30.1 3.1 %collective-permute-done.5 = f32[128,2]{0,1:T(2,128)S(1)} collective-permute-done((f32[128,2]{0,1:T(2,128)S(1)}, f32[128,2]{0,1:T(2,128)S(1)}, u32[]{:S(2)}, u32[]{:S(2)}) %collective-permute-start.5) | collective-permute-done | bytes 1056 | tf_op jit(solution)/shard_map/ppermute | solution.py:37
  36.1 1.6 %multiply_bitcast_fusion = f32[384,8,128]{2,0,1:T(8,128)} fusion(bf16[8,128,384]{1,2,0:T(8,128)(2,1)S(1)} %multiply_convert_fusion, bf16[128,8,128]{0,2,1:T(8,128)(2,1)S(1)} %bitcast.85), kind=kOutput, calls=%fused_computation.10 | convolution fusion | flops 101056512 | bytes 2621440 | tf_op jit(solution)/shard_map/hts,thd->shd/dot_general | solution.py:142
  37.6 1.9 %copy.89 = f32[384,8,128]{0,2,1:T(8,128)S(1)} copy(f32[384,8,128]{2,0,1:T(8,128)} %multiply_bitcast_fusion) | data formatting | bytes 3145728 | tf_op jit(solution)/shard_map/mul | solution.py:142
  39.7 1.0 %fusion.33 = (bf16[128,2048]{0,1:T(8,128)(2,1)}, bf16[128,2048]{0,1:T(8,128)(2,1)}) fusion(bf16[384,2048]{0,1:T(8,128)(2,1)S(1)} %fusion), kind=kLoop, calls=%fused_computation.80 | loop fusion | bytes 2097152 | tf_op jit(solution)/shard_map/slice | solution.py:150
  40.8 1.9 %collective-permute-start.11 = (bf16[128,2048]{0,1:T(8,128)(2,1)}, bf16[128,2048]{0,1:T(8,128)(2,1)}, u32[]{:S(2)}, u32[]{:S(2)}) collective-permute-start(bf16[128,2048]{0,1:T(8,128)(2,1)} %get-tuple-element.25), channel_id=1, source_target_pairs={{4,0},{8,4},{12,8},{16,12},{20,16},{24,20},{28,24},{5,1},{9,5},{13... | collective-permute-start | bytes 1572872 | tf_op jit(solution)/shard_map/ppermute | solution.py:20
  42.7 2.4 %collective-permute-start.12 = (bf16[128,2048]{0,1:T(8,128)(2,1)}, bf16[128,2048]{0,1:T(8,128)(2,1)}, u32[]{:S(2)}, u32[]{:S(2)}) collective-permute-start(bf16[128,2048]{0,1:T(8,128)(2,1)} %get-tuple-element.26), channel_id=1, source_target_pairs={{0,4},{4,8},{8,12},{12,16},{16,20},{20,24},{24,28},{1,5},{5,9},{9,... | collective-permute-start | bytes 1572872 | tf_op jit(solution)/shard_map/ppermute | solution.py:20
  46.5 3.3 %collective-permute-start.8 = (bf16[32,1024]{1,0:T(8,128)(2,1)}, bf16[32,1024]{1,0:T(8,128)(2,1)}, u32[]{:S(2)}, u32[]{:S(2)}) collective-permute-start(bf16[32,1024]{1,0:T(8,128)(2,1)} %get-tuple-element.35), channel_id=1, source_target_pairs={{0,3},{1,0},{2,1},{3,2},{4,7},{5,4},{6,5},{7,6},{8,11},{9,8},{10,9... | collective-permute-start | bytes 196616 | tf_op jit(solution)/shard_map/ppermute | solution.py:72
  51.0 2.0 %collective-permute-done.10 = bf16[32,1024]{1,0:T(8,128)(2,1)S(1)} collective-permute-done((bf16[32,1024]{1,0:T(8,128)(2,1)}, bf16[32,1024]{1,0:T(8,128)(2,1)S(1)}, u32[]{:S(2)}, u32[]{:S(2)}) %collective-permute-start.10) | collective-permute-done | bytes 65568 | tf_op jit(solution)/shard_map/ppermute | solution.py:72
  53.0 1.8 %collective-permute-done.9 = bf16[32,1024]{1,0:T(8,128)(2,1)} collective-permute-done((bf16[32,1024]{1,0:T(8,128)(2,1)}, bf16[32,1024]{1,0:T(8,128)(2,1)}, u32[]{:S(2)}, u32[]{:S(2)}) %collective-permute-start.9) | collective-permute-done | bytes 65568 | tf_op jit(solution)/shard_map/ppermute | solution.py:72
  54.8 1.2 %fusion.15 = bf16[4,4,8,1024]{3,2,1,0:T(8,128)(2,1)S(1)} fusion(s32[]{:T(128)S(6)} %select_n.92, bf16[1,32,1024]{2,1,0:T(8,128)(2,1)S(1)} %get-tuple-element.36, bf16[1,32,1024]{2,1,0:T(8,128)(2,1)} %bitcast.13, bf16[1,32,1024]{2,1,0:T(8,128)(2,1)} %bitcast.14, bf16[1,32,1024]{2,1,0:T(8,128)(2,1)S(1)} %bitcast.91), kind=kLoop, calls=%fused_computation.50 | loop fusion | flops 917504 | bytes 524292
  56.8 1.4 %fusion.10 = bf16[128,2048]{0,1:T(8,128)(2,1)S(1)} fusion(f32[384,1024]{0,1:T(8,128)S(1)} %bitcast.75, f32[384,1024]{0,1:T(8,128)S(1)} %bitcast.77, bf16[128,2048]{0,1:T(8,128)(2,1)} %collective-permute-done.12, bf16[128,2048]{0,1:T(8,128)(2,1)} %collective-permute-done.11), kind=kLoop, calls=%fused_computation.21 | loop fusion | flops 1572864 | bytes 4718592 | tf_op jit(solution)/shard_map/convert_element_type | solution.py:154
  (69 shorter events, 12.9 us)
Async XLA Ops:
  0.6 7.2 %copy-start.7 = (bf16[32,4096]{1,0:T(8,128)(2,1)S(1)}, bf16[32,4096]{1,0:T(8,128)(2,1)}, u32[]{:S(2)}) copy-start(bf16[32,4096]{1,0:T(8,128)(2,1)} %param.13) | copy-start | bytes 786436
  0.6 12.5 %copy-start.8 = (bf16[128,1024]{1,0:T(8,128)(2,1)S(1)}, bf16[128,1024]{1,0:T(8,128)(2,1)}, u32[]{:S(2)}) copy-start(bf16[128,1024]{1,0:T(8,128)(2,1)} %param.8) | copy-start | bytes 786436
  0.7 12.7 %copy-start.10 = (f32[4096]{0:T(1024)S(1)}, f32[4096]{0:T(1024)}, u32[]{:S(2)}) copy-start(f32[4096]{0:T(1024)} %param.12) | copy-start | bytes 49156
  0.7 12.7 %copy-start.11 = (s32[8,3]{0,1:T(4,128)S(1)}, s32[8,3]{0,1:T(4,128)}, u32[]{:S(2)}) copy-start(s32[8,3]{0,1:T(4,128)} %param.11) | copy-start | bytes 292
  3.0 13.0 %collective-permute-start.1 = (bf16[128,2048]{0,1:T(8,128)(2,1)S(1)}, bf16[128,2048]{0,1:T(8,128)(2,1)S(1)}, u32[]{:S(2)}, u32[]{:S(2)}) collective-permute-start(bf16[128,2048]{0,1:T(8,128)(2,1)S(1)} %pad_maximum_fusion.3), channel_id=1, source_target_pairs={{4,0},{8,4},{12,8},{16,12},{20,16},{24,20},{28,24},{5,1},{9,5},{13... | collective-permute-start | bytes 1572872 | tf_op jit(solution)/shard_map/ppermute | solution.py:20
  5.8 13.3 %collective-permute-start = (bf16[128,2048]{0,1:T(8,128)(2,1)S(1)}, bf16[128,2048]{0,1:T(8,128)(2,1)S(1)}, u32[]{:S(2)}, u32[]{:S(2)}) collective-permute-start(bf16[128,2048]{0,1:T(8,128)(2,1)S(1)} %pad_maximum_fusion.3), channel_id=1, source_target_pairs={{0,4},{4,8},{8,12},{12,16},{16,20},{20,24},{24,28},{1,5},{5,9},{9,... | collective-permute-start | bytes 1572872 | tf_op jit(solution)/shard_map/ppermute | solution.py:20
  8.5 13.3 %collective-permute-start.2 = (bf16[32,1024]{1,0:T(8,128)(2,1)}, bf16[32,1024]{1,0:T(8,128)(2,1)S(1)}, u32[]{:S(2)}, u32[]{:S(2)}) collective-permute-start(bf16[32,1024]{1,0:T(8,128)(2,1)} %get-tuple-element.38), channel_id=1, source_target_pairs={{0,3},{1,0},{2,1},{3,2},{4,7},{5,4},{6,5},{7,6},{8,11},{9,8},{10,9... | collective-permute-start | bytes 196616 | tf_op jit(solution)/shard_map/ppermute | solution.py:57
  12.1 9.7 %collective-permute-start.4 = (bf16[32,1024]{1,0:T(8,128)(2,1)}, bf16[32,1024]{1,0:T(8,128)(2,1)}, u32[]{:S(2)}, u32[]{:S(2)}) collective-permute-start(bf16[32,1024]{1,0:T(8,128)(2,1)} %get-tuple-element.39), channel_id=1, source_target_pairs={{0,1},{1,2},{2,3},{3,0},{4,5},{5,6},{6,7},{7,4},{8,9},{9,10},{10,1... | collective-permute-start | bytes 196616 | tf_op jit(solution)/shard_map/ppermute | solution.py:57
  12.1 9.7 %collective-permute-start.3 = (bf16[32,1024]{1,0:T(8,128)(2,1)}, bf16[32,1024]{1,0:T(8,128)(2,1)}, u32[]{:S(2)}, u32[]{:S(2)}) collective-permute-start(bf16[32,1024]{1,0:T(8,128)(2,1)} %get-tuple-element.40), channel_id=1, source_target_pairs={{0,2},{1,3},{2,0},{3,1},{4,6},{5,7},{6,4},{7,5},{8,10},{9,11},{10,... | collective-permute-start | bytes 196616 | tf_op jit(solution)/shard_map/ppermute | solution.py:57
  19.4 0.9 %copy-start = (bf16[384,1024]{0,1:T(8,128)(2,1)}, bf16[384,1024]{0,1:T(8,128)(2,1)S(1)}, u32[]{:S(2)}) copy-start(bf16[384,1024]{0,1:T(8,128)(2,1)S(1)} %get-tuple-element.48) | copy-start | bytes 2359300
  19.4 1.1 %copy-start.4 = (bf16[384,1024]{0,1:T(8,128)(2,1)}, bf16[384,1024]{0,1:T(8,128)(2,1)S(1)}, u32[]{:S(2)}) copy-start(bf16[384,1024]{0,1:T(8,128)(2,1)S(1)} %get-tuple-element.47) | copy-start | bytes 2359300
  24.0 6.0 %collective-permute-start.6 = (f32[128,2]{0,1:T(2,128)S(1)}, f32[128,2]{0,1:T(2,128)S(1)}, u32[]{:S(2)}, u32[]{:S(2)}) collective-permute-start(f32[128,2]{0,1:T(2,128)S(1)} %pad_maximum_fusion.4), channel_id=1, source_target_pairs={{0,2},{1,3},{2,0},{3,1},{4,6},{5,7},{6,4},{7,5},{8,10},{9,11},{10,... | collective-permute-start | bytes 3080 | tf_op jit(solution)/shard_map/ppermute | solution.py:37
  26.5 3.6 %collective-permute-start.7 = (f32[128,2]{0,1:T(2,128)S(1)}, f32[128,2]{0,1:T(2,128)S(1)}, u32[]{:S(2)}, u32[]{:S(2)}) collective-permute-start(f32[128,2]{0,1:T(2,128)S(1)} %pad_maximum_fusion.4), channel_id=1, source_target_pairs={{0,3},{1,0},{2,1},{3,2},{4,7},{5,4},{6,5},{7,6},{8,11},{9,8},{10,9... | collective-permute-start | bytes 3080 | tf_op jit(solution)/shard_map/ppermute | solution.py:37
  27.9 5.4 %collective-permute-start.5 = (f32[128,2]{0,1:T(2,128)S(1)}, f32[128,2]{0,1:T(2,128)S(1)}, u32[]{:S(2)}, u32[]{:S(2)}) collective-permute-start(f32[128,2]{0,1:T(2,128)S(1)} %pad_maximum_fusion.4), channel_id=1, source_target_pairs={{0,1},{1,2},{2,3},{3,0},{4,5},{5,6},{6,7},{7,4},{8,9},{9,10},{10,1... | collective-permute-start | bytes 3080 | tf_op jit(solution)/shard_map/ppermute | solution.py:37
  28.6 4.7 %copy-start.9 = (f32[128]{0:T(128)S(1)}, f32[128]{0:T(128)}, u32[]{:S(2)}) copy-start(f32[128]{0:T(128)} %get-tuple-element.45) | copy-start | bytes 1540
  33.5 1.1 %copy-start.5 = (bf16[384,1024]{0,1:T(8,128)(2,1)S(1)}, bf16[384,1024]{0,1:T(8,128)(2,1)}, u32[]{:S(2)}) copy-start(bf16[384,1024]{0,1:T(8,128)(2,1)} %copy-done.4) | copy-start | bytes 2359300
  39.7 5.4 %copy-start.6 = (f32[128,1024]{1,0:T(8,128)S(1)}, f32[128,1024]{1,0:T(8,128)}, u32[]{:S(2)}) copy-start(f32[128,1024]{1,0:T(8,128)} %copy.79) | copy-start | bytes 1572868
  39.7 10.1 %copy-start.1 = (bf16[384,1024]{0,1:T(8,128)(2,1)S(1)}, bf16[384,1024]{0,1:T(8,128)(2,1)}, u32[]{:S(2)}) copy-start(bf16[384,1024]{0,1:T(8,128)(2,1)} %copy-done) | copy-start | bytes 2359300
  39.7 10.0 %copy-start.3 = (bf16[8,128,384]{1,2,0:T(8,128)(2,1)S(1)}, bf16[8,128,384]{1,2,0:T(8,128)(2,1)}, u32[]{:S(2)}) copy-start(bf16[8,128,384]{1,2,0:T(8,128)(2,1)} %copy-done.2) | copy-start | bytes 2359300
  40.8 16.0 %collective-permute-start.11 = (bf16[128,2048]{0,1:T(8,128)(2,1)}, bf16[128,2048]{0,1:T(8,128)(2,1)}, u32[]{:S(2)}, u32[]{:S(2)}) collective-permute-start(bf16[128,2048]{0,1:T(8,128)(2,1)} %get-tuple-element.25), channel_id=1, source_target_pairs={{4,0},{8,4},{12,8},{16,12},{20,16},{24,20},{28,24},{5,1},{9,5},{13... | collective-permute-start | bytes 1572872 | tf_op jit(solution)/shard_map/ppermute | solution.py:20
  42.7 14.1 %collective-permute-start.12 = (bf16[128,2048]{0,1:T(8,128)(2,1)}, bf16[128,2048]{0,1:T(8,128)(2,1)}, u32[]{:S(2)}, u32[]{:S(2)}) collective-permute-start(bf16[128,2048]{0,1:T(8,128)(2,1)} %get-tuple-element.26), channel_id=1, source_target_pairs={{0,4},{4,8},{8,12},{12,16},{16,20},{20,24},{24,28},{1,5},{5,9},{9,... | collective-permute-start | bytes 1572872 | tf_op jit(solution)/shard_map/ppermute | solution.py:20
  45.9 7.1 %collective-permute-start.10 = (bf16[32,1024]{1,0:T(8,128)(2,1)}, bf16[32,1024]{1,0:T(8,128)(2,1)S(1)}, u32[]{:S(2)}, u32[]{:S(2)}) collective-permute-start(bf16[32,1024]{1,0:T(8,128)(2,1)} %get-tuple-element.33), channel_id=1, source_target_pairs={{0,1},{1,2},{2,3},{3,0},{4,5},{5,6},{6,7},{7,4},{8,9},{9,10},{10,1... | collective-permute-start | bytes 196616 | tf_op jit(solution)/shard_map/ppermute | solution.py:72
  45.9 8.9 %collective-permute-start.9 = (bf16[32,1024]{1,0:T(8,128)(2,1)}, bf16[32,1024]{1,0:T(8,128)(2,1)}, u32[]{:S(2)}, u32[]{:S(2)}) collective-permute-start(bf16[32,1024]{1,0:T(8,128)(2,1)} %get-tuple-element.34), channel_id=1, source_target_pairs={{0,2},{1,3},{2,0},{3,1},{4,6},{5,7},{6,4},{7,5},{8,10},{9,11},{10,... | collective-permute-start | bytes 196616 | tf_op jit(solution)/shard_map/ppermute | solution.py:72
  46.5 8.3 %collective-permute-start.8 = (bf16[32,1024]{1,0:T(8,128)(2,1)}, bf16[32,1024]{1,0:T(8,128)(2,1)}, u32[]{:S(2)}, u32[]{:S(2)}) collective-permute-start(bf16[32,1024]{1,0:T(8,128)(2,1)} %get-tuple-element.35), channel_id=1, source_target_pairs={{0,3},{1,0},{2,1},{3,2},{4,7},{5,4},{6,5},{7,6},{8,11},{9,8},{10,9... | collective-permute-start | bytes 196616 | tf_op jit(solution)/shard_map/ppermute | solution.py:72
  (1 other events, 0.9 us)

commit v3 on v2

--- a/solution.py
+++ b/solution.py
@@ -9,7 +9,7 @@
 
 NEGATIVE = -1e30
 EPSILON = 1e-06
-STATS_SUM = "perm"
+STATS_SUM = "xor"
 NG_MODE = "perm"
 OUT_MODE = "perm"
 
@@ -24,10 +24,40 @@
     return values.reshape(values.shape[0], -1, HSZ)
 
 
+def xor_flip(stacked, part, n):
+    bits = n.bit_length() - 1
+    view = stacked.reshape((2,) * bits + stacked.shape[1:])
+    for b in range(bits):
+        axis = bits - 1 - b
+        view = jnp.where((part >> b) & 1 == 1, jnp.flip(view, axis), view)
+    return view.reshape(stacked.shape)
+
+
+def xor_exchange(stacked, n):
+    bits = n.bit_length() - 1
+    view = stacked.reshape((2,) * bits + stacked.shape[1:])
+    for b in range(bits):
+        axis = bits - 1 - b
+        keep = lax.index_in_dim(view, 0, axis, keepdims=True)
+        sent = lax.index_in_dim(view, 1, axis, keepdims=True)
+        got = lax.ppermute(sent, "tp", [(i, i ^ (1 << b)) for i in range(n)])
+        view = jnp.concatenate([keep, got], axis)
+    return view.reshape(stacked.shape)
+
+
+def power_of_two(n):
+    return n & (n - 1) == 0
+
+
 def tp_sum(stats):
     if STATS_SUM == "psum":
         return lax.psum(stats, "tp")
     peers = lax.axis_size("tp")
+    if STATS_SUM == "xor" and power_of_two(peers):
+        total = stats
+        for b in range(peers.bit_length() - 1):
+            total = total + lax.ppermute(total, "tp", [(i, i ^ (1 << b)) for i in range(peers)])
+        return total
     if STATS_SUM == "a2a":
         spread = jnp.broadcast_to(stats[None], (peers,) + stats.shape)
         gathered = lax.all_to_all(spread, "tp", split_axis=0, concat_axis=0, tiled=True)
@@ -49,6 +79,10 @@
     part = lax.axis_index("tp")
     if NG_MODE == "a2a":
         return lax.all_to_all(tile, "tp", split_axis=1, concat_axis=0, tiled=True)
+    if NG_MODE == "xor" and power_of_two(n):
+        groups = jnp.moveaxis(tile.reshape(tile.shape[0], n, width), 1, 0)
+        got = xor_flip(xor_exchange(xor_flip(groups, part, n), n), part, n)
+        return got.reshape(n * tile.shape[0], width)
     pieces = []
     for shift in range(n):
         dest = (part + shift) % n
@@ -64,6 +98,10 @@
     part = lax.axis_index("tp")
     if OUT_MODE == "a2a":
         return lax.all_to_all(block, "tp", split_axis=0, concat_axis=1, tiled=True)
+    if OUT_MODE == "xor" and power_of_two(n):
+        tiles = block.reshape(n, rows, block.shape[1])
+        got = xor_flip(xor_exchange(xor_flip(tiles, part, n), n), part, n)
+        return jnp.moveaxis(got, 0, 1).reshape(rows, -1)
     pieces = []
     for shift in range(n):
         dest = (part + shift) % n

time: 61 us -> 59.8 us (0.980)
  waiting for transfers between devices: 12.7 us -> 10.2 us
  local copies, waits for them, and re-layouts: 13.9 us -> 15.3 us
  starting transfers between devices: 22.1 us -> 23.4 us
  other arithmetic: 5.85 us -> 5.2 us
    ppermute x3, starting transfers between devices: 3.83 us -> 5.51 us  [heads_to_tiles(): chunk = lax.ppermute(chunk, 'tp', [(i, (i + shift) % n) for i in range(n)])]
    ppermute x3 -> x2, waiting for transfers between devices: 3.35 us -> 1.83 us  [tp_sum(): lax.ppermute(total, 'tp', [(i, i ^ 1 << b) for i in range(peers)])]
    dynamic_slice x1, local copies, waits for them, and re-layouts: 0.01 us -> 0.7 us  [per_device(): gain_local = lax.dynamic_slice_in_dim(norm_gain, part * width, width, 0)]
    mul x1, local copies, waits for them, and re-layouts: 0.01 us -> 0.69 us  [per_device(): upstream = grad_tiles.astype(jnp.float32) * gain_local]
    another operation x1, other arithmetic: 0.66 us -> 0.01 us  [per_device(): jnp.stack([jnp.sum(values_f * values_f, -1), jnp.sum(upstream * values_f,...]
    ppermute x4, waiting for transfers between devices: 5.48 us -> 4.84 us  [passed_along(): return lax.ppermute(x, axis, pairs)]
    ppermute x3 -> x2, starting transfers between devices: 4.61 us -> 4.29 us  [tp_sum(): lax.ppermute(total, 'tp', [(i, i ^ 1 << b) for i in range(peers)])]
    unnamed x30 -> x26, local copies, waits for them, and re-layouts: 6.84 us -> 6.85 us
  transfers between devices with their start and end apart: 13 -> 12, of which waited for: 6 -> 7; matrix products, arithmetic and copies ran while one was open for 15% -> 16% of each run, Pallas kernels for 0% -> 0%
where the time goes in v3:
time: 59.8 us; the launch traced here: 59 us
  starting transfers between devices  23.4 us (39%)
  local copies, waits for them, and re-layouts  15.3 us (26%)
  waiting for transfers between devices  10.2 us (17%)
  other arithmetic  5.2 us (9%)
  matrix products  3.87 us (6%)
  between operations  1.01 us (2%)
    ppermute x4, starting transfers between devices, passed_along(): return lax.ppermute(x, axis, pairs)  9.02 us
    unnamed x26, local copies, waits for them, and re-layouts  6.85 us
    ppermute x3, starting transfers between devices, heads_to_tiles(): chunk = lax.ppermute(chunk, 'tp', [(i, (i + shift) % n) for i in range(n)])  5.51 us
    ppermute x4, waiting for transfers between devices, passed_along(): return lax.ppermute(x, axis, pairs)  4.84 us
    ppermute x3, starting transfers between devices, tiles_to_heads(): chunk = lax.ppermute(chunk, 'tp', [(i, (i + shift) % n) for i in range(n)])  4.61 us
    ppermute x2, starting transfers between devices, tp_sum(): lax.ppermute(total, 'tp', [(i, i ^ 1 << b) for i in range(peers)])  4.29 us
    ppermute x3, waiting for transfers between devices, heads_to_tiles(): chunk = lax.ppermute(chunk, 'tp', [(i, (i + shift) % n) for i in range(n)])  3.54 us
    mul x1, local copies, waits for them, and re-layouts, per_device(): jnp.einsum('hts,thd->shd', score_grad, q_heads, preferred_element_type=jn...  1.87 us
  transfers between devices with their start and end apart: 12, of which 7 were waited for; matrix products, arithmetic and copies ran while one was open for 16% of the time, Pallas kernels for 0%

profile of v3, /device:TPU:4, one launch (start us, length us, event | category | flops | bytes accessed | tf_op | source)
XLA Modules:
  0.0 59.0 jit_solution(18187652044080118767)
XLA Ops:
  0.7 1.2 %copy.71 = bf16[128,1024]{0,1:T(8,128)(2,1)S(1)} copy(bf16[128,1024]{1,0:T(8,128)(2,1)} %param.9) | data formatting | bytes 524288 | tf_op args[1]
  1.8 1.1 %copy.72 = bf16[128,1024]{0,1:T(8,128)(2,1)S(1)} copy(bf16[128,1024]{1,0:T(8,128)(2,1)} %param.10) | data formatting | bytes 524288 | tf_op args[2]
  3.0 2.8 %collective-permute-start.1 = (bf16[128,2048]{0,1:T(8,128)(2,1)S(1)}, bf16[128,2048]{0,1:T(8,128)(2,1)S(1)}, u32[]{:S(2)}, u32[]{:S(2)}) collective-permute-start(bf16[128,2048]{0,1:T(8,128)(2,1)S(1)} %pad_maximum_fusion.3), channel_id=1, source_target_pairs={{4,0},{8,4},{12,8},{16,12},{20,16},{24,20},{28,24},{5,1},{9,5},{13... | collective-permute-start | bytes 1572872 | tf_op jit(solution)/shard_map/ppermute | solution.py:20
  5.8 1.9 %collective-permute-start = (bf16[128,2048]{0,1:T(8,128)(2,1)S(1)}, bf16[128,2048]{0,1:T(8,128)(2,1)S(1)}, u32[]{:S(2)}, u32[]{:S(2)}) collective-permute-start(bf16[128,2048]{0,1:T(8,128)(2,1)S(1)} %pad_maximum_fusion.3), channel_id=1, source_target_pairs={{0,4},{4,8},{8,12},{12,16},{16,20},{20,24},{24,28},{1,5},{5,9},{9,... | collective-permute-start | bytes 1572872 | tf_op jit(solution)/shard_map/ppermute | solution.py:20
  8.5 3.6 %collective-permute-start.2 = (bf16[32,1024]{1,0:T(8,128)(2,1)}, bf16[32,1024]{1,0:T(8,128)(2,1)S(1)}, u32[]{:S(2)}, u32[]{:S(2)}) collective-permute-start(bf16[32,1024]{1,0:T(8,128)(2,1)} %get-tuple-element.38), channel_id=1, source_target_pairs={{0,3},{1,0},{2,1},{3,2},{4,7},{5,4},{6,5},{7,6},{8,11},{9,8},{10,9... | collective-permute-start | bytes 196616 | tf_op jit(solution)/shard_map/ppermute | solution.py:91
  12.1 1.0 %collective-permute-start.3 = (bf16[32,1024]{1,0:T(8,128)(2,1)}, bf16[32,1024]{1,0:T(8,128)(2,1)}, u32[]{:S(2)}, u32[]{:S(2)}) collective-permute-start(bf16[32,1024]{1,0:T(8,128)(2,1)} %get-tuple-element.40), channel_id=1, source_target_pairs={{0,2},{1,3},{2,0},{3,1},{4,6},{5,7},{6,4},{7,5},{8,10},{9,11},{10,... | collective-permute-start | bytes 196616 | tf_op jit(solution)/shard_map/ppermute | solution.py:91
  14.3 1.8 %collective-permute-done.1 = bf16[128,2048]{0,1:T(8,128)(2,1)S(1)} collective-permute-done((bf16[128,2048]{0,1:T(8,128)(2,1)S(1)}, bf16[128,2048]{0,1:T(8,128)(2,1)S(1)}, u32[]{:S(2)}, u32[]{:S(2)}) %collective-permute-start.1) | collective-permute-done | bytes 524320 | tf_op jit(solution)/shard_map/ppermute | solution.py:20
  16.1 3.0 %collective-permute-done = bf16[128,2048]{0,1:T(8,128)(2,1)S(1)} collective-permute-done((bf16[128,2048]{0,1:T(8,128)(2,1)S(1)}, bf16[128,2048]{0,1:T(8,128)(2,1)S(1)}, u32[]{:S(2)}, u32[]{:S(2)}) %collective-permute-start) | collective-permute-done | bytes 524320 | tf_op jit(solution)/shard_map/ppermute | solution.py:20
  21.3 1.4 %multiply_reduce_fusion.1 = (f32[4,32]{1,0:T(4,128)S(1)}, f32[4,32,1024]{2,1,0:T(8,128)S(1)}) fusion(f32[4,32,1024]{2,1,0:T(8,128)S(1)} %reshape.105, f32[1024]{0:T(1024)S(1)} %dynamic_slice.38, s32[]{:T(128)S(6)} %select_n.92, bf16[1,32,1024]{2,1,0:T(8,128)(2,1)} %bitcast.10, bf16[1,32,1024]{2,1,0:T(8,128)(2,1)} %bitcast.9, ...), kind=kLoop, calls=%fused_computation.44 | loop fusion | flops 1441664 | bytes 1315332 | tf_op jit(solution)/shard_map/reduce_sum | solution.py:156
  22.8 1.6 %collective-permute-start.5 = (f32[128,2]{0,1:T(2,128)S(1)}, f32[128,2]{0,1:T(2,128)S(1)}, u32[]{:S(2)}, u32[]{:S(2)}) collective-permute-start(f32[128,2]{0,1:T(2,128)S(1)} %pad_maximum_fusion.4), channel_id=1, source_target_pairs={{0,1},{1,0},{2,3},{3,2},{4,5},{5,4},{6,7},{7,6},{8,9},{9,8},{10,11... | collective-permute-start | bytes 3080 | tf_op jit(solution)/shard_map/ppermute | solution.py:59
  25.1 1.3 %collective-permute-done.5 = f32[128,2]{0,1:T(2,128)S(1)} collective-permute-done((f32[128,2]{0,1:T(2,128)S(1)}, f32[128,2]{0,1:T(2,128)S(1)}, u32[]{:S(2)}, u32[]{:S(2)}) %collective-permute-start.5) | collective-permute-done | bytes 1056 | tf_op jit(solution)/shard_map/ppermute | solution.py:59
  26.4 2.7 %collective-permute-start.6 = (f32[128,2]{0,1:T(2,128)S(1)}, f32[128,2]{0,1:T(2,128)S(1)}, u32[]{:S(2)}, u32[]{:S(2)}) collective-permute-start(f32[128,2]{0,1:T(2,128)S(1)} %fusion.32), channel_id=1, source_target_pairs={{0,2},{1,3},{2,0},{3,1},{4,6},{5,7},{6,4},{7,5},{8,10},{9,11},{10,... | collective-permute-start | bytes 3080 | tf_op jit(solution)/shard_map/ppermute | solution.py:59
  29.4 1.0 %copy.79 = f32[128,1024]{1,0:T(8,128)} copy(f32[128,1024]{0,1:T(8,128)S(1)} %bitcast.79) | data formatting | bytes 1048576 | tf_op jit(solution)/shard_map/convert_element_type | solution.py:153
  33.8 1.5 %multiply_bitcast_fusion = f32[384,8,128]{2,0,1:T(8,128)} fusion(bf16[8,128,384]{1,2,0:T(8,128)(2,1)S(1)} %multiply_convert_fusion, bf16[128,8,128]{0,2,1:T(8,128)(2,1)S(1)} %bitcast.85), kind=kOutput, calls=%fused_computation.10 | convolution fusion | flops 101056512 | bytes 2621440 | tf_op jit(solution)/shard_map/hts,thd->shd/dot_general | solution.py:180
  35.3 1.9 %copy.89 = f32[384,8,128]{0,2,1:T(8,128)S(1)} copy(f32[384,8,128]{2,0,1:T(8,128)} %multiply_bitcast_fusion) | data formatting | bytes 3145728 | tf_op jit(solution)/shard_map/mul | solution.py:180
  37.4 1.0 %fusion.34 = (bf16[128,2048]{0,1:T(8,128)(2,1)}, bf16[128,2048]{0,1:T(8,128)(2,1)}) fusion(bf16[384,2048]{0,1:T(8,128)(2,1)S(1)} %fusion), kind=kLoop, calls=%fused_computation.80 | loop fusion | bytes 2097152 | tf_op jit(solution)/shard_map/slice | solution.py:188
  38.5 1.9 %collective-permute-start.10 = (bf16[128,2048]{0,1:T(8,128)(2,1)}, bf16[128,2048]{0,1:T(8,128)(2,1)}, u32[]{:S(2)}, u32[]{:S(2)}) collective-permute-start(bf16[128,2048]{0,1:T(8,128)(2,1)} %get-tuple-element.25), channel_id=1, source_target_pairs={{4,0},{8,4},{12,8},{16,12},{20,16},{24,20},{28,24},{5,1},{9,5},{13... | collective-permute-start | bytes 1572872 | tf_op jit(solution)/shard_map/ppermute | solution.py:20
  40.4 2.4 %collective-permute-start.11 = (bf16[128,2048]{0,1:T(8,128)(2,1)}, bf16[128,2048]{0,1:T(8,128)(2,1)}, u32[]{:S(2)}, u32[]{:S(2)}) collective-permute-start(bf16[128,2048]{0,1:T(8,128)(2,1)} %get-tuple-element.26), channel_id=1, source_target_pairs={{0,4},{4,8},{8,12},{12,16},{16,20},{20,24},{24,28},{1,5},{5,9},{9,... | collective-permute-start | bytes 1572872 | tf_op jit(solution)/shard_map/ppermute | solution.py:20
  43.6 1.6 %collective-permute-start.9 = (bf16[32,1024]{1,0:T(8,128)(2,1)}, bf16[32,1024]{1,0:T(8,128)(2,1)S(1)}, u32[]{:S(2)}, u32[]{:S(2)}) collective-permute-start(bf16[32,1024]{1,0:T(8,128)(2,1)} %get-tuple-element.33), channel_id=1, source_target_pairs={{0,1},{1,2},{2,3},{3,0},{4,5},{5,6},{6,7},{7,4},{8,9},{9,10},{10,1... | collective-permute-start | bytes 196616 | tf_op jit(solution)/shard_map/ppermute | solution.py:110
  45.2 2.6 %collective-permute-start.8 = (bf16[32,1024]{1,0:T(8,128)(2,1)}, bf16[32,1024]{1,0:T(8,128)(2,1)}, u32[]{:S(2)}, u32[]{:S(2)}) collective-permute-start(bf16[32,1024]{1,0:T(8,128)(2,1)} %get-tuple-element.34), channel_id=1, source_target_pairs={{0,2},{1,3},{2,0},{3,1},{4,6},{5,7},{6,4},{7,5},{8,10},{9,11},{10,... | collective-permute-start | bytes 196616 | tf_op jit(solution)/shard_map/ppermute | solution.py:110
  47.8 1.3 %collective-permute-start.7 = (bf16[32,1024]{1,0:T(8,128)(2,1)}, bf16[32,1024]{1,0:T(8,128)(2,1)}, u32[]{:S(2)}, u32[]{:S(2)}) collective-permute-start(bf16[32,1024]{1,0:T(8,128)(2,1)} %get-tuple-element.35), channel_id=1, source_target_pairs={{0,3},{1,0},{2,1},{3,2},{4,7},{5,4},{6,5},{7,6},{8,11},{9,8},{10,9... | collective-permute-start | bytes 196616 | tf_op jit(solution)/shard_map/ppermute | solution.py:110
  50.5 3.1 %collective-permute-done.8 = bf16[32,1024]{1,0:T(8,128)(2,1)} collective-permute-done((bf16[32,1024]{1,0:T(8,128)(2,1)}, bf16[32,1024]{1,0:T(8,128)(2,1)}, u32[]{:S(2)}, u32[]{:S(2)}) %collective-permute-start.8) | collective-permute-done | bytes 65568 | tf_op jit(solution)/shard_map/ppermute | solution.py:110
  53.9 1.2 %fusion.15 = bf16[4,4,8,1024]{3,2,1,0:T(8,128)(2,1)S(1)} fusion(s32[]{:T(128)S(6)} %select_n.92, bf16[1,32,1024]{2,1,0:T(8,128)(2,1)S(1)} %get-tuple-element.36, bf16[1,32,1024]{2,1,0:T(8,128)(2,1)} %bitcast.13, bf16[1,32,1024]{2,1,0:T(8,128)(2,1)} %bitcast.14, bf16[1,32,1024]{2,1,0:T(8,128)(2,1)S(1)} %bitcast.91), kind=kLoop, calls=%fused_computation.50 | loop fusion | flops 917504 | bytes 524292
  55.9 1.4 %fusion.10 = bf16[128,2048]{0,1:T(8,128)(2,1)S(1)} fusion(f32[384,1024]{0,1:T(8,128)S(1)} %bitcast.75, f32[384,1024]{0,1:T(8,128)S(1)} %bitcast.77, bf16[128,2048]{0,1:T(8,128)(2,1)} %collective-permute-done.11, bf16[128,2048]{0,1:T(8,128)(2,1)} %collective-permute-done.10), kind=kLoop, calls=%fused_computation.21 | loop fusion | flops 1572864 | bytes 4718592 | tf_op jit(solution)/shard_map/convert_element_type | solution.py:192
  (64 shorter events, 13.5 us)
Async XLA Ops:
  0.6 7.2 %copy-start.7 = (bf16[32,4096]{1,0:T(8,128)(2,1)S(1)}, bf16[32,4096]{1,0:T(8,128)(2,1)}, u32[]{:S(2)}) copy-start(bf16[32,4096]{1,0:T(8,128)(2,1)} %param.13) | copy-start | bytes 786436
  0.6 12.5 %copy-start.8 = (bf16[128,1024]{1,0:T(8,128)(2,1)S(1)}, bf16[128,1024]{1,0:T(8,128)(2,1)}, u32[]{:S(2)}) copy-start(bf16[128,1024]{1,0:T(8,128)(2,1)} %param.8) | copy-start | bytes 786436
  0.7 13.3 %copy-start.9 = (s32[8,3]{0,1:T(4,128)S(1)}, s32[8,3]{0,1:T(4,128)}, u32[]{:S(2)}) copy-start(s32[8,3]{0,1:T(4,128)} %param.11) | copy-start | bytes 292
  3.0 13.0 %collective-permute-start.1 = (bf16[128,2048]{0,1:T(8,128)(2,1)S(1)}, bf16[128,2048]{0,1:T(8,128)(2,1)S(1)}, u32[]{:S(2)}, u32[]{:S(2)}) collective-permute-start(bf16[128,2048]{0,1:T(8,128)(2,1)S(1)} %pad_maximum_fusion.3), channel_id=1, source_target_pairs={{4,0},{8,4},{12,8},{16,12},{20,16},{24,20},{28,24},{5,1},{9,5},{13... | collective-permute-start | bytes 1572872 | tf_op jit(solution)/shard_map/ppermute | solution.py:20
  5.8 13.3 %collective-permute-start = (bf16[128,2048]{0,1:T(8,128)(2,1)S(1)}, bf16[128,2048]{0,1:T(8,128)(2,1)S(1)}, u32[]{:S(2)}, u32[]{:S(2)}) collective-permute-start(bf16[128,2048]{0,1:T(8,128)(2,1)S(1)} %pad_maximum_fusion.3), channel_id=1, source_target_pairs={{0,4},{4,8},{8,12},{12,16},{16,20},{20,24},{24,28},{1,5},{5,9},{9,... | collective-permute-start | bytes 1572872 | tf_op jit(solution)/shard_map/ppermute | solution.py:20
  8.5 12.8 %collective-permute-start.2 = (bf16[32,1024]{1,0:T(8,128)(2,1)}, bf16[32,1024]{1,0:T(8,128)(2,1)S(1)}, u32[]{:S(2)}, u32[]{:S(2)}) collective-permute-start(bf16[32,1024]{1,0:T(8,128)(2,1)} %get-tuple-element.38), channel_id=1, source_target_pairs={{0,3},{1,0},{2,1},{3,2},{4,7},{5,4},{6,5},{7,6},{8,11},{9,8},{10,9... | collective-permute-start | bytes 196616 | tf_op jit(solution)/shard_map/ppermute | solution.py:91
  12.1 9.2 %collective-permute-start.4 = (bf16[32,1024]{1,0:T(8,128)(2,1)}, bf16[32,1024]{1,0:T(8,128)(2,1)}, u32[]{:S(2)}, u32[]{:S(2)}) collective-permute-start(bf16[32,1024]{1,0:T(8,128)(2,1)} %get-tuple-element.39), channel_id=1, source_target_pairs={{0,1},{1,2},{2,3},{3,0},{4,5},{5,6},{6,7},{7,4},{8,9},{9,10},{10,1... | collective-permute-start | bytes 196616 | tf_op jit(solution)/shard_map/ppermute | solution.py:91
  12.1 9.2 %collective-permute-start.3 = (bf16[32,1024]{1,0:T(8,128)(2,1)}, bf16[32,1024]{1,0:T(8,128)(2,1)}, u32[]{:S(2)}, u32[]{:S(2)}) collective-permute-start(bf16[32,1024]{1,0:T(8,128)(2,1)} %get-tuple-element.40), channel_id=1, source_target_pairs={{0,2},{1,3},{2,0},{3,1},{4,6},{5,7},{6,4},{7,5},{8,10},{9,11},{10,... | collective-permute-start | bytes 196616 | tf_op jit(solution)/shard_map/ppermute | solution.py:91
  19.4 0.9 %copy-start = (bf16[384,1024]{0,1:T(8,128)(2,1)}, bf16[384,1024]{0,1:T(8,128)(2,1)S(1)}, u32[]{:S(2)}) copy-start(bf16[384,1024]{0,1:T(8,128)(2,1)S(1)} %get-tuple-element.48) | copy-start | bytes 2359300
  19.4 1.1 %copy-start.4 = (bf16[384,1024]{0,1:T(8,128)(2,1)}, bf16[384,1024]{0,1:T(8,128)(2,1)S(1)}, u32[]{:S(2)}) copy-start(bf16[384,1024]{0,1:T(8,128)(2,1)S(1)} %get-tuple-element.47) | copy-start | bytes 2359300
  22.8 3.6 %collective-permute-start.5 = (f32[128,2]{0,1:T(2,128)S(1)}, f32[128,2]{0,1:T(2,128)S(1)}, u32[]{:S(2)}, u32[]{:S(2)}) collective-permute-start(f32[128,2]{0,1:T(2,128)S(1)} %pad_maximum_fusion.4), channel_id=1, source_target_pairs={{0,1},{1,0},{2,3},{3,2},{4,5},{5,4},{6,7},{7,6},{8,9},{9,8},{10,11... | collective-permute-start | bytes 3080 | tf_op jit(solution)/shard_map/ppermute | solution.py:59
  26.4 4.5 %collective-permute-start.6 = (f32[128,2]{0,1:T(2,128)S(1)}, f32[128,2]{0,1:T(2,128)S(1)}, u32[]{:S(2)}, u32[]{:S(2)}) collective-permute-start(f32[128,2]{0,1:T(2,128)S(1)} %fusion.32), channel_id=1, source_target_pairs={{0,2},{1,3},{2,0},{3,1},{4,6},{5,7},{6,4},{7,5},{8,10},{9,11},{10,... | collective-permute-start | bytes 3080 | tf_op jit(solution)/shard_map/ppermute | solution.py:59
  31.2 1.1 %copy-start.5 = (bf16[384,1024]{0,1:T(8,128)(2,1)S(1)}, bf16[384,1024]{0,1:T(8,128)(2,1)}, u32[]{:S(2)}) copy-start(bf16[384,1024]{0,1:T(8,128)(2,1)} %copy-done.4) | copy-start | bytes 2359300
  32.9 0.9 %copy-start.2 = (bf16[8,128,384]{1,2,0:T(8,128)(2,1)}, bf16[8,128,384]{1,2,0:T(8,128)(2,1)S(1)}, u32[]{:S(2)}) copy-start(bf16[8,128,384]{1,2,0:T(8,128)(2,1)S(1)} %multiply_convert_fusion) | copy-start | bytes 2359300
  37.4 5.4 %copy-start.6 = (f32[128,1024]{1,0:T(8,128)S(1)}, f32[128,1024]{1,0:T(8,128)}, u32[]{:S(2)}) copy-start(f32[128,1024]{1,0:T(8,128)} %copy.79) | copy-start | bytes 1572868
  37.4 11.7 %copy-start.1 = (bf16[384,1024]{0,1:T(8,128)(2,1)S(1)}, bf16[384,1024]{0,1:T(8,128)(2,1)}, u32[]{:S(2)}) copy-start(bf16[384,1024]{0,1:T(8,128)(2,1)} %copy-done) | copy-start | bytes 2359300
  37.4 11.7 %copy-start.3 = (bf16[8,128,384]{1,2,0:T(8,128)(2,1)S(1)}, bf16[8,128,384]{1,2,0:T(8,128)(2,1)}, u32[]{:S(2)}) copy-start(bf16[8,128,384]{1,2,0:T(8,128)(2,1)} %copy-done.2) | copy-start | bytes 2359300
  38.5 17.4 %collective-permute-start.10 = (bf16[128,2048]{0,1:T(8,128)(2,1)}, bf16[128,2048]{0,1:T(8,128)(2,1)}, u32[]{:S(2)}, u32[]{:S(2)}) collective-permute-start(bf16[128,2048]{0,1:T(8,128)(2,1)} %get-tuple-element.25), channel_id=1, source_target_pairs={{4,0},{8,4},{12,8},{16,12},{20,16},{24,20},{28,24},{5,1},{9,5},{13... | collective-permute-start | bytes 1572872 | tf_op jit(solution)/shard_map/ppermute | solution.py:20
  40.4 15.5 %collective-permute-start.11 = (bf16[128,2048]{0,1:T(8,128)(2,1)}, bf16[128,2048]{0,1:T(8,128)(2,1)}, u32[]{:S(2)}, u32[]{:S(2)}) collective-permute-start(bf16[128,2048]{0,1:T(8,128)(2,1)} %get-tuple-element.26), channel_id=1, source_target_pairs={{0,4},{4,8},{8,12},{12,16},{16,20},{20,24},{24,28},{1,5},{5,9},{9,... | collective-permute-start | bytes 1572872 | tf_op jit(solution)/shard_map/ppermute | solution.py:20
  43.6 6.9 %collective-permute-start.9 = (bf16[32,1024]{1,0:T(8,128)(2,1)}, bf16[32,1024]{1,0:T(8,128)(2,1)S(1)}, u32[]{:S(2)}, u32[]{:S(2)}) collective-permute-start(bf16[32,1024]{1,0:T(8,128)(2,1)} %get-tuple-element.33), channel_id=1, source_target_pairs={{0,1},{1,2},{2,3},{3,0},{4,5},{5,6},{6,7},{7,4},{8,9},{9,10},{10,1... | collective-permute-start | bytes 196616 | tf_op jit(solution)/shard_map/ppermute | solution.py:110
  45.2 8.4 %collective-permute-start.8 = (bf16[32,1024]{1,0:T(8,128)(2,1)}, bf16[32,1024]{1,0:T(8,128)(2,1)}, u32[]{:S(2)}, u32[]{:S(2)}) collective-permute-start(bf16[32,1024]{1,0:T(8,128)(2,1)} %get-tuple-element.34), channel_id=1, source_target_pairs={{0,2},{1,3},{2,0},{3,1},{4,6},{5,7},{6,4},{7,5},{8,10},{9,11},{10,... | collective-permute-start | bytes 196616 | tf_op jit(solution)/shard_map/ppermute | solution.py:110
  47.8 6.1 %collective-permute-start.7 = (bf16[32,1024]{1,0:T(8,128)(2,1)}, bf16[32,1024]{1,0:T(8,128)(2,1)}, u32[]{:S(2)}, u32[]{:S(2)}) collective-permute-start(bf16[32,1024]{1,0:T(8,128)(2,1)} %get-tuple-element.35), channel_id=1, source_target_pairs={{0,3},{1,0},{2,1},{3,2},{4,7},{5,4},{6,5},{7,6},{8,11},{9,8},{10,9... | collective-permute-start | bytes 196616 | tf_op jit(solution)/shard_map/ppermute | solution.py:110

commit v4 on v3

--- a/solution.py
+++ b/solution.py
@@ -1,6 +1,10 @@
+import functools
+
 import jax
 import jax.numpy as jnp
 from jax import lax
+from jax.experimental import pallas as pl
+from jax.experimental.pallas import tpu as pltpu
 from jax.sharding import PartitionSpec as P
 
 HSZ = 128
@@ -113,12 +117,111 @@
     return jnp.moveaxis(ordered, 0, 1).reshape(rows, -1)
 
 
+def _nt(a, b):
+    return lax.dot_general(a, b, (((1,), (1,)), ((), ())), preferred_element_type=jnp.float32)
+
+
+def _nn(a, b):
+    return lax.dot_general(a, b, (((1,), (0,)), ((), ())), preferred_element_type=jnp.float32)
+
+
+def _tn(a, b):
+    return lax.dot_general(a, b, (((0,), (0,)), ((), ())), preferred_element_type=jnp.float32)
+
+
+def _scores(mask_ref, q, keys, scale):
+    parts = []
+    for c, k in enumerate(keys):
+        s = _nt(q, k) * scale
+        parts.append(jnp.where(mask_ref[c] > 0, s, NEGATIVE))
+    return jnp.concatenate(parts, axis=1)
+
+
+def _window(k_ref, v_ref, prev_ref, next_ref, h):
+    width = k_ref.shape[1]
+    cols = slice(h * HSZ, (h + 1) * HSZ)
+    far = slice(width + h * HSZ, width + (h + 1) * HSZ)
+    keys = [prev_ref[:, cols], k_ref[:, cols], next_ref[:, cols]]
+    values = [prev_ref[:, far], v_ref[:, cols], next_ref[:, far]]
+    return keys, values
+
+
+def _forward_kernel(mask_ref, q_ref, k_ref, v_ref, prev_ref, next_ref, out_ref, lse_ref, *, heads, scale):
+    for h in range(heads):
+        cols = slice(h * HSZ, (h + 1) * HSZ)
+        q = q_ref[:, cols]
+        keys, values = _window(k_ref, v_ref, prev_ref, next_ref, h)
+        s = _scores(mask_ref, q, keys, scale)
+        peak = jnp.max(s, -1, keepdims=True)
+        lse = peak + jnp.log(jnp.sum(jnp.exp(s - peak), -1, keepdims=True))
+        p = jnp.exp(s - lse).astype(jnp.bfloat16)
+        v = jnp.concatenate(values, axis=0)
+        out_ref[:, cols] = _nn(p, v).astype(out_ref.dtype)
+        lse_ref[:, h:h + 1] = lse
+
+
+def attend_forward(mask_row, q, k, v, kv_prev, kv_next):
+    length, width = q.shape
+    heads = width // HSZ
+    kern = functools.partial(_forward_kernel, heads=heads, scale=HSZ ** (-0.5))
+    vmem = pl.BlockSpec(memory_space=pltpu.VMEM)
+    return pl.pallas_call(
+        kern,
+        out_shape=(jax.ShapeDtypeStruct((length, width), jnp.bfloat16),
+                   jax.ShapeDtypeStruct((length, heads), jnp.float32)),
+        in_specs=[pl.BlockSpec(memory_space=pltpu.SMEM)] + [vmem] * 5,
+        out_specs=(vmem, vmem),
+        cost_estimate=pl.CostEstimate(
+            flops=12 * length * length * width, transcendentals=6 * length * length * heads,
+            bytes_accessed=16 * length * width),
+    )(mask_row, q, k, v, kv_prev, kv_next)
+
+
+def _backward_kernel(mask_ref, q_ref, k_ref, v_ref, kvp_ref, kvn_ref, g_ref, lse_ref, delta_ref,
+                     dq_ref, prev_ref, next_ref, own_ref, *, heads, scale):
+    length = q_ref.shape[0]
+    width = q_ref.shape[1]
+    for h in range(heads):
+        cols = slice(h * HSZ, (h + 1) * HSZ)
+        q = q_ref[:, cols]
+        g = g_ref[:, cols]
+        keys, vals = _window(k_ref, v_ref, kvp_ref, kvn_ref, h)
+        s = _scores(mask_ref, q, keys, scale)
+        p = jnp.exp(s - lse_ref[:, h:h + 1])
+        dp = jnp.concatenate([_nt(g, v) for v in vals], axis=1)
+        ds = (p * (dp - delta_ref[:, h:h + 1])).astype(jnp.bfloat16)
+        p_low = p.astype(jnp.bfloat16)
+        dq_ref[:, cols] = (_nn(ds, jnp.concatenate(keys, axis=0)) * scale).astype(dq_ref.dtype)
+        for c, ref in enumerate((prev_ref, own_ref, next_ref)):
+            blk = slice(c * length, (c + 1) * length)
+            dk = _tn(ds[:, blk], q) * scale
+            dv = _tn(p_low[:, blk], g)
+            ref[:, cols] = dk.astype(ref.dtype)
+            ref[:, width + h * HSZ:width + (h + 1) * HSZ] = dv.astype(ref.dtype)
+
+
+def attend_backward(mask_row, q, k, v, kv_prev, kv_next, grad, lse, delta):
+    length, width = q.shape
+    heads = width // HSZ
+    kern = functools.partial(_backward_kernel, heads=heads, scale=HSZ ** (-0.5))
+    vmem = pl.BlockSpec(memory_space=pltpu.VMEM)
+    sent = jax.ShapeDtypeStruct((length, 2 * width), jnp.bfloat16)
+    return pl.pallas_call(
+        kern,
+        out_shape=(jax.ShapeDtypeStruct((length, width), jnp.bfloat16), sent, sent,
+                   jax.ShapeDtypeStruct((length, 2 * width), jnp.float32)),
+        in_specs=[pl.BlockSpec(memory_space=pltpu.SMEM)] + [vmem] * 8,
+        out_specs=(vmem, vmem, vmem, vmem),
+        cost_estimate=pl.CostEstimate(
+            flops=30 * length * length * width, transcendentals=3 * length * length * heads,
+            bytes_accessed=36 * length * width),
+    )(mask_row, q, k, v, kv_prev, kv_next, grad, lse, delta)
+
+
 def per_device(queries, key_rows, value_rows, view_mask, norm_gain, normed_grad):
     length = queries.shape[0]
     width = queries.shape[1]
     features = norm_gain.shape[0]
-    span_blocks = 2 * REACH - 1
-    score_scale = HSZ ** (-0.5)
     position = lax.axis_index("ctx")
     part = lax.axis_index("tp")
 
@@ -128,27 +231,9 @@
     both = jnp.concatenate([key_rows, value_rows], axis=1)
     from_prev = passed_along(both, "ctx", 1)
     from_next = passed_along(both, "ctx", -1)
-    key_ext = jnp.concatenate([from_prev[:, :width], key_rows, from_next[:, :width]], axis=0)
-    value_ext = jnp.concatenate([from_prev[:, width:], value_rows, from_next[:, width:]], axis=0)
-
     mask_row = lax.dynamic_slice_in_dim(view_mask, position, 1, 0)[0]
-    key_live = jnp.repeat(mask_row, length) > 0
-    q_heads = split_heads(queries)
-    k_heads = split_heads(key_ext)
-    v_heads = split_heads(value_ext)
-    scores = (
-        jnp.einsum("thd,shd->hts", q_heads, k_heads, preferred_element_type=jnp.float32)
-        * score_scale
-    )
-    scores = jnp.where(key_live[None, None, :], scores, NEGATIVE)
-    peak = jnp.max(scores, -1, keepdims=True)
-    log_total = peak + jnp.log(jnp.sum(jnp.exp(scores - peak), -1, keepdims=True))
-    probs = jnp.exp(scores - log_total)
-    probs_low = probs.astype(jnp.bfloat16)
-    out_heads = jnp.einsum(
-        "hts,shd->thd", probs_low, v_heads, preferred_element_type=jnp.float32
-    ).astype(jnp.bfloat16)
-    attended = out_heads.reshape(length, -1)
+    attended, log_total = attend_forward(mask_row, queries, key_rows, value_rows, from_prev, from_next)
+    out_heads = split_heads(attended)
 
     values_f = attended.astype(jnp.float32)
     upstream = grad_tiles.astype(jnp.float32) * gain_local
@@ -166,32 +251,12 @@
 
     grad_heads = split_heads(attended_grad)
     delta = jnp.sum(grad_heads.astype(jnp.float32) * out_heads.astype(jnp.float32), -1)
-    prob_grad = jnp.einsum("thd,shd->hts", grad_heads, v_heads, preferred_element_type=jnp.float32)
-    score_grad = (probs * (prob_grad - delta.T[:, :, None])).astype(jnp.bfloat16)
-    query_grad = (
-        (
-            jnp.einsum("hts,shd->thd", score_grad, k_heads, preferred_element_type=jnp.float32)
-            * score_scale
-        )
-        .astype(jnp.bfloat16)
-        .reshape(length, -1)
-    )
-    key_terms = (
-        jnp.einsum("hts,thd->shd", score_grad, q_heads, preferred_element_type=jnp.float32)
-        * score_scale
-    ).reshape(span_blocks * length, -1)
-    value_terms = jnp.einsum(
-        "hts,thd->shd", probs_low, grad_heads, preferred_element_type=jnp.float32
-    ).reshape(span_blocks * length, -1)
-    terms = jnp.concatenate([key_terms, value_terms], axis=1)
-    total = terms[length : 2 * length]
-    to_prev = terms[:length].astype(jnp.bfloat16)
-    to_next = terms[2 * length :].astype(jnp.bfloat16)
-    total = total + passed_along(to_prev, "ctx", -1).astype(jnp.float32)
+    query_grad, to_prev, to_next, own = attend_backward(
+        mask_row, queries, key_rows, value_rows, from_prev, from_next, attended_grad, log_total, delta)
+    total = own + passed_along(to_prev, "ctx", -1).astype(jnp.float32)
     total = total + passed_along(to_next, "ctx", 1).astype(jnp.float32)
     total = total.astype(jnp.bfloat16)
     return (normed, query_grad, total[:, :width], total[:, width:])
-
 
 def solution(mesh):
     placed = (P("ctx", "tp"), P("ctx", "tp"), P("ctx", "tp"), P(), P(), P(("ctx", "tp"), None))

time: 59.8 us -> 59.6 us (level)
  Pallas kernels: 0 us -> 11.1 us
  local copies, waits for them, and re-layouts: 15.3 us -> 5.69 us
  waiting for transfers between devices: 10.2 us -> 16 us
  matrix products: 3.87 us -> 0 us
  starting transfers between devices: 23.4 us -> 21.7 us
  other arithmetic: 5.2 us -> 3.89 us
    pallas_call x0 -> x2, Pallas kernels: none -> 11.1 us  [the longest x1 5.74 us: attend_backward(): pl.pallas_call(kern, out_shape=(jax.ShapeDtypeStruct((length, width), jnp...]
    ppermute x3, waiting for transfers between devices: 0.01 us -> 4.8 us  [tiles_to_heads(): chunk = lax.ppermute(chunk, 'tp', [(i, (i + shift) % n) for i in range(n)])]
    unnamed x26 -> x16, local copies, waits for them, and re-layouts: 6.85 us -> 2.69 us
    dot_general x6 -> x0, matrix products: 3.87 us -> none  [the longest x1 1.55 us: per_device(): jnp.einsum('hts,thd->shd', score_grad, q_heads, preferred_element_type=jn...]
    ppermute x2, waiting for transfers between devices: 1.83 us -> 5.28 us  [tp_sum(): lax.ppermute(total, 'tp', [(i, i ^ 1 << b) for i in range(peers)])]
    ppermute x4, waiting for transfers between devices: 4.84 us -> 1.41 us  [passed_along(): return lax.ppermute(x, axis, pairs)]
    mul x2 -> x0, local copies, waits for them, and re-layouts: 2.56 us -> none  [the longest x1 1.87 us: per_device(): jnp.einsum('hts,thd->shd', score_grad, q_heads, preferred_element_type=jn...]
    convert_element_type x4 -> x0, local copies, waits for them, and re-layouts: 1.57 us -> none  [the longest x3 1.34 us: per_device(): values_f = attended.astype(jnp.float32)]
  transfers between devices with their start and end apart: 12 -> 12, of which waited for: 7 -> 10; matrix products, arithmetic and copies ran while one was open for 16% -> 5% of each run, Pallas kernels for 0% -> 0%
where the time goes in v4:
time: 59.6 us; the launch traced here: 59.3 us
  starting transfers between devices  21.7 us (36%)
  waiting for transfers between devices  16 us (27%)
  Pallas kernels  11.1 us (19%)
  local copies, waits for them, and re-layouts  5.69 us (10%)
  other arithmetic  3.89 us (7%)
  between operations  0.89 us (1%)
    ppermute x4, starting transfers between devices, passed_along(): return lax.ppermute(x, axis, pairs)  9.28 us
    pallas_call x1, Pallas kernels, attend_backward(): pl.pallas_call(kern, out_shape=(jax.ShapeDtypeStruct((length, width), jnp...  5.74 us
    pallas_call x1, Pallas kernels, attend_forward(): pl.pallas_call(kern, out_shape=(jax.ShapeDtypeStruct((length, width), jnp...  5.4 us
    ppermute x2, waiting for transfers between devices, tp_sum(): lax.ppermute(total, 'tp', [(i, i ^ 1 << b) for i in range(peers)])  5.28 us
    ppermute x3, starting transfers between devices, heads_to_tiles(): chunk = lax.ppermute(chunk, 'tp', [(i, (i + shift) % n) for i in range(n)])  4.86 us
    ppermute x3, waiting for transfers between devices, tiles_to_heads(): chunk = lax.ppermute(chunk, 'tp', [(i, (i + shift) % n) for i in range(n)])  4.8 us
    ppermute x3, starting transfers between devices, tiles_to_heads(): chunk = lax.ppermute(chunk, 'tp', [(i, (i + shift) % n) for i in range(n)])  4.67 us
    ppermute x3, waiting for transfers between devices, heads_to_tiles(): chunk = lax.ppermute(chunk, 'tp', [(i, (i + shift) % n) for i in range(n)])  4.47 us
  transfers between devices with their start and end apart: 12, of which 10 were waited for; matrix products, arithmetic and copies ran while one was open for 5% of the time, Pallas kernels for 0%

profile of v4, /device:TPU:4, one launch (start us, length us, event | category | flops | bytes accessed | tf_op | source)
XLA Modules:
  0.0 59.3 jit_solution(8479733097681706260)
XLA Ops:
  0.7 1.0 %constant_dynamic-update-slice_fusion.1 = bf16[128,2048]{1,0:T(8,128)(2,1)S(1)} fusion(bf16[128,1024]{1,0:T(8,128)(2,1)} %k_ref.3), kind=kLoop, calls=%fused_computation.58 | loop fusion | bytes 524288
  1.7 2.9 %collective-permute-start.1 = (bf16[128,2048]{1,0:T(8,128)(2,1)S(1)}, bf16[128,2048]{1,0:T(8,128)(2,1)S(1)}, u32[]{:S(2)}, u32[]{:S(2)}) collective-permute-start(bf16[128,2048]{1,0:T(8,128)(2,1)S(1)} %constant_dynamic-update-slice_fusion), channel_id=1, source_target_pairs={{4,0},{8,4},{12,8},{16,12},{20,16},{24,20},{28,24},{5,1},{9,5},{13... | collective-permute-start | bytes 1572872 | tf_op jit(solution)/shard_map/ppermute | solution.py:24
  4.6 1.9 %collective-permute-start = (bf16[128,2048]{1,0:T(8,128)(2,1)S(1)}, bf16[128,2048]{1,0:T(8,128)(2,1)S(1)}, u32[]{:S(2)}, u32[]{:S(2)}) collective-permute-start(bf16[128,2048]{1,0:T(8,128)(2,1)S(1)} %constant_dynamic-update-slice_fusion), channel_id=1, source_target_pairs={{0,4},{4,8},{8,12},{12,16},{16,20},{20,24},{24,28},{1,5},{5,9},{9,... | collective-permute-start | bytes 1572872 | tf_op jit(solution)/shard_map/ppermute | solution.py:24
  6.7 1.6 %collective-permute-start.4 = (bf16[32,1024]{1,0:T(8,128)(2,1)S(1)}, bf16[32,1024]{1,0:T(8,128)(2,1)S(1)}, u32[]{:S(2)}, u32[]{:S(2)}) collective-permute-start(bf16[32,1024]{1,0:T(8,128)(2,1)S(1)} %get-tuple-element.28), channel_id=1, source_target_pairs={{0,1},{1,2},{2,3},{3,0},{4,5},{5,6},{6,7},{7,4},{8,9},{9,10},{10,1... | collective-permute-start | bytes 196616 | tf_op jit(solution)/shard_map/ppermute | solution.py:95
  8.3 2.2 %collective-permute-start.2 = (bf16[32,1024]{1,0:T(8,128)(2,1)S(1)}, bf16[32,1024]{1,0:T(8,128)(2,1)S(1)}, u32[]{:S(2)}, u32[]{:S(2)}) collective-permute-start(bf16[32,1024]{1,0:T(8,128)(2,1)S(1)} %get-tuple-element.29), channel_id=1, source_target_pairs={{0,3},{1,0},{2,1},{3,2},{4,7},{5,4},{6,5},{7,6},{8,11},{9,8},{10,9... | collective-permute-start | bytes 196616 | tf_op jit(solution)/shard_map/ppermute | solution.py:95
  14.2 3.4 %collective-permute-done.3 = bf16[32,1024]{1,0:T(8,128)(2,1)S(1)} collective-permute-done((bf16[32,1024]{1,0:T(8,128)(2,1)S(1)}, bf16[32,1024]{1,0:T(8,128)(2,1)S(1)}, u32[]{:S(2)}, u32[]{:S(2)}) %collective-permute-start.3) | collective-permute-done | bytes 65568 | tf_op jit(solution)/shard_map/ppermute | solution.py:95
  19.5 5.4 %shard_map.93 = (bf16[128,1024]{1,0:T(8,128)(2,1)}, f32[128,8]{1,0:T(8,128)}) custom-call(s32[3]{0:T(128)} %fusion.26.mask_ref, bf16[128,1024]{1,0:T(8,128)(2,1)} %q_ref.3, bf16[128,1024]{1,0:T(8,128)(2,1)} %k_ref.3, bf16[128,1024]{1,0:T(8,128)(2,1)} %v_ref.3, bf16[128,2048]{1,0:T(8,128)(2,1)} %copy-done.3, bf16[128,2048]{1,0:T(8,128)(2,1)} %copy-done.2), custom_call_target="tpu_custom_call" | custom-call | flops 201326592 | bytes 2097152 | tf_op jit(solution)/shard_map/pallas_call | solution.py:168
  24.9 1.2 %fusion.7 = (f32[128]{0:T(128)S(1)}, f32[128]{0:T(128)S(1)}) fusion(bf16[128,1024]{1,0:T(8,128)(2,1)} %get-tuple-element.11, f32[1024]{0:T(1024)S(1)} %dynamic_slice.38, bf16[4,32,1024]{2,1,0:T(8,128)(2,1)S(1)} %fusion.22), kind=kLoop, calls=%fused_computation.12 | loop fusion | flops 917248 | bytes 529408 | tf_op jit(solution)/shard_map/reduce_sum | solution.py:241
  26.1 0.9 %collective-permute-start.5 = (f32[128,2]{0,1:T(2,128)S(1)}, f32[128,2]{0,1:T(2,128)S(1)}, u32[]{:S(2)}, u32[]{:S(2)}) collective-permute-start(f32[128,2]{0,1:T(2,128)S(1)} %pad_maximum_fusion), channel_id=1, source_target_pairs={{0,1},{1,0},{2,3},{3,2},{4,5},{5,4},{6,7},{7,6},{8,9},{9,8},{10,11... | collective-permute-start | bytes 3080 | tf_op jit(solution)/shard_map/ppermute | solution.py:63
  27.1 2.7 %collective-permute-done.5 = f32[128,2]{0,1:T(2,128)S(1)} collective-permute-done((f32[128,2]{0,1:T(2,128)S(1)}, f32[128,2]{0,1:T(2,128)S(1)}, u32[]{:S(2)}, u32[]{:S(2)}) %collective-permute-start.5) | collective-permute-done | bytes 1056 | tf_op jit(solution)/shard_map/ppermute | solution.py:63
  29.8 1.9 %collective-permute-start.6 = (f32[128,2]{0,1:T(2,128)S(1)}, f32[128,2]{0,1:T(2,128)S(1)}, u32[]{:S(2)}, u32[]{:S(2)}) collective-permute-start(f32[128,2]{0,1:T(2,128)S(1)} %fusion.27), channel_id=1, source_target_pairs={{0,2},{1,3},{2,0},{3,1},{4,6},{5,7},{6,4},{7,5},{8,10},{9,11},{10,... | collective-permute-start | bytes 3080 | tf_op jit(solution)/shard_map/ppermute | solution.py:63
  31.7 2.6 %collective-permute-done.6 = f32[128,2]{0,1:T(2,128)S(1)} collective-permute-done((f32[128,2]{0,1:T(2,128)S(1)}, f32[128,2]{0,1:T(2,128)S(1)}, u32[]{:S(2)}, u32[]{:S(2)}) %collective-permute-start.6) | collective-permute-done | bytes 1056 | tf_op jit(solution)/shard_map/ppermute | solution.py:63
  34.4 1.0 %fusion.9 = (f32[16,8,8,128]{3,1,2,0:T(8,128)S(1)}, bf16[128,1024]{1,0:T(8,128)(2,1)}, bf16[128,1024]{1,0:T(8,128)(2,1)S(1)}) fusion(bf16[128,1024]{1,0:T(8,128)(2,1)S(1)} %copy-done.5, f32[128]{0:T(128)S(1)} %get-tuple-element.32, f32[1024]{0:T(1024)S(1)} %dynamic_slice.38, bf16[4,32,1024]{2,1,0:T(8,128)(2,1)S(1)} %fusion.22, f32[128]{0:T(128)S(1)} %get-tuple-element.33), kind=kLoop, calls=%fused_computation.14 | loop fusion | flops 1835008 | bytes 1577984
  35.4 0.8 %reduce_sum.29.delta_ref = f32[128,8]{1,0:T(8,128)} reduce(f32[128,8,128]{2,1,0:T(8,128)S(1)} %bitcast.28, f32[]{:T(128)} %constant.71.clone.1), dimensions={2}, to_apply=%region_2.4 | reduce | flops 130048 | bytes 528388 | tf_op jit(solution)/shard_map/reduce_sum | solution.py:253
  36.3 5.7 %shard_map.94 = (bf16[128,1024]{1,0:T(8,128)(2,1)}, bf16[128,2048]{1,0:T(8,128)(2,1)}, bf16[128,2048]{1,0:T(8,128)(2,1)}, f32[128,2048]{1,0:T(8,128)}) custom-call(s32[3]{0:T(128)} %fusion.26.mask_ref, bf16[128,1024]{1,0:T(8,128)(2,1)} %q_ref.3, bf16[128,1024]{1,0:T(8,128)(2,1)} %k_ref.3, bf16[128,1024]{1,0:T(8,128)(2,1)} %v_ref.3, ...), custom_call_target="tpu_custom_call" | custom-call | flops 503316480 | bytes 4718592 | tf_op jit(solution)/shard_map/pallas_call | solution.py:209
  42.0 2.0 %collective-permute-start.10 = (bf16[128,2048]{1,0:T(8,128)(2,1)}, bf16[128,2048]{1,0:T(8,128)(2,1)S(1)}, u32[]{:S(2)}, u32[]{:S(2)}) collective-permute-start(bf16[128,2048]{1,0:T(8,128)(2,1)} %get-tuple-element.15), channel_id=1, source_target_pairs={{4,0},{8,4},{12,8},{16,12},{20,16},{24,20},{28,24},{5,1},{9,5},{13... | collective-permute-start | bytes 1572872 | tf_op jit(solution)/shard_map/ppermute | solution.py:24
  44.1 2.4 %collective-permute-start.11 = (bf16[128,2048]{1,0:T(8,128)(2,1)}, bf16[128,2048]{1,0:T(8,128)(2,1)S(1)}, u32[]{:S(2)}, u32[]{:S(2)}) collective-permute-start(bf16[128,2048]{1,0:T(8,128)(2,1)} %get-tuple-element.16), channel_id=1, source_target_pairs={{0,4},{4,8},{8,12},{12,16},{16,20},{20,24},{24,28},{1,5},{5,9},{9,... | collective-permute-start | bytes 1572872 | tf_op jit(solution)/shard_map/ppermute | solution.py:24
  46.6 0.9 %collective-permute-start.9 = (bf16[32,1024]{1,0:T(8,128)(2,1)S(1)}, bf16[32,1024]{1,0:T(8,128)(2,1)S(1)}, u32[]{:S(2)}, u32[]{:S(2)}) collective-permute-start(bf16[32,1024]{1,0:T(8,128)(2,1)S(1)} %get-tuple-element.24), channel_id=1, source_target_pairs={{0,1},{1,2},{2,3},{3,0},{4,5},{5,6},{6,7},{7,4},{8,9},{9,10},{10,1... | collective-permute-start | bytes 196616 | tf_op jit(solution)/shard_map/ppermute | solution.py:114
  47.5 2.6 %collective-permute-start.8 = (bf16[32,1024]{1,0:T(8,128)(2,1)S(1)}, bf16[32,1024]{1,0:T(8,128)(2,1)S(1)}, u32[]{:S(2)}, u32[]{:S(2)}) collective-permute-start(bf16[32,1024]{1,0:T(8,128)(2,1)S(1)} %get-tuple-element.25), channel_id=1, source_target_pairs={{0,2},{1,3},{2,0},{3,1},{4,6},{5,7},{6,4},{7,5},{8,10},{9,11},{10,... | collective-permute-start | bytes 196616 | tf_op jit(solution)/shard_map/ppermute | solution.py:114
  50.1 1.3 %collective-permute-start.7 = (bf16[32,1024]{1,0:T(8,128)(2,1)S(1)}, bf16[32,1024]{1,0:T(8,128)(2,1)S(1)}, u32[]{:S(2)}, u32[]{:S(2)}) collective-permute-start(bf16[32,1024]{1,0:T(8,128)(2,1)S(1)} %get-tuple-element.26), channel_id=1, source_target_pairs={{0,3},{1,0},{2,1},{3,2},{4,7},{5,4},{6,5},{7,6},{8,11},{9,8},{10,9... | collective-permute-start | bytes 196616 | tf_op jit(solution)/shard_map/ppermute | solution.py:114
  51.4 1.6 %collective-permute-done.9 = bf16[32,1024]{1,0:T(8,128)(2,1)S(1)} collective-permute-done((bf16[32,1024]{1,0:T(8,128)(2,1)S(1)}, bf16[32,1024]{1,0:T(8,128)(2,1)S(1)}, u32[]{:S(2)}, u32[]{:S(2)}) %collective-permute-start.9) | collective-permute-done | bytes 65568 | tf_op jit(solution)/shard_map/ppermute | solution.py:114
  53.0 2.7 %collective-permute-done.8 = bf16[32,1024]{1,0:T(8,128)(2,1)S(1)} collective-permute-done((bf16[32,1024]{1,0:T(8,128)(2,1)S(1)}, bf16[32,1024]{1,0:T(8,128)(2,1)S(1)}, u32[]{:S(2)}, u32[]{:S(2)}) %collective-permute-start.8) | collective-permute-done | bytes 65568 | tf_op jit(solution)/shard_map/ppermute | solution.py:114
  56.9 1.3 %collective-permute-done.11 = bf16[128,2048]{1,0:T(8,128)(2,1)S(1)} collective-permute-done((bf16[128,2048]{1,0:T(8,128)(2,1)}, bf16[128,2048]{1,0:T(8,128)(2,1)S(1)}, u32[]{:S(2)}, u32[]{:S(2)}) %collective-permute-start.11) | collective-permute-done | bytes 524320 | tf_op jit(solution)/shard_map/ppermute | solution.py:24
  58.4 0.8 %fusion.29 = (bf16[128,1024]{1,0:T(8,128)(2,1)}, bf16[128,1024]{1,0:T(8,128)(2,1)}) fusion(bf16[128,2048]{1,0:T(8,128)(2,1)S(1)} %add_convert_fusion), kind=kLoop, calls=%fused_computation.64 | loop fusion | bytes 1048576 | tf_op jit(solution)/shard_map/slice | solution.py:259
  (35 shorter events, 7.2 us)
Async XLA Ops:
  0.6 10.7 %copy-start = (s32[8,3]{0,1:T(4,128)S(1)}, s32[8,3]{0,1:T(4,128)}, u32[]{:S(2)}) copy-start(s32[8,3]{0,1:T(4,128)} %param.11) | copy-start | bytes 292
  0.6 1.0 %copy-start.1 = (bf16[128,1024]{1,0:T(8,128)(2,1)S(1)}, bf16[128,1024]{1,0:T(8,128)(2,1)}, u32[]{:S(2)}) copy-start(bf16[128,1024]{1,0:T(8,128)(2,1)} %v_ref.3) | copy-start | bytes 786436
  1.7 5.0 %copy-start.6 = (bf16[32,4096]{1,0:T(8,128)(2,1)S(1)}, bf16[32,4096]{1,0:T(8,128)(2,1)}, u32[]{:S(2)}) copy-start(bf16[32,4096]{1,0:T(8,128)(2,1)} %param.13) | copy-start | bytes 786436
  1.7 16.1 %collective-permute-start.1 = (bf16[128,2048]{1,0:T(8,128)(2,1)S(1)}, bf16[128,2048]{1,0:T(8,128)(2,1)S(1)}, u32[]{:S(2)}, u32[]{:S(2)}) collective-permute-start(bf16[128,2048]{1,0:T(8,128)(2,1)S(1)} %constant_dynamic-update-slice_fusion), channel_id=1, source_target_pairs={{4,0},{8,4},{12,8},{16,12},{20,16},{24,20},{28,24},{5,1},{9,5},{13... | collective-permute-start | bytes 1572872 | tf_op jit(solution)/shard_map/ppermute | solution.py:24
  4.6 13.3 %collective-permute-start = (bf16[128,2048]{1,0:T(8,128)(2,1)S(1)}, bf16[128,2048]{1,0:T(8,128)(2,1)S(1)}, u32[]{:S(2)}, u32[]{:S(2)}) collective-permute-start(bf16[128,2048]{1,0:T(8,128)(2,1)S(1)} %constant_dynamic-update-slice_fusion), channel_id=1, source_target_pairs={{0,4},{4,8},{8,12},{12,16},{16,20},{20,24},{24,28},{1,5},{5,9},{9,... | collective-permute-start | bytes 1572872 | tf_op jit(solution)/shard_map/ppermute | solution.py:24
  6.7 6.8 %collective-permute-start.4 = (bf16[32,1024]{1,0:T(8,128)(2,1)S(1)}, bf16[32,1024]{1,0:T(8,128)(2,1)S(1)}, u32[]{:S(2)}, u32[]{:S(2)}) collective-permute-start(bf16[32,1024]{1,0:T(8,128)(2,1)S(1)} %get-tuple-element.28), channel_id=1, source_target_pairs={{0,1},{1,2},{2,3},{3,0},{4,5},{5,6},{6,7},{7,4},{8,9},{9,10},{10,1... | collective-permute-start | bytes 196616 | tf_op jit(solution)/shard_map/ppermute | solution.py:95
  8.3 5.9 %collective-permute-start.2 = (bf16[32,1024]{1,0:T(8,128)(2,1)S(1)}, bf16[32,1024]{1,0:T(8,128)(2,1)S(1)}, u32[]{:S(2)}, u32[]{:S(2)}) collective-permute-start(bf16[32,1024]{1,0:T(8,128)(2,1)S(1)} %get-tuple-element.29), channel_id=1, source_target_pairs={{0,3},{1,0},{2,1},{3,2},{4,7},{5,4},{6,5},{7,6},{8,11},{9,8},{10,9... | collective-permute-start | bytes 196616 | tf_op jit(solution)/shard_map/ppermute | solution.py:95
  10.6 7.0 %collective-permute-start.3 = (bf16[32,1024]{1,0:T(8,128)(2,1)S(1)}, bf16[32,1024]{1,0:T(8,128)(2,1)S(1)}, u32[]{:S(2)}, u32[]{:S(2)}) collective-permute-start(bf16[32,1024]{1,0:T(8,128)(2,1)S(1)} %get-tuple-element.31), channel_id=1, source_target_pairs={{0,2},{1,3},{2,0},{3,1},{4,6},{5,7},{6,4},{7,5},{8,10},{9,11},{10,... | collective-permute-start | bytes 196616 | tf_op jit(solution)/shard_map/ppermute | solution.py:95
  17.9 0.8 %copy-start.2 = (bf16[128,2048]{1,0:T(8,128)(2,1)}, bf16[128,2048]{1,0:T(8,128)(2,1)S(1)}, u32[]{:S(2)}) copy-start(bf16[128,2048]{1,0:T(8,128)(2,1)S(1)} %collective-permute-done.1.next_ref.kvn_ref) | copy-start | bytes 1572868
  18.7 0.8 %copy-start.3 = (bf16[128,2048]{1,0:T(8,128)(2,1)}, bf16[128,2048]{1,0:T(8,128)(2,1)S(1)}, u32[]{:S(2)}) copy-start(bf16[128,2048]{1,0:T(8,128)(2,1)S(1)} %collective-permute-done.prev_ref.kvp_ref) | copy-start | bytes 1572868
  24.9 9.4 %copy-start.5 = (bf16[128,1024]{1,0:T(8,128)(2,1)S(1)}, bf16[128,1024]{1,0:T(8,128)(2,1)}, u32[]{:S(2)}) copy-start(bf16[128,1024]{1,0:T(8,128)(2,1)} %get-tuple-element.11) | copy-start | bytes 786436
  26.1 3.6 %collective-permute-start.5 = (f32[128,2]{0,1:T(2,128)S(1)}, f32[128,2]{0,1:T(2,128)S(1)}, u32[]{:S(2)}, u32[]{:S(2)}) collective-permute-start(f32[128,2]{0,1:T(2,128)S(1)} %pad_maximum_fusion), channel_id=1, source_target_pairs={{0,1},{1,0},{2,3},{3,2},{4,5},{5,4},{6,7},{7,6},{8,9},{9,8},{10,11... | collective-permute-start | bytes 3080 | tf_op jit(solution)/shard_map/ppermute | solution.py:63
  29.8 4.5 %collective-permute-start.6 = (f32[128,2]{0,1:T(2,128)S(1)}, f32[128,2]{0,1:T(2,128)S(1)}, u32[]{:S(2)}, u32[]{:S(2)}) collective-permute-start(f32[128,2]{0,1:T(2,128)S(1)} %fusion.27), channel_id=1, source_target_pairs={{0,2},{1,3},{2,0},{3,1},{4,6},{5,7},{6,4},{7,5},{8,10},{9,11},{10,... | collective-permute-start | bytes 3080 | tf_op jit(solution)/shard_map/ppermute | solution.py:63
  42.0 16.2 %copy-start.4 = (f32[128,2048]{1,0:T(8,128)S(1)}, f32[128,2048]{1,0:T(8,128)}, u32[]{:S(2)}) copy-start(f32[128,2048]{1,0:T(8,128)} %get-tuple-element.14) | copy-start | bytes 3145732
  42.0 14.9 %collective-permute-start.10 = (bf16[128,2048]{1,0:T(8,128)(2,1)}, bf16[128,2048]{1,0:T(8,128)(2,1)S(1)}, u32[]{:S(2)}, u32[]{:S(2)}) collective-permute-start(bf16[128,2048]{1,0:T(8,128)(2,1)} %get-tuple-element.15), channel_id=1, source_target_pairs={{4,0},{8,4},{12,8},{16,12},{20,16},{24,20},{28,24},{5,1},{9,5},{13... | collective-permute-start | bytes 1572872 | tf_op jit(solution)/shard_map/ppermute | solution.py:24
  44.1 14.2 %collective-permute-start.11 = (bf16[128,2048]{1,0:T(8,128)(2,1)}, bf16[128,2048]{1,0:T(8,128)(2,1)S(1)}, u32[]{:S(2)}, u32[]{:S(2)}) collective-permute-start(bf16[128,2048]{1,0:T(8,128)(2,1)} %get-tuple-element.16), channel_id=1, source_target_pairs={{0,4},{4,8},{8,12},{12,16},{16,20},{20,24},{24,28},{1,5},{5,9},{9,... | collective-permute-start | bytes 1572872 | tf_op jit(solution)/shard_map/ppermute | solution.py:24
  46.6 6.5 %collective-permute-start.9 = (bf16[32,1024]{1,0:T(8,128)(2,1)S(1)}, bf16[32,1024]{1,0:T(8,128)(2,1)S(1)}, u32[]{:S(2)}, u32[]{:S(2)}) collective-permute-start(bf16[32,1024]{1,0:T(8,128)(2,1)S(1)} %get-tuple-element.24), channel_id=1, source_target_pairs={{0,1},{1,2},{2,3},{3,0},{4,5},{5,6},{6,7},{7,4},{8,9},{9,10},{10,1... | collective-permute-start | bytes 196616 | tf_op jit(solution)/shard_map/ppermute | solution.py:114
  47.5 8.3 %collective-permute-start.8 = (bf16[32,1024]{1,0:T(8,128)(2,1)S(1)}, bf16[32,1024]{1,0:T(8,128)(2,1)S(1)}, u32[]{:S(2)}, u32[]{:S(2)}) collective-permute-start(bf16[32,1024]{1,0:T(8,128)(2,1)S(1)} %get-tuple-element.25), channel_id=1, source_target_pairs={{0,2},{1,3},{2,0},{3,1},{4,6},{5,7},{6,4},{7,5},{8,10},{9,11},{10,... | collective-permute-start | bytes 196616 | tf_op jit(solution)/shard_map/ppermute | solution.py:114
  50.1 5.8 %collective-permute-start.7 = (bf16[32,1024]{1,0:T(8,128)(2,1)S(1)}, bf16[32,1024]{1,0:T(8,128)(2,1)S(1)}, u32[]{:S(2)}, u32[]{:S(2)}) collective-permute-start(bf16[32,1024]{1,0:T(8,128)(2,1)S(1)} %get-tuple-element.26), channel_id=1, source_target_pairs={{0,3},{1,0},{2,1},{3,2},{4,7},{5,4},{6,5},{7,6},{8,11},{9,8},{10,9... | collective-permute-start | bytes 196616 | tf_op jit(solution)/shard_map/ppermute | solution.py:114

commit v5 on v4

--- a/solution.py
+++ b/solution.py
@@ -147,16 +147,20 @@
 
 
 def _forward_kernel(mask_ref, q_ref, k_ref, v_ref, prev_ref, next_ref, out_ref, lse_ref, *, heads, scale):
+    def scores(h):
+        keys, values = _window(k_ref, v_ref, prev_ref, next_ref, h)
+        return _scores(mask_ref, q_ref[:, h * HSZ:(h + 1) * HSZ], keys, scale), values
+
+    ahead = scores(0)
     for h in range(heads):
-        cols = slice(h * HSZ, (h + 1) * HSZ)
-        q = q_ref[:, cols]
-        keys, values = _window(k_ref, v_ref, prev_ref, next_ref, h)
-        s = _scores(mask_ref, q, keys, scale)
+        s, values = ahead
+        if h + 1 < heads:
+            ahead = scores(h + 1)
         peak = jnp.max(s, -1, keepdims=True)
         lse = peak + jnp.log(jnp.sum(jnp.exp(s - peak), -1, keepdims=True))
         p = jnp.exp(s - lse).astype(jnp.bfloat16)
         v = jnp.concatenate(values, axis=0)
-        out_ref[:, cols] = _nn(p, v).astype(out_ref.dtype)
+        out_ref[:, h * HSZ:(h + 1) * HSZ] = _nn(p, v).astype(out_ref.dtype)
         lse_ref[:, h:h + 1] = lse
 
 
@@ -181,14 +185,23 @@
                      dq_ref, prev_ref, next_ref, own_ref, *, heads, scale):
     length = q_ref.shape[0]
     width = q_ref.shape[1]
-    for h in range(heads):
+
+    def front(h):
         cols = slice(h * HSZ, (h + 1) * HSZ)
         q = q_ref[:, cols]
         g = g_ref[:, cols]
         keys, vals = _window(k_ref, v_ref, kvp_ref, kvn_ref, h)
         s = _scores(mask_ref, q, keys, scale)
+        dp = jnp.concatenate([_nt(g, v) for v in vals], axis=1)
+        return q, g, keys, s, dp
+
+    ahead = front(0)
+    for h in range(heads):
+        cols = slice(h * HSZ, (h + 1) * HSZ)
+        q, g, keys, s, dp = ahead
+        if h + 1 < heads:
+            ahead = front(h + 1)
         p = jnp.exp(s - lse_ref[:, h:h + 1])
-        dp = jnp.concatenate([_nt(g, v) for v in vals], axis=1)
         ds = (p * (dp - delta_ref[:, h:h + 1])).astype(jnp.bfloat16)
         p_low = p.astype(jnp.bfloat16)
         dq_ref[:, cols] = (_nn(ds, jnp.concatenate(keys, axis=0)) * scale).astype(dq_ref.dtype)

time: 59.6 us -> 57.2 us (0.960)
  Pallas kernels: 11.1 us -> 8.79 us
    pallas_call x1, Pallas kernels: 5.4 us -> 4.03 us  [attend_forward(): pl.pallas_call(kern, out_shape=(jax.ShapeDtypeStruct((length, width), jnp...]
    pallas_call x1, Pallas kernels: 5.74 us -> 4.77 us  [attend_backward(): pl.pallas_call(kern, out_shape=(jax.ShapeDtypeStruct((length, width), jnp...]
where the time goes in v5:
time: 57.2 us; the launch traced here: 56.9 us
  starting transfers between devices  21.7 us (38%)
  waiting for transfers between devices  16 us (28%)
  Pallas kernels  8.79 us (15%)
  local copies, waits for them, and re-layouts  5.69 us (10%)
  other arithmetic  3.89 us (7%)
  between operations  0.89 us (2%)
    ppermute x4, starting transfers between devices, passed_along(): return lax.ppermute(x, axis, pairs)  9.28 us
    ppermute x2, waiting for transfers between devices, tp_sum(): lax.ppermute(total, 'tp', [(i, i ^ 1 << b) for i in range(peers)])  5.29 us
    ppermute x3, starting transfers between devices, heads_to_tiles(): chunk = lax.ppermute(chunk, 'tp', [(i, (i + shift) % n) for i in range(n)])  4.85 us
    ppermute x3, waiting for transfers between devices, tiles_to_heads(): chunk = lax.ppermute(chunk, 'tp', [(i, (i + shift) % n) for i in range(n)])  4.8 us
    pallas_call x1, Pallas kernels, attend_backward(): pl.pallas_call(kern, out_shape=(jax.ShapeDtypeStruct((length, width), jnp...  4.77 us
    ppermute x3, starting transfers between devices, tiles_to_heads(): chunk = lax.ppermute(chunk, 'tp', [(i, (i + shift) % n) for i in range(n)])  4.67 us
    ppermute x3, waiting for transfers between devices, heads_to_tiles(): chunk = lax.ppermute(chunk, 'tp', [(i, (i + shift) % n) for i in range(n)])  4.47 us
    pallas_call x1, Pallas kernels, attend_forward(): pl.pallas_call(kern, out_shape=(jax.ShapeDtypeStruct((length, width), jnp...  4.03 us
  transfers between devices with their start and end apart: 12, of which 10 were waited for; matrix products, arithmetic and copies ran while one was open for 5% of the time, Pallas kernels for 0%

profile of v5, /device:TPU:4, one launch (start us, length us, event | category | flops | bytes accessed | tf_op | source)
XLA Modules:
  0.0 56.9 jit_solution(1901372102521247550)
XLA Ops:
  0.7 1.0 %constant_dynamic-update-slice_fusion.1 = bf16[128,2048]{1,0:T(8,128)(2,1)S(1)} fusion(bf16[128,1024]{1,0:T(8,128)(2,1)} %k_ref.3), kind=kLoop, calls=%fused_computation.58 | loop fusion | bytes 524288
  1.7 2.9 %collective-permute-start.1 = (bf16[128,2048]{1,0:T(8,128)(2,1)S(1)}, bf16[128,2048]{1,0:T(8,128)(2,1)S(1)}, u32[]{:S(2)}, u32[]{:S(2)}) collective-permute-start(bf16[128,2048]{1,0:T(8,128)(2,1)S(1)} %constant_dynamic-update-slice_fusion), channel_id=1, source_target_pairs={{4,0},{8,4},{12,8},{16,12},{20,16},{24,20},{28,24},{5,1},{9,5},{13... | collective-permute-start | bytes 1572872 | tf_op jit(solution)/shard_map/ppermute | solution.py:24
  4.6 1.9 %collective-permute-start = (bf16[128,2048]{1,0:T(8,128)(2,1)S(1)}, bf16[128,2048]{1,0:T(8,128)(2,1)S(1)}, u32[]{:S(2)}, u32[]{:S(2)}) collective-permute-start(bf16[128,2048]{1,0:T(8,128)(2,1)S(1)} %constant_dynamic-update-slice_fusion), channel_id=1, source_target_pairs={{0,4},{4,8},{8,12},{12,16},{16,20},{20,24},{24,28},{1,5},{5,9},{9,... | collective-permute-start | bytes 1572872 | tf_op jit(solution)/shard_map/ppermute | solution.py:24
  6.7 1.6 %collective-permute-start.4 = (bf16[32,1024]{1,0:T(8,128)(2,1)S(1)}, bf16[32,1024]{1,0:T(8,128)(2,1)S(1)}, u32[]{:S(2)}, u32[]{:S(2)}) collective-permute-start(bf16[32,1024]{1,0:T(8,128)(2,1)S(1)} %get-tuple-element.28), channel_id=1, source_target_pairs={{0,1},{1,2},{2,3},{3,0},{4,5},{5,6},{6,7},{7,4},{8,9},{9,10},{10,1... | collective-permute-start | bytes 196616 | tf_op jit(solution)/shard_map/ppermute | solution.py:95
  8.3 2.2 %collective-permute-start.2 = (bf16[32,1024]{1,0:T(8,128)(2,1)S(1)}, bf16[32,1024]{1,0:T(8,128)(2,1)S(1)}, u32[]{:S(2)}, u32[]{:S(2)}) collective-permute-start(bf16[32,1024]{1,0:T(8,128)(2,1)S(1)} %get-tuple-element.29), channel_id=1, source_target_pairs={{0,3},{1,0},{2,1},{3,2},{4,7},{5,4},{6,5},{7,6},{8,11},{9,8},{10,9... | collective-permute-start | bytes 196616 | tf_op jit(solution)/shard_map/ppermute | solution.py:95
  14.2 3.4 %collective-permute-done.3 = bf16[32,1024]{1,0:T(8,128)(2,1)S(1)} collective-permute-done((bf16[32,1024]{1,0:T(8,128)(2,1)S(1)}, bf16[32,1024]{1,0:T(8,128)(2,1)S(1)}, u32[]{:S(2)}, u32[]{:S(2)}) %collective-permute-start.3) | collective-permute-done | bytes 65568 | tf_op jit(solution)/shard_map/ppermute | solution.py:95
  19.5 4.0 %shard_map.93 = (bf16[128,1024]{1,0:T(8,128)(2,1)}, f32[128,8]{1,0:T(8,128)}) custom-call(s32[3]{0:T(128)} %fusion.26.mask_ref, bf16[128,1024]{1,0:T(8,128)(2,1)} %q_ref.3, bf16[128,1024]{1,0:T(8,128)(2,1)} %k_ref.3, bf16[128,1024]{1,0:T(8,128)(2,1)} %v_ref.3, bf16[128,2048]{1,0:T(8,128)(2,1)} %copy-done.3, bf16[128,2048]{1,0:T(8,128)(2,1)} %copy-done.2), custom_call_target="tpu_custom_call" | custom-call | flops 201326592 | bytes 2097152 | tf_op jit(solution)/shard_map/pallas_call | solution.py:172
  23.5 1.2 %fusion.7 = (f32[128]{0:T(128)S(1)}, f32[128]{0:T(128)S(1)}) fusion(bf16[128,1024]{1,0:T(8,128)(2,1)} %get-tuple-element.11, f32[1024]{0:T(1024)S(1)} %dynamic_slice.38, bf16[4,32,1024]{2,1,0:T(8,128)(2,1)S(1)} %fusion.22), kind=kLoop, calls=%fused_computation.12 | loop fusion | flops 917248 | bytes 529408 | tf_op jit(solution)/shard_map/reduce_sum | solution.py:254
  24.8 0.9 %collective-permute-start.5 = (f32[128,2]{0,1:T(2,128)S(1)}, f32[128,2]{0,1:T(2,128)S(1)}, u32[]{:S(2)}, u32[]{:S(2)}) collective-permute-start(f32[128,2]{0,1:T(2,128)S(1)} %pad_maximum_fusion), channel_id=1, source_target_pairs={{0,1},{1,0},{2,3},{3,2},{4,5},{5,4},{6,7},{7,6},{8,9},{9,8},{10,11... | collective-permute-start | bytes 3080 | tf_op jit(solution)/shard_map/ppermute | solution.py:63
  25.7 2.7 %collective-permute-done.5 = f32[128,2]{0,1:T(2,128)S(1)} collective-permute-done((f32[128,2]{0,1:T(2,128)S(1)}, f32[128,2]{0,1:T(2,128)S(1)}, u32[]{:S(2)}, u32[]{:S(2)}) %collective-permute-start.5) | collective-permute-done | bytes 1056 | tf_op jit(solution)/shard_map/ppermute | solution.py:63
  28.4 1.9 %collective-permute-start.6 = (f32[128,2]{0,1:T(2,128)S(1)}, f32[128,2]{0,1:T(2,128)S(1)}, u32[]{:S(2)}, u32[]{:S(2)}) collective-permute-start(f32[128,2]{0,1:T(2,128)S(1)} %fusion.27), channel_id=1, source_target_pairs={{0,2},{1,3},{2,0},{3,1},{4,6},{5,7},{6,4},{7,5},{8,10},{9,11},{10,... | collective-permute-start | bytes 3080 | tf_op jit(solution)/shard_map/ppermute | solution.py:63
  30.4 2.6 %collective-permute-done.6 = f32[128,2]{0,1:T(2,128)S(1)} collective-permute-done((f32[128,2]{0,1:T(2,128)S(1)}, f32[128,2]{0,1:T(2,128)S(1)}, u32[]{:S(2)}, u32[]{:S(2)}) %collective-permute-start.6) | collective-permute-done | bytes 1056 | tf_op jit(solution)/shard_map/ppermute | solution.py:63
  33.0 1.0 %fusion.9 = (f32[16,8,8,128]{3,1,2,0:T(8,128)S(1)}, bf16[128,1024]{1,0:T(8,128)(2,1)}, bf16[128,1024]{1,0:T(8,128)(2,1)S(1)}) fusion(bf16[128,1024]{1,0:T(8,128)(2,1)S(1)} %copy-done.5, f32[128]{0:T(128)S(1)} %get-tuple-element.32, f32[1024]{0:T(1024)S(1)} %dynamic_slice.38, bf16[4,32,1024]{2,1,0:T(8,128)(2,1)S(1)} %fusion.22, f32[128]{0:T(128)S(1)} %get-tuple-element.33), kind=kLoop, calls=%fused_computation.14 | loop fusion | flops 1835008 | bytes 1577984
  34.1 0.8 %reduce_sum.29.delta_ref = f32[128,8]{1,0:T(8,128)} reduce(f32[128,8,128]{2,1,0:T(8,128)S(1)} %bitcast.28, f32[]{:T(128)} %constant.71.clone.1), dimensions={2}, to_apply=%region_2.4 | reduce | flops 130048 | bytes 528388 | tf_op jit(solution)/shard_map/reduce_sum | solution.py:266
  34.9 4.8 %shard_map.94 = (bf16[128,1024]{1,0:T(8,128)(2,1)}, bf16[128,2048]{1,0:T(8,128)(2,1)}, bf16[128,2048]{1,0:T(8,128)(2,1)}, f32[128,2048]{1,0:T(8,128)}) custom-call(s32[3]{0:T(128)} %fusion.26.mask_ref, bf16[128,1024]{1,0:T(8,128)(2,1)} %q_ref.3, bf16[128,1024]{1,0:T(8,128)(2,1)} %k_ref.3, bf16[128,1024]{1,0:T(8,128)(2,1)} %v_ref.3, ...), custom_call_target="tpu_custom_call" | custom-call | flops 503316480 | bytes 4718592 | tf_op jit(solution)/shard_map/pallas_call | solution.py:222
  39.7 2.0 %collective-permute-start.10 = (bf16[128,2048]{1,0:T(8,128)(2,1)}, bf16[128,2048]{1,0:T(8,128)(2,1)S(1)}, u32[]{:S(2)}, u32[]{:S(2)}) collective-permute-start(bf16[128,2048]{1,0:T(8,128)(2,1)} %get-tuple-element.15), channel_id=1, source_target_pairs={{4,0},{8,4},{12,8},{16,12},{20,16},{24,20},{28,24},{5,1},{9,5},{13... | collective-permute-start | bytes 1572872 | tf_op jit(solution)/shard_map/ppermute | solution.py:24
  41.7 2.4 %collective-permute-start.11 = (bf16[128,2048]{1,0:T(8,128)(2,1)}, bf16[128,2048]{1,0:T(8,128)(2,1)S(1)}, u32[]{:S(2)}, u32[]{:S(2)}) collective-permute-start(bf16[128,2048]{1,0:T(8,128)(2,1)} %get-tuple-element.16), channel_id=1, source_target_pairs={{0,4},{4,8},{8,12},{12,16},{16,20},{20,24},{24,28},{1,5},{5,9},{9,... | collective-permute-start | bytes 1572872 | tf_op jit(solution)/shard_map/ppermute | solution.py:24
  44.2 0.9 %collective-permute-start.9 = (bf16[32,1024]{1,0:T(8,128)(2,1)S(1)}, bf16[32,1024]{1,0:T(8,128)(2,1)S(1)}, u32[]{:S(2)}, u32[]{:S(2)}) collective-permute-start(bf16[32,1024]{1,0:T(8,128)(2,1)S(1)} %get-tuple-element.24), channel_id=1, source_target_pairs={{0,1},{1,2},{2,3},{3,0},{4,5},{5,6},{6,7},{7,4},{8,9},{9,10},{10,1... | collective-permute-start | bytes 196616 | tf_op jit(solution)/shard_map/ppermute | solution.py:114
  45.1 2.6 %collective-permute-start.8 = (bf16[32,1024]{1,0:T(8,128)(2,1)S(1)}, bf16[32,1024]{1,0:T(8,128)(2,1)S(1)}, u32[]{:S(2)}, u32[]{:S(2)}) collective-permute-start(bf16[32,1024]{1,0:T(8,128)(2,1)S(1)} %get-tuple-element.25), channel_id=1, source_target_pairs={{0,2},{1,3},{2,0},{3,1},{4,6},{5,7},{6,4},{7,5},{8,10},{9,11},{10,... | collective-permute-start | bytes 196616 | tf_op jit(solution)/shard_map/ppermute | solution.py:114
  47.7 1.3 %collective-permute-start.7 = (bf16[32,1024]{1,0:T(8,128)(2,1)S(1)}, bf16[32,1024]{1,0:T(8,128)(2,1)S(1)}, u32[]{:S(2)}, u32[]{:S(2)}) collective-permute-start(bf16[32,1024]{1,0:T(8,128)(2,1)S(1)} %get-tuple-element.26), channel_id=1, source_target_pairs={{0,3},{1,0},{2,1},{3,2},{4,7},{5,4},{6,5},{7,6},{8,11},{9,8},{10,9... | collective-permute-start | bytes 196616 | tf_op jit(solution)/shard_map/ppermute | solution.py:114
  49.1 1.6 %collective-permute-done.9 = bf16[32,1024]{1,0:T(8,128)(2,1)S(1)} collective-permute-done((bf16[32,1024]{1,0:T(8,128)(2,1)S(1)}, bf16[32,1024]{1,0:T(8,128)(2,1)S(1)}, u32[]{:S(2)}, u32[]{:S(2)}) %collective-permute-start.9) | collective-permute-done | bytes 65568 | tf_op jit(solution)/shard_map/ppermute | solution.py:114
  50.7 2.7 %collective-permute-done.8 = bf16[32,1024]{1,0:T(8,128)(2,1)S(1)} collective-permute-done((bf16[32,1024]{1,0:T(8,128)(2,1)S(1)}, bf16[32,1024]{1,0:T(8,128)(2,1)S(1)}, u32[]{:S(2)}, u32[]{:S(2)}) %collective-permute-start.8) | collective-permute-done | bytes 65568 | tf_op jit(solution)/shard_map/ppermute | solution.py:114
  54.6 1.3 %collective-permute-done.11 = bf16[128,2048]{1,0:T(8,128)(2,1)S(1)} collective-permute-done((bf16[128,2048]{1,0:T(8,128)(2,1)}, bf16[128,2048]{1,0:T(8,128)(2,1)S(1)}, u32[]{:S(2)}, u32[]{:S(2)}) %collective-permute-start.11) | collective-permute-done | bytes 524320 | tf_op jit(solution)/shard_map/ppermute | solution.py:24
  56.1 0.8 %fusion.29 = (bf16[128,1024]{1,0:T(8,128)(2,1)}, bf16[128,1024]{1,0:T(8,128)(2,1)}) fusion(bf16[128,2048]{1,0:T(8,128)(2,1)S(1)} %add_convert_fusion), kind=kLoop, calls=%fused_computation.64 | loop fusion | bytes 1048576 | tf_op jit(solution)/shard_map/slice | solution.py:272
  (35 shorter events, 7.2 us)
Async XLA Ops:
  0.6 10.7 %copy-start = (s32[8,3]{0,1:T(4,128)S(1)}, s32[8,3]{0,1:T(4,128)}, u32[]{:S(2)}) copy-start(s32[8,3]{0,1:T(4,128)} %param.11) | copy-start | bytes 292
  0.6 1.0 %copy-start.1 = (bf16[128,1024]{1,0:T(8,128)(2,1)S(1)}, bf16[128,1024]{1,0:T(8,128)(2,1)}, u32[]{:S(2)}) copy-start(bf16[128,1024]{1,0:T(8,128)(2,1)} %v_ref.3) | copy-start | bytes 786436
  1.7 5.0 %copy-start.6 = (bf16[32,4096]{1,0:T(8,128)(2,1)S(1)}, bf16[32,4096]{1,0:T(8,128)(2,1)}, u32[]{:S(2)}) copy-start(bf16[32,4096]{1,0:T(8,128)(2,1)} %param.13) | copy-start | bytes 786436
  1.7 16.1 %collective-permute-start.1 = (bf16[128,2048]{1,0:T(8,128)(2,1)S(1)}, bf16[128,2048]{1,0:T(8,128)(2,1)S(1)}, u32[]{:S(2)}, u32[]{:S(2)}) collective-permute-start(bf16[128,2048]{1,0:T(8,128)(2,1)S(1)} %constant_dynamic-update-slice_fusion), channel_id=1, source_target_pairs={{4,0},{8,4},{12,8},{16,12},{20,16},{24,20},{28,24},{5,1},{9,5},{13... | collective-permute-start | bytes 1572872 | tf_op jit(solution)/shard_map/ppermute | solution.py:24
  4.6 13.3 %collective-permute-start = (bf16[128,2048]{1,0:T(8,128)(2,1)S(1)}, bf16[128,2048]{1,0:T(8,128)(2,1)S(1)}, u32[]{:S(2)}, u32[]{:S(2)}) collective-permute-start(bf16[128,2048]{1,0:T(8,128)(2,1)S(1)} %constant_dynamic-update-slice_fusion), channel_id=1, source_target_pairs={{0,4},{4,8},{8,12},{12,16},{16,20},{20,24},{24,28},{1,5},{5,9},{9,... | collective-permute-start | bytes 1572872 | tf_op jit(solution)/shard_map/ppermute | solution.py:24
  6.7 6.8 %collective-permute-start.4 = (bf16[32,1024]{1,0:T(8,128)(2,1)S(1)}, bf16[32,1024]{1,0:T(8,128)(2,1)S(1)}, u32[]{:S(2)}, u32[]{:S(2)}) collective-permute-start(bf16[32,1024]{1,0:T(8,128)(2,1)S(1)} %get-tuple-element.28), channel_id=1, source_target_pairs={{0,1},{1,2},{2,3},{3,0},{4,5},{5,6},{6,7},{7,4},{8,9},{9,10},{10,1... | collective-permute-start | bytes 196616 | tf_op jit(solution)/shard_map/ppermute | solution.py:95
  8.3 5.9 %collective-permute-start.2 = (bf16[32,1024]{1,0:T(8,128)(2,1)S(1)}, bf16[32,1024]{1,0:T(8,128)(2,1)S(1)}, u32[]{:S(2)}, u32[]{:S(2)}) collective-permute-start(bf16[32,1024]{1,0:T(8,128)(2,1)S(1)} %get-tuple-element.29), channel_id=1, source_target_pairs={{0,3},{1,0},{2,1},{3,2},{4,7},{5,4},{6,5},{7,6},{8,11},{9,8},{10,9... | collective-permute-start | bytes 196616 | tf_op jit(solution)/shard_map/ppermute | solution.py:95
  10.6 7.0 %collective-permute-start.3 = (bf16[32,1024]{1,0:T(8,128)(2,1)S(1)}, bf16[32,1024]{1,0:T(8,128)(2,1)S(1)}, u32[]{:S(2)}, u32[]{:S(2)}) collective-permute-start(bf16[32,1024]{1,0:T(8,128)(2,1)S(1)} %get-tuple-element.31), channel_id=1, source_target_pairs={{0,2},{1,3},{2,0},{3,1},{4,6},{5,7},{6,4},{7,5},{8,10},{9,11},{10,... | collective-permute-start | bytes 196616 | tf_op jit(solution)/shard_map/ppermute | solution.py:95
  17.9 0.8 %copy-start.2 = (bf16[128,2048]{1,0:T(8,128)(2,1)}, bf16[128,2048]{1,0:T(8,128)(2,1)S(1)}, u32[]{:S(2)}) copy-start(bf16[128,2048]{1,0:T(8,128)(2,1)S(1)} %collective-permute-done.1.next_ref.kvn_ref) | copy-start | bytes 1572868
  18.7 0.8 %copy-start.3 = (bf16[128,2048]{1,0:T(8,128)(2,1)}, bf16[128,2048]{1,0:T(8,128)(2,1)S(1)}, u32[]{:S(2)}) copy-start(bf16[128,2048]{1,0:T(8,128)(2,1)S(1)} %collective-permute-done.prev_ref.kvp_ref) | copy-start | bytes 1572868
  23.5 9.4 %copy-start.5 = (bf16[128,1024]{1,0:T(8,128)(2,1)S(1)}, bf16[128,1024]{1,0:T(8,128)(2,1)}, u32[]{:S(2)}) copy-start(bf16[128,1024]{1,0:T(8,128)(2,1)} %get-tuple-element.11) | copy-start | bytes 786436
  24.8 3.6 %collective-permute-start.5 = (f32[128,2]{0,1:T(2,128)S(1)}, f32[128,2]{0,1:T(2,128)S(1)}, u32[]{:S(2)}, u32[]{:S(2)}) collective-permute-start(f32[128,2]{0,1:T(2,128)S(1)} %pad_maximum_fusion), channel_id=1, source_target_pairs={{0,1},{1,0},{2,3},{3,2},{4,5},{5,4},{6,7},{7,6},{8,9},{9,8},{10,11... | collective-permute-start | bytes 3080 | tf_op jit(solution)/shard_map/ppermute | solution.py:63
  28.4 4.5 %collective-permute-start.6 = (f32[128,2]{0,1:T(2,128)S(1)}, f32[128,2]{0,1:T(2,128)S(1)}, u32[]{:S(2)}, u32[]{:S(2)}) collective-permute-start(f32[128,2]{0,1:T(2,128)S(1)} %fusion.27), channel_id=1, source_target_pairs={{0,2},{1,3},{2,0},{3,1},{4,6},{5,7},{6,4},{7,5},{8,10},{9,11},{10,... | collective-permute-start | bytes 3080 | tf_op jit(solution)/shard_map/ppermute | solution.py:63
  39.7 16.2 %copy-start.4 = (f32[128,2048]{1,0:T(8,128)S(1)}, f32[128,2048]{1,0:T(8,128)}, u32[]{:S(2)}) copy-start(f32[128,2048]{1,0:T(8,128)} %get-tuple-element.14) | copy-start | bytes 3145732
  39.7 14.9 %collective-permute-start.10 = (bf16[128,2048]{1,0:T(8,128)(2,1)}, bf16[128,2048]{1,0:T(8,128)(2,1)S(1)}, u32[]{:S(2)}, u32[]{:S(2)}) collective-permute-start(bf16[128,2048]{1,0:T(8,128)(2,1)} %get-tuple-element.15), channel_id=1, source_target_pairs={{4,0},{8,4},{12,8},{16,12},{20,16},{24,20},{28,24},{5,1},{9,5},{13... | collective-permute-start | bytes 1572872 | tf_op jit(solution)/shard_map/ppermute | solution.py:24
  41.7 14.2 %collective-permute-start.11 = (bf16[128,2048]{1,0:T(8,128)(2,1)}, bf16[128,2048]{1,0:T(8,128)(2,1)S(1)}, u32[]{:S(2)}, u32[]{:S(2)}) collective-permute-start(bf16[128,2048]{1,0:T(8,128)(2,1)} %get-tuple-element.16), channel_id=1, source_target_pairs={{0,4},{4,8},{8,12},{12,16},{16,20},{20,24},{24,28},{1,5},{5,9},{9,... | collective-permute-start | bytes 1572872 | tf_op jit(solution)/shard_map/ppermute | solution.py:24
  44.2 6.5 %collective-permute-start.9 = (bf16[32,1024]{1,0:T(8,128)(2,1)S(1)}, bf16[32,1024]{1,0:T(8,128)(2,1)S(1)}, u32[]{:S(2)}, u32[]{:S(2)}) collective-permute-start(bf16[32,1024]{1,0:T(8,128)(2,1)S(1)} %get-tuple-element.24), channel_id=1, source_target_pairs={{0,1},{1,2},{2,3},{3,0},{4,5},{5,6},{6,7},{7,4},{8,9},{9,10},{10,1... | collective-permute-start | bytes 196616 | tf_op jit(solution)/shard_map/ppermute | solution.py:114
  45.1 8.3 %collective-permute-start.8 = (bf16[32,1024]{1,0:T(8,128)(2,1)S(1)}, bf16[32,1024]{1,0:T(8,128)(2,1)S(1)}, u32[]{:S(2)}, u32[]{:S(2)}) collective-permute-start(bf16[32,1024]{1,0:T(8,128)(2,1)S(1)} %get-tuple-element.25), channel_id=1, source_target_pairs={{0,2},{1,3},{2,0},{3,1},{4,6},{5,7},{6,4},{7,5},{8,10},{9,11},{10,... | collective-permute-start | bytes 196616 | tf_op jit(solution)/shard_map/ppermute | solution.py:114
  47.7 5.8 %collective-permute-start.7 = (bf16[32,1024]{1,0:T(8,128)(2,1)S(1)}, bf16[32,1024]{1,0:T(8,128)(2,1)S(1)}, u32[]{:S(2)}, u32[]{:S(2)}) collective-permute-start(bf16[32,1024]{1,0:T(8,128)(2,1)S(1)} %get-tuple-element.26), channel_id=1, source_target_pairs={{0,3},{1,0},{2,1},{3,2},{4,7},{5,4},{6,5},{7,6},{8,11},{9,8},{10,9... | collective-permute-start | bytes 196616 | tf_op jit(solution)/shard_map/ppermute | solution.py:114

commit v6 on v5

--- a/solution.py
+++ b/solution.py
@@ -13,6 +13,7 @@
 
 NEGATIVE = -1e30
 EPSILON = 1e-06
+LOOKAHEAD = 3
 STATS_SUM = "xor"
 NG_MODE = "perm"
 OUT_MODE = "perm"
@@ -151,11 +152,11 @@
         keys, values = _window(k_ref, v_ref, prev_ref, next_ref, h)
         return _scores(mask_ref, q_ref[:, h * HSZ:(h + 1) * HSZ], keys, scale), values
 
-    ahead = scores(0)
+    ahead = [scores(h) for h in range(min(LOOKAHEAD, heads))]
     for h in range(heads):
-        s, values = ahead
-        if h + 1 < heads:
-            ahead = scores(h + 1)
+        s, values = ahead.pop(0)
+        if h + LOOKAHEAD < heads:
+            ahead.append(scores(h + LOOKAHEAD))
         peak = jnp.max(s, -1, keepdims=True)
         lse = peak + jnp.log(jnp.sum(jnp.exp(s - peak), -1, keepdims=True))
         p = jnp.exp(s - lse).astype(jnp.bfloat16)
@@ -185,32 +186,36 @@
                      dq_ref, prev_ref, next_ref, own_ref, *, heads, scale):
     length = q_ref.shape[0]
     width = q_ref.shape[1]
+    row = lax.broadcasted_iota(jnp.int32, (3 * length, 1), 0)
+    live = jnp.zeros((3 * length, 1), jnp.bool_)
+    for c in range(3):
+        live = live | ((row >= c * length) & (row < (c + 1) * length) & (mask_ref[c] > 0))
 
     def front(h):
         cols = slice(h * HSZ, (h + 1) * HSZ)
         q = q_ref[:, cols]
         g = g_ref[:, cols]
         keys, vals = _window(k_ref, v_ref, kvp_ref, kvn_ref, h)
-        s = _scores(mask_ref, q, keys, scale)
-        dp = jnp.concatenate([_nt(g, v) for v in vals], axis=1)
-        return q, g, keys, s, dp
-
-    ahead = front(0)
+        keys = jnp.concatenate(keys, axis=0)
+        s_t = jnp.where(live, _nt(keys, q) * scale, NEGATIVE)
+        dp_t = _nt(jnp.concatenate(vals, axis=0), g)
+        return q, g, keys, s_t, dp_t
+
+    ahead = [front(h) for h in range(min(LOOKAHEAD, heads))]
     for h in range(heads):
         cols = slice(h * HSZ, (h + 1) * HSZ)
-        q, g, keys, s, dp = ahead
-        if h + 1 < heads:
-            ahead = front(h + 1)
-        p = jnp.exp(s - lse_ref[:, h:h + 1])
-        ds = (p * (dp - delta_ref[:, h:h + 1])).astype(jnp.bfloat16)
-        p_low = p.astype(jnp.bfloat16)
-        dq_ref[:, cols] = (_nn(ds, jnp.concatenate(keys, axis=0)) * scale).astype(dq_ref.dtype)
+        q, g, keys, s_t, dp_t = ahead.pop(0)
+        if h + LOOKAHEAD < heads:
+            ahead.append(front(h + LOOKAHEAD))
+        p_t = jnp.exp(s_t - lse_ref[h:h + 1, :])
+        ds_t = (p_t * (dp_t - delta_ref[h:h + 1, :])).astype(jnp.bfloat16)
+        dq_ref[:, cols] = (_tn(ds_t, keys) * scale).astype(dq_ref.dtype)
+        dk = _nn(ds_t, q) * scale
+        dv = _nn(p_t.astype(jnp.bfloat16), g)
         for c, ref in enumerate((prev_ref, own_ref, next_ref)):
             blk = slice(c * length, (c + 1) * length)
-            dk = _tn(ds[:, blk], q) * scale
-            dv = _tn(p_low[:, blk], g)
-            ref[:, cols] = dk.astype(ref.dtype)
-            ref[:, width + h * HSZ:width + (h + 1) * HSZ] = dv.astype(ref.dtype)
+            ref[:, cols] = dk[blk].astype(ref.dtype)
+            ref[:, width + h * HSZ:width + (h + 1) * HSZ] = dv[blk].astype(ref.dtype)
 
 
 def attend_backward(mask_row, q, k, v, kv_prev, kv_next, grad, lse, delta):
@@ -228,7 +233,7 @@
         cost_estimate=pl.CostEstimate(
             flops=30 * length * length * width, transcendentals=3 * length * length * heads,
             bytes_accessed=36 * length * width),
-    )(mask_row, q, k, v, kv_prev, kv_next, grad, lse, delta)
+    )(mask_row, q, k, v, kv_prev, kv_next, grad, lse.T, delta.T)
 
 
 def per_device(queries, key_rows, value_rows, view_mask, norm_gain, normed_grad):

time: 57.2 us -> 56.3 us (0.984)
  local copies, waits for them, and re-layouts: 5.69 us -> 7.1 us
  Pallas kernels: 8.79 us -> 7.8 us
  waiting for transfers between devices: 16 us -> 15.3 us
  other arithmetic: 3.89 us -> 3.25 us
    reduce_sum x0 -> x1, local copies, waits for them, and re-layouts: none -> 0.66 us  [per_device(): jnp.sum(grad_heads.astype(jnp.float32) * out_heads.astype(jnp.float32), -1)]
    pallas_call x0 -> x1, local copies, waits for them, and re-layouts: none -> 0.66 us  [attend_forward(): pl.pallas_call(kern, out_shape=(jax.ShapeDtypeStruct((length, width), jnp...]
    ppermute x2, waiting for transfers between devices: 5.29 us -> 4.65 us  [tp_sum(): lax.ppermute(total, 'tp', [(i, i ^ 1 << b) for i in range(peers)])]
    reduce_sum x1, other arithmetic: 0.84 us -> 0.2 us  [per_device(): jnp.sum(grad_heads.astype(jnp.float32) * out_heads.astype(jnp.float32), -1)]
    unnamed x16 -> x18, local copies, waits for them, and re-layouts: 2.69 us -> 2.7 us
  transfers between devices with their start and end apart: 12 -> 12, of which waited for: 10 -> 10; matrix products, arithmetic and copies ran while one was open for 5% -> 6% of each run, Pallas kernels for 0% -> 0%
where the time goes in v6:
time: 56.3 us; the launch traced here: 56 us
  starting transfers between devices  21.6 us (38%)
  waiting for transfers between devices  15.3 us (27%)
  Pallas kernels  7.8 us (14%)
  local copies, waits for them, and re-layouts  7.1 us (13%)
  other arithmetic  3.25 us (6%)
  between operations  0.9 us (2%)
    ppermute x4, starting transfers between devices, passed_along(): return lax.ppermute(x, axis, pairs)  9.28 us
    ppermute x3, starting transfers between devices, heads_to_tiles(): chunk = lax.ppermute(chunk, 'tp', [(i, (i + shift) % n) for i in range(n)])  4.84 us
    ppermute x3, waiting for transfers between devices, tiles_to_heads(): chunk = lax.ppermute(chunk, 'tp', [(i, (i + shift) % n) for i in range(n)])  4.73 us
    ppermute x3, starting transfers between devices, tiles_to_heads(): chunk = lax.ppermute(chunk, 'tp', [(i, (i + shift) % n) for i in range(n)])  4.67 us
    ppermute x2, waiting for transfers between devices, tp_sum(): lax.ppermute(total, 'tp', [(i, i ^ 1 << b) for i in range(peers)])  4.65 us
    ppermute x3, waiting for transfers between devices, heads_to_tiles(): chunk = lax.ppermute(chunk, 'tp', [(i, (i + shift) % n) for i in range(n)])  4.46 us
    pallas_call x1, Pallas kernels, attend_backward(): pl.pallas_call(kern, out_shape=(jax.ShapeDtypeStruct((length, width), jnp...  4.25 us
    pallas_call x1, Pallas kernels, attend_forward(): pl.pallas_call(kern, out_shape=(jax.ShapeDtypeStruct((length, width), jnp...  3.55 us
  transfers between devices with their start and end apart: 12, of which 10 were waited for; matrix products, arithmetic and copies ran while one was open for 6% of the time, Pallas kernels for 0%

profile of v6, /device:TPU:4, one launch (start us, length us, event | category | flops | bytes accessed | tf_op | source)
XLA Modules:
  0.0 56.0 jit_solution(8977435167005644738)
XLA Ops:
  0.7 1.0 %constant_dynamic-update-slice_fusion.1 = bf16[128,2048]{1,0:T(8,128)(2,1)S(1)} fusion(bf16[128,1024]{1,0:T(8,128)(2,1)} %k_ref.3), kind=kLoop, calls=%fused_computation.58 | loop fusion | bytes 524288
  1.7 2.9 %collective-permute-start.1 = (bf16[128,2048]{1,0:T(8,128)(2,1)S(1)}, bf16[128,2048]{1,0:T(8,128)(2,1)S(1)}, u32[]{:S(2)}, u32[]{:S(2)}) collective-permute-start(bf16[128,2048]{1,0:T(8,128)(2,1)S(1)} %constant_dynamic-update-slice_fusion), channel_id=1, source_target_pairs={{4,0},{8,4},{12,8},{16,12},{20,16},{24,20},{28,24},{5,1},{9,5},{13... | collective-permute-start | bytes 1572872 | tf_op jit(solution)/shard_map/ppermute | solution.py:25
  4.6 1.9 %collective-permute-start = (bf16[128,2048]{1,0:T(8,128)(2,1)S(1)}, bf16[128,2048]{1,0:T(8,128)(2,1)S(1)}, u32[]{:S(2)}, u32[]{:S(2)}) collective-permute-start(bf16[128,2048]{1,0:T(8,128)(2,1)S(1)} %constant_dynamic-update-slice_fusion), channel_id=1, source_target_pairs={{0,4},{4,8},{8,12},{12,16},{16,20},{20,24},{24,28},{1,5},{5,9},{9,... | collective-permute-start | bytes 1572872 | tf_op jit(solution)/shard_map/ppermute | solution.py:25
  6.7 1.6 %collective-permute-start.4 = (bf16[32,1024]{1,0:T(8,128)(2,1)S(1)}, bf16[32,1024]{1,0:T(8,128)(2,1)S(1)}, u32[]{:S(2)}, u32[]{:S(2)}) collective-permute-start(bf16[32,1024]{1,0:T(8,128)(2,1)S(1)} %get-tuple-element.28), channel_id=1, source_target_pairs={{0,1},{1,2},{2,3},{3,0},{4,5},{5,6},{6,7},{7,4},{8,9},{9,10},{10,1... | collective-permute-start | bytes 196616 | tf_op jit(solution)/shard_map/ppermute | solution.py:96
  8.3 2.2 %collective-permute-start.2 = (bf16[32,1024]{1,0:T(8,128)(2,1)S(1)}, bf16[32,1024]{1,0:T(8,128)(2,1)S(1)}, u32[]{:S(2)}, u32[]{:S(2)}) collective-permute-start(bf16[32,1024]{1,0:T(8,128)(2,1)S(1)} %get-tuple-element.29), channel_id=1, source_target_pairs={{0,3},{1,0},{2,1},{3,2},{4,7},{5,4},{6,5},{7,6},{8,11},{9,8},{10,9... | collective-permute-start | bytes 196616 | tf_op jit(solution)/shard_map/ppermute | solution.py:96
  14.2 3.4 %collective-permute-done.3 = bf16[32,1024]{1,0:T(8,128)(2,1)S(1)} collective-permute-done((bf16[32,1024]{1,0:T(8,128)(2,1)S(1)}, bf16[32,1024]{1,0:T(8,128)(2,1)S(1)}, u32[]{:S(2)}, u32[]{:S(2)}) %collective-permute-start.3) | collective-permute-done | bytes 65568 | tf_op jit(solution)/shard_map/ppermute | solution.py:96
  18.7 0.8 %copy-done.3 = bf16[128,2048]{1,0:T(8,128)(2,1)} copy-done((bf16[128,2048]{1,0:T(8,128)(2,1)}, bf16[128,2048]{1,0:T(8,128)(2,1)S(1)}, u32[]{:S(2)}) %copy-start.3) | copy-done | bytes 524312
  19.5 3.5 %shard_map.93 = (bf16[128,1024]{1,0:T(8,128)(2,1)}, f32[128,8]{1,0:T(8,128)}) custom-call(s32[3]{0:T(128)} %fusion.26.mask_ref, bf16[128,1024]{1,0:T(8,128)(2,1)} %q_ref.3, bf16[128,1024]{1,0:T(8,128)(2,1)} %k_ref.3, bf16[128,1024]{1,0:T(8,128)(2,1)} %v_ref.3, bf16[128,2048]{1,0:T(8,128)(2,1)} %copy-done.3, bf16[128,2048]{1,0:T(8,128)(2,1)} %copy-done.2), custom_call_target="tpu_custom_call" | custom-call | flops 201326592 | bytes 2097152 | tf_op jit(solution)/shard_map/pallas_call | solution.py:173
  23.1 1.2 %fusion.7 = (f32[128]{0:T(128)S(1)}, f32[128]{0:T(128)S(1)}) fusion(bf16[128,1024]{1,0:T(8,128)(2,1)} %get-tuple-element.11, f32[1024]{0:T(1024)S(1)} %dynamic_slice.38, bf16[4,32,1024]{2,1,0:T(8,128)(2,1)S(1)} %fusion.22), kind=kLoop, calls=%fused_computation.12 | loop fusion | flops 917248 | bytes 529408 | tf_op jit(solution)/shard_map/reduce_sum | solution.py:259
  24.3 0.9 %collective-permute-start.5 = (f32[128,2]{0,1:T(2,128)S(1)}, f32[128,2]{0,1:T(2,128)S(1)}, u32[]{:S(2)}, u32[]{:S(2)}) collective-permute-start(f32[128,2]{0,1:T(2,128)S(1)} %pad_maximum_fusion), channel_id=1, source_target_pairs={{0,1},{1,0},{2,3},{3,2},{4,5},{5,4},{6,7},{7,6},{8,9},{9,8},{10,11... | collective-permute-start | bytes 3080 | tf_op jit(solution)/shard_map/ppermute | solution.py:64
  25.2 2.7 %collective-permute-done.5 = f32[128,2]{0,1:T(2,128)S(1)} collective-permute-done((f32[128,2]{0,1:T(2,128)S(1)}, f32[128,2]{0,1:T(2,128)S(1)}, u32[]{:S(2)}, u32[]{:S(2)}) %collective-permute-start.5) | collective-permute-done | bytes 1056 | tf_op jit(solution)/shard_map/ppermute | solution.py:64
  27.9 1.9 %collective-permute-start.6 = (f32[128,2]{0,1:T(2,128)S(1)}, f32[128,2]{0,1:T(2,128)S(1)}, u32[]{:S(2)}, u32[]{:S(2)}) collective-permute-start(f32[128,2]{0,1:T(2,128)S(1)} %fusion.27), channel_id=1, source_target_pairs={{0,2},{1,3},{2,0},{3,1},{4,6},{5,7},{6,4},{7,5},{8,10},{9,11},{10,... | collective-permute-start | bytes 3080 | tf_op jit(solution)/shard_map/ppermute | solution.py:64
  30.5 1.9 %collective-permute-done.6 = f32[128,2]{0,1:T(2,128)S(1)} collective-permute-done((f32[128,2]{0,1:T(2,128)S(1)}, f32[128,2]{0,1:T(2,128)S(1)}, u32[]{:S(2)}, u32[]{:S(2)}) %collective-permute-start.6) | collective-permute-done | bytes 1056 | tf_op jit(solution)/shard_map/ppermute | solution.py:64
  32.5 1.0 %fusion.9 = (f32[16,8,8,128]{3,1,2,0:T(8,128)S(1)}, bf16[128,1024]{1,0:T(8,128)(2,1)}, bf16[128,1024]{1,0:T(8,128)(2,1)S(1)}) fusion(bf16[128,1024]{1,0:T(8,128)(2,1)S(1)} %copy-done.5, f32[128]{0:T(128)S(1)} %get-tuple-element.32, f32[1024]{0:T(1024)S(1)} %dynamic_slice.38, bf16[4,32,1024]{2,1,0:T(8,128)(2,1)S(1)} %fusion.22, f32[128]{0:T(128)S(1)} %get-tuple-element.33), kind=kLoop, calls=%fused_computation.14 | loop fusion | flops 1835008 | bytes 1577984
  34.5 4.3 %shard_map.94 = (bf16[128,1024]{1,0:T(8,128)(2,1)}, bf16[128,2048]{1,0:T(8,128)(2,1)}, bf16[128,2048]{1,0:T(8,128)(2,1)}, f32[128,2048]{1,0:T(8,128)}) custom-call(s32[3]{0:T(128)} %fusion.26.mask_ref, bf16[128,1024]{1,0:T(8,128)(2,1)} %q_ref.3, bf16[128,1024]{1,0:T(8,128)(2,1)} %k_ref.3, bf16[128,1024]{1,0:T(8,128)(2,1)} %v_ref.3, ...), custom_call_target="tpu_custom_call" | custom-call | flops 503316480 | bytes 4718592 | tf_op jit(solution)/shard_map/pallas_call | solution.py:227
  38.7 2.0 %collective-permute-start.10 = (bf16[128,2048]{1,0:T(8,128)(2,1)}, bf16[128,2048]{1,0:T(8,128)(2,1)S(1)}, u32[]{:S(2)}, u32[]{:S(2)}) collective-permute-start(bf16[128,2048]{1,0:T(8,128)(2,1)} %get-tuple-element.15), channel_id=1, source_target_pairs={{4,0},{8,4},{12,8},{16,12},{20,16},{24,20},{28,24},{5,1},{9,5},{13... | collective-permute-start | bytes 1572872 | tf_op jit(solution)/shard_map/ppermute | solution.py:25
  40.8 2.4 %collective-permute-start.11 = (bf16[128,2048]{1,0:T(8,128)(2,1)}, bf16[128,2048]{1,0:T(8,128)(2,1)S(1)}, u32[]{:S(2)}, u32[]{:S(2)}) collective-permute-start(bf16[128,2048]{1,0:T(8,128)(2,1)} %get-tuple-element.16), channel_id=1, source_target_pairs={{0,4},{4,8},{8,12},{12,16},{16,20},{20,24},{24,28},{1,5},{5,9},{9,... | collective-permute-start | bytes 1572872 | tf_op jit(solution)/shard_map/ppermute | solution.py:25
  43.3 0.9 %collective-permute-start.9 = (bf16[32,1024]{1,0:T(8,128)(2,1)S(1)}, bf16[32,1024]{1,0:T(8,128)(2,1)S(1)}, u32[]{:S(2)}, u32[]{:S(2)}) collective-permute-start(bf16[32,1024]{1,0:T(8,128)(2,1)S(1)} %get-tuple-element.24), channel_id=1, source_target_pairs={{0,1},{1,2},{2,3},{3,0},{4,5},{5,6},{6,7},{7,4},{8,9},{9,10},{10,1... | collective-permute-start | bytes 196616 | tf_op jit(solution)/shard_map/ppermute | solution.py:115
  44.2 2.6 %collective-permute-start.8 = (bf16[32,1024]{1,0:T(8,128)(2,1)S(1)}, bf16[32,1024]{1,0:T(8,128)(2,1)S(1)}, u32[]{:S(2)}, u32[]{:S(2)}) collective-permute-start(bf16[32,1024]{1,0:T(8,128)(2,1)S(1)} %get-tuple-element.25), channel_id=1, source_target_pairs={{0,2},{1,3},{2,0},{3,1},{4,6},{5,7},{6,4},{7,5},{8,10},{9,11},{10,... | collective-permute-start | bytes 196616 | tf_op jit(solution)/shard_map/ppermute | solution.py:115
  46.8 1.3 %collective-permute-start.7 = (bf16[32,1024]{1,0:T(8,128)(2,1)S(1)}, bf16[32,1024]{1,0:T(8,128)(2,1)S(1)}, u32[]{:S(2)}, u32[]{:S(2)}) collective-permute-start(bf16[32,1024]{1,0:T(8,128)(2,1)S(1)} %get-tuple-element.26), channel_id=1, source_target_pairs={{0,3},{1,0},{2,1},{3,2},{4,7},{5,4},{6,5},{7,6},{8,11},{9,8},{10,9... | collective-permute-start | bytes 196616 | tf_op jit(solution)/shard_map/ppermute | solution.py:115
  48.1 1.6 %collective-permute-done.9 = bf16[32,1024]{1,0:T(8,128)(2,1)S(1)} collective-permute-done((bf16[32,1024]{1,0:T(8,128)(2,1)S(1)}, bf16[32,1024]{1,0:T(8,128)(2,1)S(1)}, u32[]{:S(2)}, u32[]{:S(2)}) %collective-permute-start.9) | collective-permute-done | bytes 65568 | tf_op jit(solution)/shard_map/ppermute | solution.py:115
  49.7 2.7 %collective-permute-done.8 = bf16[32,1024]{1,0:T(8,128)(2,1)S(1)} collective-permute-done((bf16[32,1024]{1,0:T(8,128)(2,1)S(1)}, bf16[32,1024]{1,0:T(8,128)(2,1)S(1)}, u32[]{:S(2)}, u32[]{:S(2)}) %collective-permute-start.8) | collective-permute-done | bytes 65568 | tf_op jit(solution)/shard_map/ppermute | solution.py:115
  53.6 1.3 %collective-permute-done.11 = bf16[128,2048]{1,0:T(8,128)(2,1)S(1)} collective-permute-done((bf16[128,2048]{1,0:T(8,128)(2,1)}, bf16[128,2048]{1,0:T(8,128)(2,1)S(1)}, u32[]{:S(2)}, u32[]{:S(2)}) %collective-permute-start.11) | collective-permute-done | bytes 524320 | tf_op jit(solution)/shard_map/ppermute | solution.py:25
  55.1 0.8 %fusion.29 = (bf16[128,1024]{1,0:T(8,128)(2,1)}, bf16[128,1024]{1,0:T(8,128)(2,1)}) fusion(bf16[128,2048]{1,0:T(8,128)(2,1)S(1)} %add_convert_fusion), kind=kLoop, calls=%fused_computation.64 | loop fusion | bytes 1048576 | tf_op jit(solution)/shard_map/slice | solution.py:277
  (39 shorter events, 7.9 us)
Async XLA Ops:
  0.6 10.7 %copy-start = (s32[8,3]{0,1:T(4,128)S(1)}, s32[8,3]{0,1:T(4,128)}, u32[]{:S(2)}) copy-start(s32[8,3]{0,1:T(4,128)} %param.11) | copy-start | bytes 292
  0.6 1.0 %copy-start.1 = (bf16[128,1024]{1,0:T(8,128)(2,1)S(1)}, bf16[128,1024]{1,0:T(8,128)(2,1)}, u32[]{:S(2)}) copy-start(bf16[128,1024]{1,0:T(8,128)(2,1)} %v_ref.3) | copy-start | bytes 786436
  1.7 5.0 %copy-start.6 = (bf16[32,4096]{1,0:T(8,128)(2,1)S(1)}, bf16[32,4096]{1,0:T(8,128)(2,1)}, u32[]{:S(2)}) copy-start(bf16[32,4096]{1,0:T(8,128)(2,1)} %param.13) | copy-start | bytes 786436
  1.7 16.1 %collective-permute-start.1 = (bf16[128,2048]{1,0:T(8,128)(2,1)S(1)}, bf16[128,2048]{1,0:T(8,128)(2,1)S(1)}, u32[]{:S(2)}, u32[]{:S(2)}) collective-permute-start(bf16[128,2048]{1,0:T(8,128)(2,1)S(1)} %constant_dynamic-update-slice_fusion), channel_id=1, source_target_pairs={{4,0},{8,4},{12,8},{16,12},{20,16},{24,20},{28,24},{5,1},{9,5},{13... | collective-permute-start | bytes 1572872 | tf_op jit(solution)/shard_map/ppermute | solution.py:25
  4.6 13.3 %collective-permute-start = (bf16[128,2048]{1,0:T(8,128)(2,1)S(1)}, bf16[128,2048]{1,0:T(8,128)(2,1)S(1)}, u32[]{:S(2)}, u32[]{:S(2)}) collective-permute-start(bf16[128,2048]{1,0:T(8,128)(2,1)S(1)} %constant_dynamic-update-slice_fusion), channel_id=1, source_target_pairs={{0,4},{4,8},{8,12},{12,16},{16,20},{20,24},{24,28},{1,5},{5,9},{9,... | collective-permute-start | bytes 1572872 | tf_op jit(solution)/shard_map/ppermute | solution.py:25
  6.7 6.8 %collective-permute-start.4 = (bf16[32,1024]{1,0:T(8,128)(2,1)S(1)}, bf16[32,1024]{1,0:T(8,128)(2,1)S(1)}, u32[]{:S(2)}, u32[]{:S(2)}) collective-permute-start(bf16[32,1024]{1,0:T(8,128)(2,1)S(1)} %get-tuple-element.28), channel_id=1, source_target_pairs={{0,1},{1,2},{2,3},{3,0},{4,5},{5,6},{6,7},{7,4},{8,9},{9,10},{10,1... | collective-permute-start | bytes 196616 | tf_op jit(solution)/shard_map/ppermute | solution.py:96
  8.3 5.9 %collective-permute-start.2 = (bf16[32,1024]{1,0:T(8,128)(2,1)S(1)}, bf16[32,1024]{1,0:T(8,128)(2,1)S(1)}, u32[]{:S(2)}, u32[]{:S(2)}) collective-permute-start(bf16[32,1024]{1,0:T(8,128)(2,1)S(1)} %get-tuple-element.29), channel_id=1, source_target_pairs={{0,3},{1,0},{2,1},{3,2},{4,7},{5,4},{6,5},{7,6},{8,11},{9,8},{10,9... | collective-permute-start | bytes 196616 | tf_op jit(solution)/shard_map/ppermute | solution.py:96
  10.6 7.0 %collective-permute-start.3 = (bf16[32,1024]{1,0:T(8,128)(2,1)S(1)}, bf16[32,1024]{1,0:T(8,128)(2,1)S(1)}, u32[]{:S(2)}, u32[]{:S(2)}) collective-permute-start(bf16[32,1024]{1,0:T(8,128)(2,1)S(1)} %get-tuple-element.31), channel_id=1, source_target_pairs={{0,2},{1,3},{2,0},{3,1},{4,6},{5,7},{6,4},{7,5},{8,10},{9,11},{10,... | collective-permute-start | bytes 196616 | tf_op jit(solution)/shard_map/ppermute | solution.py:96
  17.9 0.8 %copy-start.2 = (bf16[128,2048]{1,0:T(8,128)(2,1)}, bf16[128,2048]{1,0:T(8,128)(2,1)S(1)}, u32[]{:S(2)}) copy-start(bf16[128,2048]{1,0:T(8,128)(2,1)S(1)} %collective-permute-done.1.next_ref.kvn_ref) | copy-start | bytes 1572868
  18.7 0.8 %copy-start.3 = (bf16[128,2048]{1,0:T(8,128)(2,1)}, bf16[128,2048]{1,0:T(8,128)(2,1)S(1)}, u32[]{:S(2)}) copy-start(bf16[128,2048]{1,0:T(8,128)(2,1)S(1)} %collective-permute-done.prev_ref.kvp_ref) | copy-start | bytes 1572868
  23.1 6.8 %copy-start.7 = (f32[128,8]{1,0:T(8,128)S(1)}, f32[128,8]{1,0:T(8,128)}, u32[]{:S(2)}) copy-start(f32[128,8]{1,0:T(8,128)} %get-tuple-element.12) | copy-start | bytes 12292
  23.1 9.4 %copy-start.5 = (bf16[128,1024]{1,0:T(8,128)(2,1)S(1)}, bf16[128,1024]{1,0:T(8,128)(2,1)}, u32[]{:S(2)}) copy-start(bf16[128,1024]{1,0:T(8,128)(2,1)} %get-tuple-element.11) | copy-start | bytes 786436
  24.3 3.6 %collective-permute-start.5 = (f32[128,2]{0,1:T(2,128)S(1)}, f32[128,2]{0,1:T(2,128)S(1)}, u32[]{:S(2)}, u32[]{:S(2)}) collective-permute-start(f32[128,2]{0,1:T(2,128)S(1)} %pad_maximum_fusion), channel_id=1, source_target_pairs={{0,1},{1,0},{2,3},{3,2},{4,5},{5,4},{6,7},{7,6},{8,9},{9,8},{10,11... | collective-permute-start | bytes 3080 | tf_op jit(solution)/shard_map/ppermute | solution.py:64
  27.9 4.5 %collective-permute-start.6 = (f32[128,2]{0,1:T(2,128)S(1)}, f32[128,2]{0,1:T(2,128)S(1)}, u32[]{:S(2)}, u32[]{:S(2)}) collective-permute-start(f32[128,2]{0,1:T(2,128)S(1)} %fusion.27), channel_id=1, source_target_pairs={{0,2},{1,3},{2,0},{3,1},{4,6},{5,7},{6,4},{7,5},{8,10},{9,11},{10,... | collective-permute-start | bytes 3080 | tf_op jit(solution)/shard_map/ppermute | solution.py:64
  38.7 16.2 %copy-start.4 = (f32[128,2048]{1,0:T(8,128)S(1)}, f32[128,2048]{1,0:T(8,128)}, u32[]{:S(2)}) copy-start(f32[128,2048]{1,0:T(8,128)} %get-tuple-element.14) | copy-start | bytes 3145732
  38.7 14.9 %collective-permute-start.10 = (bf16[128,2048]{1,0:T(8,128)(2,1)}, bf16[128,2048]{1,0:T(8,128)(2,1)S(1)}, u32[]{:S(2)}, u32[]{:S(2)}) collective-permute-start(bf16[128,2048]{1,0:T(8,128)(2,1)} %get-tuple-element.15), channel_id=1, source_target_pairs={{4,0},{8,4},{12,8},{16,12},{20,16},{24,20},{28,24},{5,1},{9,5},{13... | collective-permute-start | bytes 1572872 | tf_op jit(solution)/shard_map/ppermute | solution.py:25
  40.8 14.2 %collective-permute-start.11 = (bf16[128,2048]{1,0:T(8,128)(2,1)}, bf16[128,2048]{1,0:T(8,128)(2,1)S(1)}, u32[]{:S(2)}, u32[]{:S(2)}) collective-permute-start(bf16[128,2048]{1,0:T(8,128)(2,1)} %get-tuple-element.16), channel_id=1, source_target_pairs={{0,4},{4,8},{8,12},{12,16},{16,20},{20,24},{24,28},{1,5},{5,9},{9,... | collective-permute-start | bytes 1572872 | tf_op jit(solution)/shard_map/ppermute | solution.py:25
  43.3 6.4 %collective-permute-start.9 = (bf16[32,1024]{1,0:T(8,128)(2,1)S(1)}, bf16[32,1024]{1,0:T(8,128)(2,1)S(1)}, u32[]{:S(2)}, u32[]{:S(2)}) collective-permute-start(bf16[32,1024]{1,0:T(8,128)(2,1)S(1)} %get-tuple-element.24), channel_id=1, source_target_pairs={{0,1},{1,2},{2,3},{3,0},{4,5},{5,6},{6,7},{7,4},{8,9},{9,10},{10,1... | collective-permute-start | bytes 196616 | tf_op jit(solution)/shard_map/ppermute | solution.py:115
  44.2 8.3 %collective-permute-start.8 = (bf16[32,1024]{1,0:T(8,128)(2,1)S(1)}, bf16[32,1024]{1,0:T(8,128)(2,1)S(1)}, u32[]{:S(2)}, u32[]{:S(2)}) collective-permute-start(bf16[32,1024]{1,0:T(8,128)(2,1)S(1)} %get-tuple-element.25), channel_id=1, source_target_pairs={{0,2},{1,3},{2,0},{3,1},{4,6},{5,7},{6,4},{7,5},{8,10},{9,11},{10,... | collective-permute-start | bytes 196616 | tf_op jit(solution)/shard_map/ppermute | solution.py:115
  46.8 5.8 %collective-permute-start.7 = (bf16[32,1024]{1,0:T(8,128)(2,1)S(1)}, bf16[32,1024]{1,0:T(8,128)(2,1)S(1)}, u32[]{:S(2)}, u32[]{:S(2)}) collective-permute-start(bf16[32,1024]{1,0:T(8,128)(2,1)S(1)} %get-tuple-element.26), channel_id=1, source_target_pairs={{0,3},{1,0},{2,1},{3,2},{4,7},{5,4},{6,5},{7,6},{8,11},{9,8},{10,9... | collective-permute-start | bytes 196616 | tf_op jit(solution)/shard_map/ppermute | solution.py:115

commit v7 on v6

--- a/solution.py
+++ b/solution.py
@@ -138,52 +138,76 @@
     return jnp.concatenate(parts, axis=1)
 
 
-def _window(k_ref, v_ref, prev_ref, next_ref, h):
-    width = k_ref.shape[1]
+def _window(refs, h):
+    k_ref, v_ref, kp_ref, vp_ref, kn_ref, vn_ref = refs
     cols = slice(h * HSZ, (h + 1) * HSZ)
-    far = slice(width + h * HSZ, width + (h + 1) * HSZ)
-    keys = [prev_ref[:, cols], k_ref[:, cols], next_ref[:, cols]]
-    values = [prev_ref[:, far], v_ref[:, cols], next_ref[:, far]]
+    keys = [kp_ref[:, cols], k_ref[:, cols], kn_ref[:, cols]]
+    values = [vp_ref[:, cols], v_ref[:, cols], vn_ref[:, cols]]
     return keys, values
 
 
-def _forward_kernel(mask_ref, q_ref, k_ref, v_ref, prev_ref, next_ref, out_ref, lse_ref, *, heads, scale):
+def _group(heads):
+    return max(g for g in (1, 2, 4) if heads % g == 0)
+
+
+def _block_specs(length, group, steps):
+    span = group * HSZ
+    own = pl.BlockSpec((length, span), lambda j: (0, j))
+    far = pl.BlockSpec((length, span), lambda j: (0, steps + j))
+    rows = pl.BlockSpec((1, group, length), lambda j: (j, 0, 0))
+    pair = pl.BlockSpec((2, length, span), lambda j: (0, 0, j))
+    return own, far, rows, pair
+
+
+def _forward_kernel(mask_ref, q_ref, k_ref, v_ref, kp_ref, vp_ref, kn_ref, vn_ref, out_ref, lse_ref, *,
+                    heads, scale):
+    refs = (k_ref, v_ref, kp_ref, vp_ref, kn_ref, vn_ref)
+    length = q_ref.shape[0]
+    row = lax.broadcasted_iota(jnp.int32, (3 * length, 1), 0)
+    live = jnp.zeros((3 * length, 1), jnp.bool_)
+    for c in range(3):
+        live = live | ((row >= c * length) & (row < (c + 1) * length) & (mask_ref[c] > 0))
+
     def scores(h):
-        keys, values = _window(k_ref, v_ref, prev_ref, next_ref, h)
-        return _scores(mask_ref, q_ref[:, h * HSZ:(h + 1) * HSZ], keys, scale), values
+        keys, values = _window(refs, h)
+        s_t = _nt(jnp.concatenate(keys, axis=0), q_ref[:, h * HSZ:(h + 1) * HSZ]) * scale
+        return jnp.where(live, s_t, NEGATIVE), values
 
     ahead = [scores(h) for h in range(min(LOOKAHEAD, heads))]
     for h in range(heads):
-        s, values = ahead.pop(0)
+        s_t, values = ahead.pop(0)
         if h + LOOKAHEAD < heads:
             ahead.append(scores(h + LOOKAHEAD))
-        peak = jnp.max(s, -1, keepdims=True)
-        lse = peak + jnp.log(jnp.sum(jnp.exp(s - peak), -1, keepdims=True))
-        p = jnp.exp(s - lse).astype(jnp.bfloat16)
+        peak = jnp.max(s_t, 0, keepdims=True)
+        lse = peak + jnp.log(jnp.sum(jnp.exp(s_t - peak), 0, keepdims=True))
+        p_t = jnp.exp(s_t - lse).astype(jnp.bfloat16)
         v = jnp.concatenate(values, axis=0)
-        out_ref[:, h * HSZ:(h + 1) * HSZ] = _nn(p, v).astype(out_ref.dtype)
-        lse_ref[:, h:h + 1] = lse
+        out_ref[:, h * HSZ:(h + 1) * HSZ] = _tn(p_t, v).astype(out_ref.dtype)
+        lse_ref[0, h:h + 1, :] = lse
 
 
 def attend_forward(mask_row, q, k, v, kv_prev, kv_next):
     length, width = q.shape
     heads = width // HSZ
-    kern = functools.partial(_forward_kernel, heads=heads, scale=HSZ ** (-0.5))
-    vmem = pl.BlockSpec(memory_space=pltpu.VMEM)
+    group = _group(heads)
+    steps = heads // group
+    own, far, rows, _ = _block_specs(length, group, steps)
     return pl.pallas_call(
-        kern,
+        functools.partial(_forward_kernel, heads=group, scale=HSZ ** (-0.5)),
+        grid=(steps,),
         out_shape=(jax.ShapeDtypeStruct((length, width), jnp.bfloat16),
-                   jax.ShapeDtypeStruct((length, heads), jnp.float32)),
-        in_specs=[pl.BlockSpec(memory_space=pltpu.SMEM)] + [vmem] * 5,
-        out_specs=(vmem, vmem),
+                   jax.ShapeDtypeStruct((steps, group, length), jnp.float32)),
+        in_specs=[pl.BlockSpec(memory_space=pltpu.SMEM), own, own, own, own, far, own, far],
+        out_specs=(own, rows),
         cost_estimate=pl.CostEstimate(
             flops=12 * length * length * width, transcendentals=6 * length * length * heads,
             bytes_accessed=16 * length * width),
-    )(mask_row, q, k, v, kv_prev, kv_next)
-
-
-def _backward_kernel(mask_ref, q_ref, k_ref, v_ref, kvp_ref, kvn_ref, g_ref, lse_ref, delta_ref,
+    )(mask_row, q, k, v, kv_prev, kv_prev, kv_next, kv_next)
+
+
+def _backward_kernel(mask_ref, q_ref, k_ref, v_ref, kp_ref, vp_ref, kn_ref, vn_ref, g_ref, lse_ref, delta_ref,
                      dq_ref, prev_ref, next_ref, own_ref, *, heads, scale):
+    refs = (k_ref, v_ref, kp_ref, vp_ref, kn_ref, vn_ref)
     length = q_ref.shape[0]
     width = q_ref.shape[1]
     row = lax.broadcasted_iota(jnp.int32, (3 * length, 1), 0)
@@ -195,7 +219,7 @@
         cols = slice(h * HSZ, (h + 1) * HSZ)
         q = q_ref[:, cols]
         g = g_ref[:, cols]
-        keys, vals = _window(k_ref, v_ref, kvp_ref, kvn_ref, h)
+        keys, vals = _window(refs, h)
         keys = jnp.concatenate(keys, axis=0)
         s_t = jnp.where(live, _nt(keys, q) * scale, NEGATIVE)
         dp_t = _nt(jnp.concatenate(vals, axis=0), g)
@@ -207,33 +231,35 @@
         q, g, keys, s_t, dp_t = ahead.pop(0)
         if h + LOOKAHEAD < heads:
             ahead.append(front(h + LOOKAHEAD))
-        p_t = jnp.exp(s_t - lse_ref[h:h + 1, :])
-        ds_t = (p_t * (dp_t - delta_ref[h:h + 1, :])).astype(jnp.bfloat16)
+        p_t = jnp.exp(s_t - lse_ref[0, h:h + 1, :])
+        ds_t = (p_t * (dp_t - delta_ref[0, h:h + 1, :])).astype(jnp.bfloat16)
         dq_ref[:, cols] = (_tn(ds_t, keys) * scale).astype(dq_ref.dtype)
         dk = _nn(ds_t, q) * scale
         dv = _nn(p_t.astype(jnp.bfloat16), g)
         for c, ref in enumerate((prev_ref, own_ref, next_ref)):
             blk = slice(c * length, (c + 1) * length)
-            ref[:, cols] = dk[blk].astype(ref.dtype)
-            ref[:, width + h * HSZ:width + (h + 1) * HSZ] = dv[blk].astype(ref.dtype)
+            ref[0, :, cols] = dk[blk].astype(ref.dtype)
+            ref[1, :, cols] = dv[blk].astype(ref.dtype)
 
 
 def attend_backward(mask_row, q, k, v, kv_prev, kv_next, grad, lse, delta):
     length, width = q.shape
     heads = width // HSZ
-    kern = functools.partial(_backward_kernel, heads=heads, scale=HSZ ** (-0.5))
-    vmem = pl.BlockSpec(memory_space=pltpu.VMEM)
-    sent = jax.ShapeDtypeStruct((length, 2 * width), jnp.bfloat16)
+    group = _group(heads)
+    steps = heads // group
+    own, far, rows, pair = _block_specs(length, group, steps)
+    sent = jax.ShapeDtypeStruct((2, length, width), jnp.bfloat16)
     return pl.pallas_call(
-        kern,
+        functools.partial(_backward_kernel, heads=group, scale=HSZ ** (-0.5)),
+        grid=(steps,),
         out_shape=(jax.ShapeDtypeStruct((length, width), jnp.bfloat16), sent, sent,
-                   jax.ShapeDtypeStruct((length, 2 * width), jnp.float32)),
-        in_specs=[pl.BlockSpec(memory_space=pltpu.SMEM)] + [vmem] * 8,
-        out_specs=(vmem, vmem, vmem, vmem),
+                   jax.ShapeDtypeStruct((2, length, width), jnp.float32)),
+        in_specs=[pl.BlockSpec(memory_space=pltpu.SMEM), own, own, own, own, far, own, far, own, rows, rows],
+        out_specs=(own, pair, pair, pair),
         cost_estimate=pl.CostEstimate(
             flops=30 * length * length * width, transcendentals=3 * length * length * heads,
             bytes_accessed=36 * length * width),
-    )(mask_row, q, k, v, kv_prev, kv_next, grad, lse.T, delta.T)
+    )(mask_row, q, k, v, kv_prev, kv_prev, kv_next, kv_next, grad, lse, delta.T.reshape(lse.shape))
 
 
 def per_device(queries, key_rows, value_rows, view_mask, norm_gain, normed_grad):
@@ -274,7 +300,8 @@
     total = own + passed_along(to_prev, "ctx", -1).astype(jnp.float32)
     total = total + passed_along(to_next, "ctx", 1).astype(jnp.float32)
     total = total.astype(jnp.bfloat16)
-    return (normed, query_grad, total[:, :width], total[:, width:])
+    return (normed, query_grad, total[0], total[1])
+
 
 def solution(mesh):
     placed = (P("ctx", "tp"), P("ctx", "tp"), P("ctx", "tp"), P(), P(), P(("ctx", "tp"), None))

time: 56.3 us -> 55.8 us (level)
  local copies, waits for them, and re-layouts: 7.1 us -> 6.35 us
  waiting for transfers between devices: 15.3 us -> 16 us
    slice x1 -> x0, local copies, waits for them, and re-layouts: 0.83 us -> none  [per_device(): return (normed, query_grad, total[:, :width], total[:, width:])]
    squeeze x0 -> x1, local copies, waits for them, and re-layouts: none -> 0.82 us  [per_device(): return (normed, query_grad, total[0], total[1])]
    transpose x0 -> x1, local copies, waits for them, and re-layouts: none -> 0.66 us  [attend_backward(): delta.T.reshape(lse.shape)]
    reduce_sum x1 -> x0, local copies, waits for them, and re-layouts: 0.66 us -> none  [per_device(): jnp.sum(grad_heads.astype(jnp.float32) * out_heads.astype(jnp.float32), -1)]
    pallas_call x1 -> x0, local copies, waits for them, and re-layouts: 0.66 us -> none  [attend_forward(): pl.pallas_call(kern, out_shape=(jax.ShapeDtypeStruct((length, width), jnp...]
    ppermute x2, waiting for transfers between devices: 4.65 us -> 5.27 us  [tp_sum(): lax.ppermute(total, 'tp', [(i, i ^ 1 << b) for i in range(peers)])]
    unnamed x18 -> x16, local copies, waits for them, and re-layouts: 2.7 us -> 2.69 us
  transfers between devices with their start and end apart: 12 -> 12, of which waited for: 10 -> 10; matrix products, arithmetic and copies ran while one was open for 6% -> 5% of each run, Pallas kernels for 0% -> 0%
where the time goes in v7:
time: 55.8 us; the launch traced here: 55.5 us
  starting transfers between devices  21.7 us (39%)
  waiting for transfers between devices  16 us (29%)
  Pallas kernels  7.26 us (13%)
  local copies, waits for them, and re-layouts  6.35 us (11%)
  other arithmetic  3.31 us (6%)
  between operations  0.91 us (2%)
    ppermute x4, starting transfers between devices, passed_along(): return lax.ppermute(x, axis, pairs)  9.29 us
    ppermute x2, waiting for transfers between devices, tp_sum(): lax.ppermute(total, 'tp', [(i, i ^ 1 << b) for i in range(peers)])  5.27 us
    ppermute x3, starting transfers between devices, heads_to_tiles(): chunk = lax.ppermute(chunk, 'tp', [(i, (i + shift) % n) for i in range(n)])  4.87 us
    ppermute x3, waiting for transfers between devices, tiles_to_heads(): chunk = lax.ppermute(chunk, 'tp', [(i, (i + shift) % n) for i in range(n)])  4.8 us
    ppermute x3, starting transfers between devices, tiles_to_heads(): chunk = lax.ppermute(chunk, 'tp', [(i, (i + shift) % n) for i in range(n)])  4.67 us
    ppermute x3, waiting for transfers between devices, heads_to_tiles(): chunk = lax.ppermute(chunk, 'tp', [(i, (i + shift) % n) for i in range(n)])  4.47 us
    pallas_call x1, Pallas kernels, attend_backward(): pl.pallas_call(functools.partial(_backward_kernel, heads=group, scale=HSZ...  3.78 us
    pallas_call x1, Pallas kernels, attend_forward(): pl.pallas_call(functools.partial(_forward_kernel, heads=group, scale=HSZ...  3.48 us
  transfers between devices with their start and end apart: 12, of which 10 were waited for; matrix products, arithmetic and copies ran while one was open for 5% of the time, Pallas kernels for 0%

profile of v7, /device:TPU:4, one launch (start us, length us, event | category | flops | bytes accessed | tf_op | source)
XLA Modules:
  0.0 55.5 jit_solution(8445282024693873855)
XLA Ops:
  0.7 1.0 %constant_dynamic-update-slice_fusion.1 = bf16[128,2048]{1,0:T(8,128)(2,1)S(1)} fusion(bf16[128,1024]{1,0:T(8,128)(2,1)} %k_ref.3), kind=kLoop, calls=%fused_computation.60 | loop fusion | bytes 524288
  1.7 2.9 %collective-permute-start.1 = (bf16[128,2048]{1,0:T(8,128)(2,1)S(1)}, bf16[128,2048]{1,0:T(8,128)(2,1)S(1)}, u32[]{:S(2)}, u32[]{:S(2)}) collective-permute-start(bf16[128,2048]{1,0:T(8,128)(2,1)S(1)} %constant_dynamic-update-slice_fusion), channel_id=1, source_target_pairs={{4,0},{8,4},{12,8},{16,12},{20,16},{24,20},{28,24},{5,1},{9,5},{13... | collective-permute-start | bytes 1572872 | tf_op jit(solution)/shard_map/ppermute | solution.py:25
  4.6 1.9 %collective-permute-start = (bf16[128,2048]{1,0:T(8,128)(2,1)S(1)}, bf16[128,2048]{1,0:T(8,128)(2,1)S(1)}, u32[]{:S(2)}, u32[]{:S(2)}) collective-permute-start(bf16[128,2048]{1,0:T(8,128)(2,1)S(1)} %constant_dynamic-update-slice_fusion), channel_id=1, source_target_pairs={{0,4},{4,8},{8,12},{12,16},{16,20},{20,24},{24,28},{1,5},{5,9},{9,... | collective-permute-start | bytes 1572872 | tf_op jit(solution)/shard_map/ppermute | solution.py:25
  6.7 1.6 %collective-permute-start.4 = (bf16[32,1024]{1,0:T(8,128)(2,1)S(1)}, bf16[32,1024]{1,0:T(8,128)(2,1)S(1)}, u32[]{:S(2)}, u32[]{:S(2)}) collective-permute-start(bf16[32,1024]{1,0:T(8,128)(2,1)S(1)} %get-tuple-element.28), channel_id=1, source_target_pairs={{0,1},{1,2},{2,3},{3,0},{4,5},{5,6},{6,7},{7,4},{8,9},{9,10},{10,1... | collective-permute-start | bytes 196616 | tf_op jit(solution)/shard_map/ppermute | solution.py:96
  8.3 2.2 %collective-permute-start.2 = (bf16[32,1024]{1,0:T(8,128)(2,1)S(1)}, bf16[32,1024]{1,0:T(8,128)(2,1)S(1)}, u32[]{:S(2)}, u32[]{:S(2)}) collective-permute-start(bf16[32,1024]{1,0:T(8,128)(2,1)S(1)} %get-tuple-element.29), channel_id=1, source_target_pairs={{0,3},{1,0},{2,1},{3,2},{4,7},{5,4},{6,5},{7,6},{8,11},{9,8},{10,9... | collective-permute-start | bytes 196616 | tf_op jit(solution)/shard_map/ppermute | solution.py:96
  14.2 3.4 %collective-permute-done.3 = bf16[32,1024]{1,0:T(8,128)(2,1)S(1)} collective-permute-done((bf16[32,1024]{1,0:T(8,128)(2,1)S(1)}, bf16[32,1024]{1,0:T(8,128)(2,1)S(1)}, u32[]{:S(2)}, u32[]{:S(2)}) %collective-permute-start.3) | collective-permute-done | bytes 65568 | tf_op jit(solution)/shard_map/ppermute | solution.py:96
  18.7 0.8 %copy-done.2 = bf16[128,2048]{1,0:T(8,128)(2,1)} copy-done((bf16[128,2048]{1,0:T(8,128)(2,1)}, bf16[128,2048]{1,0:T(8,128)(2,1)S(1)}, u32[]{:S(2)}) %copy-start.2) | copy-done | bytes 524312
  19.5 3.5 %shard_map.93 = (bf16[128,1024]{1,0:T(8,128)(2,1)}, f32[2,4,128]{2,1,0:T(4,128)}) custom-call(s32[3]{0:T(128)} %fusion.26.mask_ref, bf16[128,1024]{1,0:T(8,128)(2,1)} %q_ref.3, bf16[128,1024]{1,0:T(8,128)(2,1)} %k_ref.3, bf16[128,1024]{1,0:T(8,128)(2,1)} %v_ref.3, bf16[128,2048]{1,0:T(8,128)(2,1)} %copy-done.2, bf16[128,2048]{1,0:T(8,128)(2,1)} %copy-done.2, ...), custom_call_target="tpu_custom_call" | custom-call | flops 201326592 | bytes 2097152 | tf_op jit(solution)/shard_map/pallas_call | solution.py:195
  23.0 1.2 %fusion.7 = (f32[128]{0:T(128)S(1)}, f32[128]{0:T(128)S(1)}) fusion(bf16[128,1024]{1,0:T(8,128)(2,1)} %get-tuple-element.11, f32[1024]{0:T(1024)S(1)} %dynamic_slice.38, bf16[4,32,1024]{2,1,0:T(8,128)(2,1)S(1)} %fusion.22), kind=kLoop, calls=%fused_computation.12 | loop fusion | flops 917248 | bytes 529408 | tf_op jit(solution)/shard_map/reduce_sum | solution.py:285
  24.2 0.9 %collective-permute-start.5 = (f32[128,2]{0,1:T(2,128)S(1)}, f32[128,2]{0,1:T(2,128)S(1)}, u32[]{:S(2)}, u32[]{:S(2)}) collective-permute-start(f32[128,2]{0,1:T(2,128)S(1)} %pad_maximum_fusion), channel_id=1, source_target_pairs={{0,1},{1,0},{2,3},{3,2},{4,5},{5,4},{6,7},{7,6},{8,9},{9,8},{10,11... | collective-permute-start | bytes 3080 | tf_op jit(solution)/shard_map/ppermute | solution.py:64
  25.2 2.7 %collective-permute-done.5 = f32[128,2]{0,1:T(2,128)S(1)} collective-permute-done((f32[128,2]{0,1:T(2,128)S(1)}, f32[128,2]{0,1:T(2,128)S(1)}, u32[]{:S(2)}, u32[]{:S(2)}) %collective-permute-start.5) | collective-permute-done | bytes 1056 | tf_op jit(solution)/shard_map/ppermute | solution.py:64
  27.9 2.0 %collective-permute-start.6 = (f32[128,2]{0,1:T(2,128)S(1)}, f32[128,2]{0,1:T(2,128)S(1)}, u32[]{:S(2)}, u32[]{:S(2)}) collective-permute-start(f32[128,2]{0,1:T(2,128)S(1)} %fusion.27), channel_id=1, source_target_pairs={{0,2},{1,3},{2,0},{3,1},{4,6},{5,7},{6,4},{7,5},{8,10},{9,11},{10,... | collective-permute-start | bytes 3080 | tf_op jit(solution)/shard_map/ppermute | solution.py:64
  29.8 2.6 %collective-permute-done.6 = f32[128,2]{0,1:T(2,128)S(1)} collective-permute-done((f32[128,2]{0,1:T(2,128)S(1)}, f32[128,2]{0,1:T(2,128)S(1)}, u32[]{:S(2)}, u32[]{:S(2)}) %collective-permute-start.6) | collective-permute-done | bytes 1056 | tf_op jit(solution)/shard_map/ppermute | solution.py:64
  32.4 1.0 %fusion.9 = (f32[16,8,8,128]{3,1,2,0:T(8,128)S(1)}, bf16[128,1024]{1,0:T(8,128)(2,1)}, bf16[128,1024]{1,0:T(8,128)(2,1)S(1)}) fusion(bf16[128,1024]{1,0:T(8,128)(2,1)S(1)} %copy-done.5, f32[128]{0:T(128)S(1)} %get-tuple-element.32, f32[1024]{0:T(1024)S(1)} %dynamic_slice.38, bf16[4,32,1024]{2,1,0:T(8,128)(2,1)S(1)} %fusion.22, f32[128]{0:T(128)S(1)} %get-tuple-element.33), kind=kLoop, calls=%fused_computation.14 | loop fusion | flops 1835008 | bytes 1577984
  34.4 3.8 %shard_map.94 = (bf16[128,1024]{1,0:T(8,128)(2,1)}, bf16[2,128,1024]{2,1,0:T(8,128)(2,1)}, bf16[2,128,1024]{2,1,0:T(8,128)(2,1)}, f32[2,128,1024]{2,1,0:T(8,128)}) custom-call(s32[3]{0:T(128)} %fusion.26.mask_ref, bf16[128,1024]{1,0:T(8,128)(2,1)} %q_ref.3, bf16[128,1024]{1,0:T(8,128)(2,1)} %k_ref.3, bf16[128,1024]{1,0:T(8,128)(2,1)} %v_ref.3, ...), custom_call_target="tpu_custom_call" | custom-call | flops 503316480 | bytes 4718592 | tf_op jit(solution)/shard_map/pallas_call | solution.py:252
  38.2 2.1 %collective-permute-start.10 = (bf16[2,128,1024]{2,1,0:T(8,128)(2,1)}, bf16[2,128,1024]{2,1,0:T(8,128)(2,1)S(1)}, u32[]{:S(2)}, u32[]{:S(2)}) collective-permute-start(bf16[2,128,1024]{2,1,0:T(8,128)(2,1)} %get-tuple-element.15), channel_id=1, source_target_pairs={{4,0},{8,4},{12,8},{16,12},{20,16},{24,20},{28,24},{5,1},{9,5},{13... | collective-permute-start | bytes 1572872 | tf_op jit(solution)/shard_map/ppermute | solution.py:25
  40.2 2.4 %collective-permute-start.11 = (bf16[2,128,1024]{2,1,0:T(8,128)(2,1)}, bf16[2,128,1024]{2,1,0:T(8,128)(2,1)S(1)}, u32[]{:S(2)}, u32[]{:S(2)}) collective-permute-start(bf16[2,128,1024]{2,1,0:T(8,128)(2,1)} %get-tuple-element.16), channel_id=1, source_target_pairs={{0,4},{4,8},{8,12},{12,16},{16,20},{20,24},{24,28},{1,5},{5,9},{9,... | collective-permute-start | bytes 1572872 | tf_op jit(solution)/shard_map/ppermute | solution.py:25
  42.7 0.9 %collective-permute-start.9 = (bf16[32,1024]{1,0:T(8,128)(2,1)S(1)}, bf16[32,1024]{1,0:T(8,128)(2,1)S(1)}, u32[]{:S(2)}, u32[]{:S(2)}) collective-permute-start(bf16[32,1024]{1,0:T(8,128)(2,1)S(1)} %get-tuple-element.24), channel_id=1, source_target_pairs={{0,1},{1,2},{2,3},{3,0},{4,5},{5,6},{6,7},{7,4},{8,9},{9,10},{10,1... | collective-permute-start | bytes 196616 | tf_op jit(solution)/shard_map/ppermute | solution.py:115
  43.7 2.6 %collective-permute-start.8 = (bf16[32,1024]{1,0:T(8,128)(2,1)S(1)}, bf16[32,1024]{1,0:T(8,128)(2,1)S(1)}, u32[]{:S(2)}, u32[]{:S(2)}) collective-permute-start(bf16[32,1024]{1,0:T(8,128)(2,1)S(1)} %get-tuple-element.25), channel_id=1, source_target_pairs={{0,2},{1,3},{2,0},{3,1},{4,6},{5,7},{6,4},{7,5},{8,10},{9,11},{10,... | collective-permute-start | bytes 196616 | tf_op jit(solution)/shard_map/ppermute | solution.py:115
  46.2 1.3 %collective-permute-start.7 = (bf16[32,1024]{1,0:T(8,128)(2,1)S(1)}, bf16[32,1024]{1,0:T(8,128)(2,1)S(1)}, u32[]{:S(2)}, u32[]{:S(2)}) collective-permute-start(bf16[32,1024]{1,0:T(8,128)(2,1)S(1)} %get-tuple-element.26), channel_id=1, source_target_pairs={{0,3},{1,0},{2,1},{3,2},{4,7},{5,4},{6,5},{7,6},{8,11},{9,8},{10,9... | collective-permute-start | bytes 196616 | tf_op jit(solution)/shard_map/ppermute | solution.py:115
  47.6 1.6 %collective-permute-done.9 = bf16[32,1024]{1,0:T(8,128)(2,1)S(1)} collective-permute-done((bf16[32,1024]{1,0:T(8,128)(2,1)S(1)}, bf16[32,1024]{1,0:T(8,128)(2,1)S(1)}, u32[]{:S(2)}, u32[]{:S(2)}) %collective-permute-start.9) | collective-permute-done | bytes 65568 | tf_op jit(solution)/shard_map/ppermute | solution.py:115
  49.2 2.7 %collective-permute-done.8 = bf16[32,1024]{1,0:T(8,128)(2,1)S(1)} collective-permute-done((bf16[32,1024]{1,0:T(8,128)(2,1)S(1)}, bf16[32,1024]{1,0:T(8,128)(2,1)S(1)}, u32[]{:S(2)}, u32[]{:S(2)}) %collective-permute-start.8) | collective-permute-done | bytes 65568 | tf_op jit(solution)/shard_map/ppermute | solution.py:115
  53.1 1.3 %collective-permute-done.11 = bf16[2,128,1024]{2,1,0:T(8,128)(2,1)S(1)} collective-permute-done((bf16[2,128,1024]{2,1,0:T(8,128)(2,1)}, bf16[2,128,1024]{2,1,0:T(8,128)(2,1)S(1)}, u32[]{:S(2)}, u32[]{:S(2)}) %collective-permute-start.11) | collective-permute-done | bytes 524320 | tf_op jit(solution)/shard_map/ppermute | solution.py:25
  54.7 0.8 %slice_bitcast_fusion = (bf16[128,1024]{1,0:T(8,128)(2,1)}, bf16[128,1024]{1,0:T(8,128)(2,1)}) fusion(bf16[2,128,1024]{2,1,0:T(8,128)(2,1)S(1)} %add_convert_fusion), kind=kLoop, calls=%fused_computation.48 | loop fusion | bytes 1048576 | tf_op jit(solution)/shard_map/squeeze | solution.py:303
  (36 shorter events, 7.3 us)
Async XLA Ops:
  0.6 10.7 %copy-start = (s32[8,3]{0,1:T(4,128)S(1)}, s32[8,3]{0,1:T(4,128)}, u32[]{:S(2)}) copy-start(s32[8,3]{0,1:T(4,128)} %param.11) | copy-start | bytes 292
  0.6 1.0 %copy-start.3 = (bf16[128,1024]{1,0:T(8,128)(2,1)S(1)}, bf16[128,1024]{1,0:T(8,128)(2,1)}, u32[]{:S(2)}) copy-start(bf16[128,1024]{1,0:T(8,128)(2,1)} %v_ref.3) | copy-start | bytes 786436
  1.7 5.0 %copy-start.6 = (bf16[32,4096]{1,0:T(8,128)(2,1)S(1)}, bf16[32,4096]{1,0:T(8,128)(2,1)}, u32[]{:S(2)}) copy-start(bf16[32,4096]{1,0:T(8,128)(2,1)} %param.13) | copy-start | bytes 786436
  1.7 16.1 %collective-permute-start.1 = (bf16[128,2048]{1,0:T(8,128)(2,1)S(1)}, bf16[128,2048]{1,0:T(8,128)(2,1)S(1)}, u32[]{:S(2)}, u32[]{:S(2)}) collective-permute-start(bf16[128,2048]{1,0:T(8,128)(2,1)S(1)} %constant_dynamic-update-slice_fusion), channel_id=1, source_target_pairs={{4,0},{8,4},{12,8},{16,12},{20,16},{24,20},{28,24},{5,1},{9,5},{13... | collective-permute-start | bytes 1572872 | tf_op jit(solution)/shard_map/ppermute | solution.py:25
  4.6 13.3 %collective-permute-start = (bf16[128,2048]{1,0:T(8,128)(2,1)S(1)}, bf16[128,2048]{1,0:T(8,128)(2,1)S(1)}, u32[]{:S(2)}, u32[]{:S(2)}) collective-permute-start(bf16[128,2048]{1,0:T(8,128)(2,1)S(1)} %constant_dynamic-update-slice_fusion), channel_id=1, source_target_pairs={{0,4},{4,8},{8,12},{12,16},{16,20},{20,24},{24,28},{1,5},{5,9},{9,... | collective-permute-start | bytes 1572872 | tf_op jit(solution)/shard_map/ppermute | solution.py:25
  6.7 6.8 %collective-permute-start.4 = (bf16[32,1024]{1,0:T(8,128)(2,1)S(1)}, bf16[32,1024]{1,0:T(8,128)(2,1)S(1)}, u32[]{:S(2)}, u32[]{:S(2)}) collective-permute-start(bf16[32,1024]{1,0:T(8,128)(2,1)S(1)} %get-tuple-element.28), channel_id=1, source_target_pairs={{0,1},{1,2},{2,3},{3,0},{4,5},{5,6},{6,7},{7,4},{8,9},{9,10},{10,1... | collective-permute-start | bytes 196616 | tf_op jit(solution)/shard_map/ppermute | solution.py:96
  8.3 5.9 %collective-permute-start.2 = (bf16[32,1024]{1,0:T(8,128)(2,1)S(1)}, bf16[32,1024]{1,0:T(8,128)(2,1)S(1)}, u32[]{:S(2)}, u32[]{:S(2)}) collective-permute-start(bf16[32,1024]{1,0:T(8,128)(2,1)S(1)} %get-tuple-element.29), channel_id=1, source_target_pairs={{0,3},{1,0},{2,1},{3,2},{4,7},{5,4},{6,5},{7,6},{8,11},{9,8},{10,9... | collective-permute-start | bytes 196616 | tf_op jit(solution)/shard_map/ppermute | solution.py:96
  10.6 7.0 %collective-permute-start.3 = (bf16[32,1024]{1,0:T(8,128)(2,1)S(1)}, bf16[32,1024]{1,0:T(8,128)(2,1)S(1)}, u32[]{:S(2)}, u32[]{:S(2)}) collective-permute-start(bf16[32,1024]{1,0:T(8,128)(2,1)S(1)} %get-tuple-element.31), channel_id=1, source_target_pairs={{0,2},{1,3},{2,0},{3,1},{4,6},{5,7},{6,4},{7,5},{8,10},{9,11},{10,... | collective-permute-start | bytes 196616 | tf_op jit(solution)/shard_map/ppermute | solution.py:96
  17.9 0.8 %copy-start.1 = (bf16[128,2048]{1,0:T(8,128)(2,1)}, bf16[128,2048]{1,0:T(8,128)(2,1)S(1)}, u32[]{:S(2)}) copy-start(bf16[128,2048]{1,0:T(8,128)(2,1)S(1)} %collective-permute-done.1.kn_ref.vn_ref) | copy-start | bytes 1572868
  18.7 0.8 %copy-start.2 = (bf16[128,2048]{1,0:T(8,128)(2,1)}, bf16[128,2048]{1,0:T(8,128)(2,1)S(1)}, u32[]{:S(2)}) copy-start(bf16[128,2048]{1,0:T(8,128)(2,1)S(1)} %collective-permute-done.kp_ref.vp_ref) | copy-start | bytes 1572868
  23.0 9.4 %copy-start.5 = (bf16[128,1024]{1,0:T(8,128)(2,1)S(1)}, bf16[128,1024]{1,0:T(8,128)(2,1)}, u32[]{:S(2)}) copy-start(bf16[128,1024]{1,0:T(8,128)(2,1)} %get-tuple-element.11) | copy-start | bytes 786436
  24.2 3.6 %collective-permute-start.5 = (f32[128,2]{0,1:T(2,128)S(1)}, f32[128,2]{0,1:T(2,128)S(1)}, u32[]{:S(2)}, u32[]{:S(2)}) collective-permute-start(f32[128,2]{0,1:T(2,128)S(1)} %pad_maximum_fusion), channel_id=1, source_target_pairs={{0,1},{1,0},{2,3},{3,2},{4,5},{5,4},{6,7},{7,6},{8,9},{9,8},{10,11... | collective-permute-start | bytes 3080 | tf_op jit(solution)/shard_map/ppermute | solution.py:64
  27.9 4.5 %collective-permute-start.6 = (f32[128,2]{0,1:T(2,128)S(1)}, f32[128,2]{0,1:T(2,128)S(1)}, u32[]{:S(2)}, u32[]{:S(2)}) collective-permute-start(f32[128,2]{0,1:T(2,128)S(1)} %fusion.27), channel_id=1, source_target_pairs={{0,2},{1,3},{2,0},{3,1},{4,6},{5,7},{6,4},{7,5},{8,10},{9,11},{10,... | collective-permute-start | bytes 3080 | tf_op jit(solution)/shard_map/ppermute | solution.py:64
  38.2 16.3 %copy-start.4 = (f32[2,128,1024]{2,1,0:T(8,128)S(1)}, f32[2,128,1024]{2,1,0:T(8,128)}, u32[]{:S(2)}) copy-start(f32[2,128,1024]{2,1,0:T(8,128)} %get-tuple-element.14) | copy-start | bytes 3145732
  38.2 14.9 %collective-permute-start.10 = (bf16[2,128,1024]{2,1,0:T(8,128)(2,1)}, bf16[2,128,1024]{2,1,0:T(8,128)(2,1)S(1)}, u32[]{:S(2)}, u32[]{:S(2)}) collective-permute-start(bf16[2,128,1024]{2,1,0:T(8,128)(2,1)} %get-tuple-element.15), channel_id=1, source_target_pairs={{4,0},{8,4},{12,8},{16,12},{20,16},{24,20},{28,24},{5,1},{9,5},{13... | collective-permute-start | bytes 1572872 | tf_op jit(solution)/shard_map/ppermute | solution.py:25
  40.2 14.2 %collective-permute-start.11 = (bf16[2,128,1024]{2,1,0:T(8,128)(2,1)}, bf16[2,128,1024]{2,1,0:T(8,128)(2,1)S(1)}, u32[]{:S(2)}, u32[]{:S(2)}) collective-permute-start(bf16[2,128,1024]{2,1,0:T(8,128)(2,1)} %get-tuple-element.16), channel_id=1, source_target_pairs={{0,4},{4,8},{8,12},{12,16},{16,20},{20,24},{24,28},{1,5},{5,9},{9,... | collective-permute-start | bytes 1572872 | tf_op jit(solution)/shard_map/ppermute | solution.py:25
  42.7 6.5 %collective-permute-start.9 = (bf16[32,1024]{1,0:T(8,128)(2,1)S(1)}, bf16[32,1024]{1,0:T(8,128)(2,1)S(1)}, u32[]{:S(2)}, u32[]{:S(2)}) collective-permute-start(bf16[32,1024]{1,0:T(8,128)(2,1)S(1)} %get-tuple-element.24), channel_id=1, source_target_pairs={{0,1},{1,2},{2,3},{3,0},{4,5},{5,6},{6,7},{7,4},{8,9},{9,10},{10,1... | collective-permute-start | bytes 196616 | tf_op jit(solution)/shard_map/ppermute | solution.py:115
  43.7 8.3 %collective-permute-start.8 = (bf16[32,1024]{1,0:T(8,128)(2,1)S(1)}, bf16[32,1024]{1,0:T(8,128)(2,1)S(1)}, u32[]{:S(2)}, u32[]{:S(2)}) collective-permute-start(bf16[32,1024]{1,0:T(8,128)(2,1)S(1)} %get-tuple-element.25), channel_id=1, source_target_pairs={{0,2},{1,3},{2,0},{3,1},{4,6},{5,7},{6,4},{7,5},{8,10},{9,11},{10,... | collective-permute-start | bytes 196616 | tf_op jit(solution)/shard_map/ppermute | solution.py:115
  46.2 5.8 %collective-permute-start.7 = (bf16[32,1024]{1,0:T(8,128)(2,1)S(1)}, bf16[32,1024]{1,0:T(8,128)(2,1)S(1)}, u32[]{:S(2)}, u32[]{:S(2)}) collective-permute-start(bf16[32,1024]{1,0:T(8,128)(2,1)S(1)} %get-tuple-element.26), channel_id=1, source_target_pairs={{0,3},{1,0},{2,1},{3,2},{4,7},{5,4},{6,5},{7,6},{8,11},{9,8},{10,9... | collective-permute-start | bytes 196616 | tf_op jit(solution)/shard_map/ppermute | solution.py:115

commit v8 on v7

--- a/solution.py
+++ b/solution.py
@@ -205,8 +205,8 @@
     )(mask_row, q, k, v, kv_prev, kv_prev, kv_next, kv_next)
 
 
-def _backward_kernel(mask_ref, q_ref, k_ref, v_ref, kp_ref, vp_ref, kn_ref, vn_ref, g_ref, lse_ref, delta_ref,
-                     dq_ref, prev_ref, next_ref, own_ref, *, heads, scale):
+def _backward_kernel(mask_ref, q_ref, k_ref, v_ref, kp_ref, vp_ref, kn_ref, vn_ref, t_ref, o_ref, gain_ref,
+                     norm_ref, lse_ref, dq_ref, prev_ref, next_ref, own_ref, *, heads, scale):
     refs = (k_ref, v_ref, kp_ref, vp_ref, kn_ref, vn_ref)
     length = q_ref.shape[0]
     width = q_ref.shape[1]
@@ -218,21 +218,26 @@
     def front(h):
         cols = slice(h * HSZ, (h + 1) * HSZ)
         q = q_ref[:, cols]
-        g = g_ref[:, cols]
+        inverse = norm_ref[:, 0:1]
+        inner_mean = norm_ref[:, 1:2]
+        out_f = o_ref[:, cols].astype(jnp.float32)
+        upstream = t_ref[:, cols].astype(jnp.float32) * gain_ref[:, cols]
+        g = (inverse * upstream - out_f * inverse * inverse * inverse * inner_mean).astype(jnp.bfloat16)
+        delta = jnp.sum((g.astype(jnp.float32) * out_f).T, 0, keepdims=True)
         keys, vals = _window(refs, h)
         keys = jnp.concatenate(keys, axis=0)
         s_t = jnp.where(live, _nt(keys, q) * scale, NEGATIVE)
         dp_t = _nt(jnp.concatenate(vals, axis=0), g)
-        return q, g, keys, s_t, dp_t
+        return q, g, keys, s_t, dp_t, delta
 
     ahead = [front(h) for h in range(min(LOOKAHEAD, heads))]
     for h in range(heads):
         cols = slice(h * HSZ, (h + 1) * HSZ)
-        q, g, keys, s_t, dp_t = ahead.pop(0)
+        q, g, keys, s_t, dp_t, delta = ahead.pop(0)
         if h + LOOKAHEAD < heads:
             ahead.append(front(h + LOOKAHEAD))
         p_t = jnp.exp(s_t - lse_ref[0, h:h + 1, :])
-        ds_t = (p_t * (dp_t - delta_ref[0, h:h + 1, :])).astype(jnp.bfloat16)
+        ds_t = (p_t * (dp_t - delta)).astype(jnp.bfloat16)
         dq_ref[:, cols] = (_tn(ds_t, keys) * scale).astype(dq_ref.dtype)
         dk = _nn(ds_t, q) * scale
         dv = _nn(p_t.astype(jnp.bfloat16), g)
@@ -242,7 +247,7 @@
             ref[1, :, cols] = dv[blk].astype(ref.dtype)
 
 
-def attend_backward(mask_row, q, k, v, kv_prev, kv_next, grad, lse, delta):
+def attend_backward(mask_row, q, k, v, kv_prev, kv_next, grad_tiles, attended, gain, norm, lse):
     length, width = q.shape
     heads = width // HSZ
     group = _group(heads)
@@ -254,12 +259,14 @@
         grid=(steps,),
         out_shape=(jax.ShapeDtypeStruct((length, width), jnp.bfloat16), sent, sent,
                    jax.ShapeDtypeStruct((2, length, width), jnp.float32)),
-        in_specs=[pl.BlockSpec(memory_space=pltpu.SMEM), own, own, own, own, far, own, far, own, rows, rows],
+        in_specs=[pl.BlockSpec(memory_space=pltpu.SMEM), own, own, own, own, far, own, far, own, own,
+                  pl.BlockSpec((1, group * HSZ), lambda j: (0, j)), pl.BlockSpec((length, 2), lambda j: (0, 0)),
+                  rows],
         out_specs=(own, pair, pair, pair),
         cost_estimate=pl.CostEstimate(
             flops=30 * length * length * width, transcendentals=3 * length * length * heads,
             bytes_accessed=36 * length * width),
-    )(mask_row, q, k, v, kv_prev, kv_prev, kv_next, kv_next, grad, lse, delta.T.reshape(lse.shape))
+    )(mask_row, q, k, v, kv_prev, kv_prev, kv_next, kv_next, grad_tiles, attended, gain, norm, lse)
 
 
 def per_device(queries, key_rows, value_rows, view_mask, norm_gain, normed_grad):
@@ -277,7 +284,6 @@
     from_next = passed_along(both, "ctx", -1)
     mask_row = lax.dynamic_slice_in_dim(view_mask, position, 1, 0)[0]
     attended, log_total = attend_forward(mask_row, queries, key_rows, value_rows, from_prev, from_next)
-    out_heads = split_heads(attended)
 
     values_f = attended.astype(jnp.float32)
     upstream = grad_tiles.astype(jnp.float32) * gain_local
@@ -289,14 +295,10 @@
     inner_mean = totals[:, 1:2] / features
     normed_heads = (values_f * inverse * gain_local).astype(jnp.bfloat16)
     normed = heads_to_tiles(normed_heads, normed_grad.shape[0])
-    attended_grad = (
-        inverse * upstream - values_f * inverse * inverse * inverse * inner_mean
-    ).astype(jnp.bfloat16)
-
-    grad_heads = split_heads(attended_grad)
-    delta = jnp.sum(grad_heads.astype(jnp.float32) * out_heads.astype(jnp.float32), -1)
+    norm = jnp.concatenate([inverse, inner_mean], axis=1)
     query_grad, to_prev, to_next, own = attend_backward(
-        mask_row, queries, key_rows, value_rows, from_prev, from_next, attended_grad, log_total, delta)
+        mask_row, queries, key_rows, value_rows, from_prev, from_next, grad_tiles, attended,
+        gain_local[None, :], norm, log_total)
     total = own + passed_along(to_prev, "ctx", -1).astype(jnp.float32)
     total = total + passed_along(to_next, "ctx", 1).astype(jnp.float32)
     total = total.astype(jnp.bfloat16)

time: 55.8 us -> 55.6 us (level)
  other arithmetic: 3.31 us -> 2.2 us
  Pallas kernels: 7.26 us -> 8.01 us
  starting transfers between devices: 21.7 us -> 22.4 us
  waiting for transfers between devices: 16 us -> 15.3 us
    ppermute x4, starting transfers between devices: 9.29 us -> 10.9 us  [passed_along(): return lax.ppermute(x, axis, pairs)]
    ppermute x2, starting transfers between devices: 2.89 us -> 1.51 us  [tp_sum(): lax.ppermute(total, 'tp', [(i, i ^ 1 << b) for i in range(peers)])]
    ppermute x2, waiting for transfers between devices: 5.27 us -> 6.64 us  [tp_sum(): lax.ppermute(total, 'tp', [(i, i ^ 1 << b) for i in range(peers)])]
    ppermute x3, waiting for transfers between devices: 4.47 us -> 3.14 us  [heads_to_tiles(): chunk = lax.ppermute(chunk, 'tp', [(i, (i + shift) % n) for i in range(n)])]
    ppermute x3, waiting for transfers between devices: 4.8 us -> 3.65 us  [tiles_to_heads(): chunk = lax.ppermute(chunk, 'tp', [(i, (i + shift) % n) for i in range(n)])]
    unnamed x2 -> x1, other arithmetic: 1.29 us -> 0.32 us
    pallas_call x1, Pallas kernels: 3.78 us -> 4.52 us  [attend_backward(): pl.pallas_call(functools.partial(_backward_kernel, heads=group, scale=HSZ...]
    concatenate x0 -> x1, local copies, waits for them, and re-layouts: none -> 0.74 us  [per_device(): norm = jnp.concatenate([inverse, inner_mean], axis=1)]
  transfers between devices with their start and end apart: 12 -> 12, of which waited for: 10 -> 8; matrix products, arithmetic and copies ran while one was open for 5% -> 5% of each run, Pallas kernels for 0% -> 0%
where the time goes in v8:
time: 55.6 us; the launch traced here: 55.3 us
  starting transfers between devices  22.4 us (40%)
  waiting for transfers between devices  15.3 us (28%)
  Pallas kernels  8.01 us (14%)
  local copies, waits for them, and re-layouts  6.47 us (12%)
  other arithmetic  2.2 us (4%)
  between operations  0.92 us (2%)
    ppermute x4, starting transfers between devices, passed_along(): return lax.ppermute(x, axis, pairs)  10.9 us
    ppermute x2, waiting for transfers between devices, tp_sum(): lax.ppermute(total, 'tp', [(i, i ^ 1 << b) for i in range(peers)])  6.64 us
    ppermute x3, starting transfers between devices, heads_to_tiles(): chunk = lax.ppermute(chunk, 'tp', [(i, (i + shift) % n) for i in range(n)])  5.27 us
    ppermute x3, starting transfers between devices, tiles_to_heads(): chunk = lax.ppermute(chunk, 'tp', [(i, (i + shift) % n) for i in range(n)])  4.67 us
    pallas_call x1, Pallas kernels, attend_backward(): pl.pallas_call(functools.partial(_backward_kernel, heads=group, scale=HSZ...  4.52 us
    ppermute x3, waiting for transfers between devices, tiles_to_heads(): chunk = lax.ppermute(chunk, 'tp', [(i, (i + shift) % n) for i in range(n)])  3.65 us
    pallas_call x1, Pallas kernels, attend_forward(): pl.pallas_call(functools.partial(_forward_kernel, heads=group, scale=HSZ...  3.49 us
    ppermute x3, waiting for transfers between devices, heads_to_tiles(): chunk = lax.ppermute(chunk, 'tp', [(i, (i + shift) % n) for i in range(n)])  3.14 us
  transfers between devices with their start and end apart: 12, of which 8 were waited for; matrix products, arithmetic and copies ran while one was open for 5% of the time, Pallas kernels for 0%

profile of v8, /device:TPU:4, one launch (start us, length us, event | category | flops | bytes accessed | tf_op | source)
XLA Modules:
  0.0 55.3 jit_solution(8760116180028854907)
XLA Ops:
  0.7 1.0 %constant_dynamic-update-slice_fusion.1 = bf16[128,2048]{1,0:T(8,128)(2,1)S(1)} fusion(bf16[128,1024]{1,0:T(8,128)(2,1)} %k_ref.3), kind=kLoop, calls=%fused_computation.51 | loop fusion | bytes 524288
  1.7 2.1 %collective-permute-start = (bf16[128,2048]{1,0:T(8,128)(2,1)S(1)}, bf16[128,2048]{1,0:T(8,128)(2,1)S(1)}, u32[]{:S(2)}, u32[]{:S(2)}) collective-permute-start(bf16[128,2048]{1,0:T(8,128)(2,1)S(1)} %constant_dynamic-update-slice_fusion), channel_id=1, source_target_pairs={{0,4},{4,8},{8,12},{12,16},{16,20},{20,24},{24,28},{1,5},{5,9},{9,... | collective-permute-start | bytes 1572872 | tf_op jit(solution)/shard_map/ppermute | solution.py:25
  3.8 4.5 %collective-permute-start.1 = (bf16[128,2048]{1,0:T(8,128)(2,1)S(1)}, bf16[128,2048]{1,0:T(8,128)(2,1)S(1)}, u32[]{:S(2)}, u32[]{:S(2)}) collective-permute-start(bf16[128,2048]{1,0:T(8,128)(2,1)S(1)} %constant_dynamic-update-slice_fusion), channel_id=1, source_target_pairs={{4,0},{8,4},{12,8},{16,12},{20,16},{24,20},{28,24},{5,1},{9,5},{13... | collective-permute-start | bytes 1572872 | tf_op jit(solution)/shard_map/ppermute | solution.py:25
  8.4 3.7 %collective-permute-start.2 = (bf16[32,1024]{1,0:T(8,128)(2,1)S(1)}, bf16[32,1024]{1,0:T(8,128)(2,1)S(1)}, u32[]{:S(2)}, u32[]{:S(2)}) collective-permute-start(bf16[32,1024]{1,0:T(8,128)(2,1)S(1)} %get-tuple-element.26), channel_id=1, source_target_pairs={{0,3},{1,0},{2,1},{3,2},{4,7},{5,4},{6,5},{7,6},{8,11},{9,8},{10,9... | collective-permute-start | bytes 196616 | tf_op jit(solution)/shard_map/ppermute | solution.py:96
  12.1 1.0 %collective-permute-start.4 = (bf16[32,1024]{1,0:T(8,128)(2,1)S(1)}, bf16[32,1024]{1,0:T(8,128)(2,1)S(1)}, u32[]{:S(2)}, u32[]{:S(2)}) collective-permute-start(bf16[32,1024]{1,0:T(8,128)(2,1)S(1)} %get-tuple-element.25), channel_id=1, source_target_pairs={{0,1},{1,2},{2,3},{3,0},{4,5},{5,6},{6,7},{7,4},{8,9},{9,10},{10,1... | collective-permute-start | bytes 196616 | tf_op jit(solution)/shard_map/ppermute | solution.py:96
  14.5 2.7 %collective-permute-done.3 = bf16[32,1024]{1,0:T(8,128)(2,1)S(1)} collective-permute-done((bf16[32,1024]{1,0:T(8,128)(2,1)S(1)}, bf16[32,1024]{1,0:T(8,128)(2,1)S(1)}, u32[]{:S(2)}, u32[]{:S(2)}) %collective-permute-start.3) | collective-permute-done | bytes 65568 | tf_op jit(solution)/shard_map/ppermute | solution.py:96
  17.3 0.9 %collective-permute-done.4 = bf16[32,1024]{1,0:T(8,128)(2,1)S(1)} collective-permute-done((bf16[32,1024]{1,0:T(8,128)(2,1)S(1)}, bf16[32,1024]{1,0:T(8,128)(2,1)S(1)}, u32[]{:S(2)}, u32[]{:S(2)}) %collective-permute-start.4) | collective-permute-done | bytes 65568 | tf_op jit(solution)/shard_map/ppermute | solution.py:96
  18.5 0.8 %copy-done.1 = bf16[128,2048]{1,0:T(8,128)(2,1)} copy-done((bf16[128,2048]{1,0:T(8,128)(2,1)}, bf16[128,2048]{1,0:T(8,128)(2,1)S(1)}, u32[]{:S(2)}) %copy-start.1) | copy-done | bytes 524312
  19.4 0.8 %copy-done.2 = bf16[128,2048]{1,0:T(8,128)(2,1)} copy-done((bf16[128,2048]{1,0:T(8,128)(2,1)}, bf16[128,2048]{1,0:T(8,128)(2,1)S(1)}, u32[]{:S(2)}) %copy-start.2) | copy-done | bytes 524312
  20.2 3.5 %shard_map.93 = (bf16[128,1024]{1,0:T(8,128)(2,1)}, f32[2,4,128]{2,1,0:T(4,128)}) custom-call(s32[3]{0:T(128)} %fusion.19.mask_ref, bf16[128,1024]{1,0:T(8,128)(2,1)} %q_ref.3, bf16[128,1024]{1,0:T(8,128)(2,1)} %k_ref.3, bf16[128,1024]{1,0:T(8,128)(2,1)} %v_ref.3, bf16[128,2048]{1,0:T(8,128)(2,1)} %copy-done.1, bf16[128,2048]{1,0:T(8,128)(2,1)} %copy-done.1, ...), custom_call_target="tpu_custom_call" | custom-call | flops 201326592 | bytes 2097152 | tf_op jit(solution)/shard_map/pallas_call | solution.py:195
  23.7 1.2 %fusion = (f32[128]{0:T(128)S(1)}, f32[128]{0:T(128)S(1)}) fusion(bf16[128,1024]{1,0:T(8,128)(2,1)} %get-tuple-element.11.o_ref, f32[1024]{0:T(1024)S(1)} %dynamic_slice.38, bf16[4,32,1024]{2,1,0:T(8,128)(2,1)S(1)} %fusion.15), kind=kLoop, calls=%fused_computation.4 | loop fusion | flops 917248 | bytes 529408 | tf_op jit(solution)/shard_map/reduce_sum | solution.py:291
  24.9 3.6 %collective-permute-done.5 = f32[128,2]{0,1:T(2,128)S(1)} collective-permute-done((f32[128,2]{0,1:T(2,128)S(1)}, f32[128,2]{0,1:T(2,128)S(1)}, u32[]{:S(2)}, u32[]{:S(2)}) %collective-permute-start.5) | collective-permute-done | bytes 1056 | tf_op jit(solution)/shard_map/ppermute | solution.py:64
  28.5 1.4 %collective-permute-start.6 = (f32[128,2]{0,1:T(2,128)S(1)}, f32[128,2]{0,1:T(2,128)S(1)}, u32[]{:S(2)}, u32[]{:S(2)}) collective-permute-start(f32[128,2]{0,1:T(2,128)S(1)} %fusion.20), channel_id=1, source_target_pairs={{0,2},{1,3},{2,0},{3,1},{4,6},{5,7},{6,4},{7,5},{8,10},{9,11},{10,... | collective-permute-start | bytes 3080 | tf_op jit(solution)/shard_map/ppermute | solution.py:64
  29.9 3.1 %collective-permute-done.6 = f32[128,2]{0,1:T(2,128)S(1)} collective-permute-done((f32[128,2]{0,1:T(2,128)S(1)}, f32[128,2]{0,1:T(2,128)S(1)}, u32[]{:S(2)}, u32[]{:S(2)}) %collective-permute-start.6) | collective-permute-done | bytes 1056 | tf_op jit(solution)/shard_map/ppermute | solution.py:64
  33.8 4.5 %shard_map.94 = (bf16[128,1024]{1,0:T(8,128)(2,1)}, bf16[2,128,1024]{2,1,0:T(8,128)(2,1)}, bf16[2,128,1024]{2,1,0:T(8,128)(2,1)}, f32[2,128,1024]{2,1,0:T(8,128)}) custom-call(s32[3]{0:T(128)} %fusion.19.mask_ref, bf16[128,1024]{1,0:T(8,128)(2,1)} %q_ref.3, bf16[128,1024]{1,0:T(8,128)(2,1)} %k_ref.3, bf16[128,1024]{1,0:T(8,128)(2,1)} %v_ref.3, ...), custom_call_target="tpu_custom_call" | custom-call | flops 503316480 | bytes 4718592 | tf_op jit(solution)/shard_map/pallas_call | solution.py:257
  38.3 1.9 %collective-permute-start.10 = (bf16[2,128,1024]{2,1,0:T(8,128)(2,1)}, bf16[2,128,1024]{2,1,0:T(8,128)(2,1)S(1)}, u32[]{:S(2)}, u32[]{:S(2)}) collective-permute-start(bf16[2,128,1024]{2,1,0:T(8,128)(2,1)} %get-tuple-element.15), channel_id=1, source_target_pairs={{4,0},{8,4},{12,8},{16,12},{20,16},{24,20},{28,24},{5,1},{9,5},{13... | collective-permute-start | bytes 1572872 | tf_op jit(solution)/shard_map/ppermute | solution.py:25
  40.3 2.4 %collective-permute-start.11 = (bf16[2,128,1024]{2,1,0:T(8,128)(2,1)}, bf16[2,128,1024]{2,1,0:T(8,128)(2,1)S(1)}, u32[]{:S(2)}, u32[]{:S(2)}) collective-permute-start(bf16[2,128,1024]{2,1,0:T(8,128)(2,1)} %get-tuple-element.16), channel_id=1, source_target_pairs={{0,4},{4,8},{8,12},{12,16},{16,20},{20,24},{24,28},{1,5},{5,9},{9,... | collective-permute-start | bytes 1572872 | tf_op jit(solution)/shard_map/ppermute | solution.py:25
  42.9 1.4 %collective-permute-start.8 = (bf16[32,1024]{1,0:T(8,128)(2,1)S(1)}, bf16[32,1024]{1,0:T(8,128)(2,1)S(1)}, u32[]{:S(2)}, u32[]{:S(2)}) collective-permute-start(bf16[32,1024]{1,0:T(8,128)(2,1)S(1)} %get-tuple-element.22), channel_id=1, source_target_pairs={{0,2},{1,3},{2,0},{3,1},{4,6},{5,7},{6,4},{7,5},{8,10},{9,11},{10,... | collective-permute-start | bytes 196616 | tf_op jit(solution)/shard_map/ppermute | solution.py:115
  44.3 0.8 %collective-permute-start.9 = (bf16[32,1024]{1,0:T(8,128)(2,1)S(1)}, bf16[32,1024]{1,0:T(8,128)(2,1)S(1)}, u32[]{:S(2)}, u32[]{:S(2)}) collective-permute-start(bf16[32,1024]{1,0:T(8,128)(2,1)S(1)} %get-tuple-element.21), channel_id=1, source_target_pairs={{0,1},{1,2},{2,3},{3,0},{4,5},{5,6},{6,7},{7,4},{8,9},{9,10},{10,1... | collective-permute-start | bytes 196616 | tf_op jit(solution)/shard_map/ppermute | solution.py:115
  45.1 3.1 %collective-permute-start.7 = (bf16[32,1024]{1,0:T(8,128)(2,1)S(1)}, bf16[32,1024]{1,0:T(8,128)(2,1)S(1)}, u32[]{:S(2)}, u32[]{:S(2)}) collective-permute-start(bf16[32,1024]{1,0:T(8,128)(2,1)S(1)} %get-tuple-element.23), channel_id=1, source_target_pairs={{0,3},{1,0},{2,1},{3,2},{4,7},{5,4},{6,5},{7,6},{8,11},{9,8},{10,9... | collective-permute-start | bytes 196616 | tf_op jit(solution)/shard_map/ppermute | solution.py:115
  48.2 1.6 %collective-permute-done.8 = bf16[32,1024]{1,0:T(8,128)(2,1)S(1)} collective-permute-done((bf16[32,1024]{1,0:T(8,128)(2,1)S(1)}, bf16[32,1024]{1,0:T(8,128)(2,1)S(1)}, u32[]{:S(2)}, u32[]{:S(2)}) %collective-permute-start.8) | collective-permute-done | bytes 65568 | tf_op jit(solution)/shard_map/ppermute | solution.py:115
  49.8 0.9 %collective-permute-done.9 = bf16[32,1024]{1,0:T(8,128)(2,1)S(1)} collective-permute-done((bf16[32,1024]{1,0:T(8,128)(2,1)S(1)}, bf16[32,1024]{1,0:T(8,128)(2,1)S(1)}, u32[]{:S(2)}, u32[]{:S(2)}) %collective-permute-start.9) | collective-permute-done | bytes 65568 | tf_op jit(solution)/shard_map/ppermute | solution.py:115
  52.3 1.9 %collective-permute-done.11 = bf16[2,128,1024]{2,1,0:T(8,128)(2,1)S(1)} collective-permute-done((bf16[2,128,1024]{2,1,0:T(8,128)(2,1)}, bf16[2,128,1024]{2,1,0:T(8,128)(2,1)S(1)}, u32[]{:S(2)}, u32[]{:S(2)}) %collective-permute-start.11) | collective-permute-done | bytes 524320 | tf_op jit(solution)/shard_map/ppermute | solution.py:25
  54.5 0.8 %slice_bitcast_fusion = (bf16[128,1024]{1,0:T(8,128)(2,1)}, bf16[128,1024]{1,0:T(8,128)(2,1)}) fusion(bf16[2,128,1024]{2,1,0:T(8,128)(2,1)S(1)} %add_convert_fusion), kind=kLoop, calls=%fused_computation.39 | loop fusion | bytes 1048576 | tf_op jit(solution)/shard_map/squeeze | solution.py:305
  (41 shorter events, 4.8 us)
Async XLA Ops:
  0.6 13.2 %copy-start = (s32[8,3]{0,1:T(4,128)S(1)}, s32[8,3]{0,1:T(4,128)}, u32[]{:S(2)}) copy-start(s32[8,3]{0,1:T(4,128)} %param.11) | copy-start | bytes 292
  0.6 1.0 %copy-start.3 = (bf16[128,1024]{1,0:T(8,128)(2,1)S(1)}, bf16[128,1024]{1,0:T(8,128)(2,1)}, u32[]{:S(2)}) copy-start(bf16[128,1024]{1,0:T(8,128)(2,1)} %v_ref.3) | copy-start | bytes 786436
  1.7 6.7 %copy-start.7 = (bf16[32,4096]{1,0:T(8,128)(2,1)S(1)}, bf16[32,4096]{1,0:T(8,128)(2,1)}, u32[]{:S(2)}) copy-start(bf16[32,4096]{1,0:T(8,128)(2,1)} %param.13) | copy-start | bytes 786436
  1.7 16.8 %collective-permute-start = (bf16[128,2048]{1,0:T(8,128)(2,1)S(1)}, bf16[128,2048]{1,0:T(8,128)(2,1)S(1)}, u32[]{:S(2)}, u32[]{:S(2)}) collective-permute-start(bf16[128,2048]{1,0:T(8,128)(2,1)S(1)} %constant_dynamic-update-slice_fusion), channel_id=1, source_target_pairs={{0,4},{4,8},{8,12},{12,16},{16,20},{20,24},{24,28},{1,5},{5,9},{9,... | collective-permute-start | bytes 1572872 | tf_op jit(solution)/shard_map/ppermute | solution.py:25
  3.8 14.7 %collective-permute-start.1 = (bf16[128,2048]{1,0:T(8,128)(2,1)S(1)}, bf16[128,2048]{1,0:T(8,128)(2,1)S(1)}, u32[]{:S(2)}, u32[]{:S(2)}) collective-permute-start(bf16[128,2048]{1,0:T(8,128)(2,1)S(1)} %constant_dynamic-update-slice_fusion), channel_id=1, source_target_pairs={{4,0},{8,4},{12,8},{16,12},{20,16},{24,20},{28,24},{5,1},{9,5},{13... | collective-permute-start | bytes 1572872 | tf_op jit(solution)/shard_map/ppermute | solution.py:25
  8.4 6.1 %collective-permute-start.2 = (bf16[32,1024]{1,0:T(8,128)(2,1)S(1)}, bf16[32,1024]{1,0:T(8,128)(2,1)S(1)}, u32[]{:S(2)}, u32[]{:S(2)}) collective-permute-start(bf16[32,1024]{1,0:T(8,128)(2,1)S(1)} %get-tuple-element.26), channel_id=1, source_target_pairs={{0,3},{1,0},{2,1},{3,2},{4,7},{5,4},{6,5},{7,6},{8,11},{9,8},{10,9... | collective-permute-start | bytes 196616 | tf_op jit(solution)/shard_map/ppermute | solution.py:96
  12.1 5.2 %collective-permute-start.3 = (bf16[32,1024]{1,0:T(8,128)(2,1)S(1)}, bf16[32,1024]{1,0:T(8,128)(2,1)S(1)}, u32[]{:S(2)}, u32[]{:S(2)}) collective-permute-start(bf16[32,1024]{1,0:T(8,128)(2,1)S(1)} %get-tuple-element.28), channel_id=1, source_target_pairs={{0,2},{1,3},{2,0},{3,1},{4,6},{5,7},{6,4},{7,5},{8,10},{9,11},{10,... | collective-permute-start | bytes 196616 | tf_op jit(solution)/shard_map/ppermute | solution.py:96
  12.1 6.1 %collective-permute-start.4 = (bf16[32,1024]{1,0:T(8,128)(2,1)S(1)}, bf16[32,1024]{1,0:T(8,128)(2,1)S(1)}, u32[]{:S(2)}, u32[]{:S(2)}) collective-permute-start(bf16[32,1024]{1,0:T(8,128)(2,1)S(1)} %get-tuple-element.25), channel_id=1, source_target_pairs={{0,1},{1,2},{2,3},{3,0},{4,5},{5,6},{6,7},{7,4},{8,9},{9,10},{10,1... | collective-permute-start | bytes 196616 | tf_op jit(solution)/shard_map/ppermute | solution.py:96
  13.8 9.9 %copy-start.8 = (f32[1024]{0:T(1024)}, f32[1024]{0:T(1024)S(1)}, u32[]{:S(2)}) copy-start(f32[1024]{0:T(1024)S(1)} %dynamic_slice.38) | copy-start | bytes 12292
  18.5 5.2 %copy-start.4 = (bf16[4,32,1024]{2,1,0:T(8,128)(2,1)}, bf16[4,32,1024]{2,1,0:T(8,128)(2,1)S(1)}, u32[]{:S(2)}) copy-start(bf16[4,32,1024]{2,1,0:T(8,128)(2,1)S(1)} %fusion.15) | copy-start | bytes 786436
  18.5 0.9 %copy-start.1 = (bf16[128,2048]{1,0:T(8,128)(2,1)}, bf16[128,2048]{1,0:T(8,128)(2,1)S(1)}, u32[]{:S(2)}) copy-start(bf16[128,2048]{1,0:T(8,128)(2,1)S(1)} %collective-permute-done.kp_ref.vp_ref) | copy-start | bytes 1572868
  19.4 0.8 %copy-start.2 = (bf16[128,2048]{1,0:T(8,128)(2,1)}, bf16[128,2048]{1,0:T(8,128)(2,1)S(1)}, u32[]{:S(2)}) copy-start(bf16[128,2048]{1,0:T(8,128)(2,1)S(1)} %collective-permute-done.1.kn_ref.vn_ref) | copy-start | bytes 1572868
  24.8 3.6 %collective-permute-start.5 = (f32[128,2]{0,1:T(2,128)S(1)}, f32[128,2]{0,1:T(2,128)S(1)}, u32[]{:S(2)}, u32[]{:S(2)}) collective-permute-start(f32[128,2]{0,1:T(2,128)S(1)} %pad_maximum_fusion), channel_id=1, source_target_pairs={{0,1},{1,0},{2,3},{3,2},{4,5},{5,4},{6,7},{7,6},{8,9},{9,8},{10,11... | collective-permute-start | bytes 3080 | tf_op jit(solution)/shard_map/ppermute | solution.py:64
  28.5 4.5 %collective-permute-start.6 = (f32[128,2]{0,1:T(2,128)S(1)}, f32[128,2]{0,1:T(2,128)S(1)}, u32[]{:S(2)}, u32[]{:S(2)}) collective-permute-start(f32[128,2]{0,1:T(2,128)S(1)} %fusion.20), channel_id=1, source_target_pairs={{0,2},{1,3},{2,0},{3,1},{4,6},{5,7},{6,4},{7,5},{8,10},{9,11},{10,... | collective-permute-start | bytes 3080 | tf_op jit(solution)/shard_map/ppermute | solution.py:64
  33.8 8.9 %copy-start.5 = (bf16[128,1024]{1,0:T(8,128)(2,1)S(1)}, bf16[128,1024]{1,0:T(8,128)(2,1)}, u32[]{:S(2)}) copy-start(bf16[128,1024]{1,0:T(8,128)(2,1)} %get-tuple-element.11.o_ref) | copy-start | bytes 786436
  38.3 4.4 %copy-start.9 = (f32[1024]{0:T(1024)S(1)}, f32[1024]{0:T(1024)}, u32[]{:S(2)}) copy-start(f32[1024]{0:T(1024)} %copy-done.8) | copy-start | bytes 12292
  38.3 14.0 %collective-permute-start.10 = (bf16[2,128,1024]{2,1,0:T(8,128)(2,1)}, bf16[2,128,1024]{2,1,0:T(8,128)(2,1)S(1)}, u32[]{:S(2)}, u32[]{:S(2)}) collective-permute-start(bf16[2,128,1024]{2,1,0:T(8,128)(2,1)} %get-tuple-element.15), channel_id=1, source_target_pairs={{4,0},{8,4},{12,8},{16,12},{20,16},{24,20},{28,24},{5,1},{9,5},{13... | collective-permute-start | bytes 1572872 | tf_op jit(solution)/shard_map/ppermute | solution.py:25
  40.3 13.9 %collective-permute-start.11 = (bf16[2,128,1024]{2,1,0:T(8,128)(2,1)}, bf16[2,128,1024]{2,1,0:T(8,128)(2,1)S(1)}, u32[]{:S(2)}, u32[]{:S(2)}) collective-permute-start(bf16[2,128,1024]{2,1,0:T(8,128)(2,1)} %get-tuple-element.16), channel_id=1, source_target_pairs={{0,4},{4,8},{8,12},{12,16},{16,20},{20,24},{24,28},{1,5},{5,9},{9,... | collective-permute-start | bytes 1572872 | tf_op jit(solution)/shard_map/ppermute | solution.py:25
  42.7 11.5 %copy-start.6 = (f32[2,128,1024]{2,1,0:T(8,128)S(1)}, f32[2,128,1024]{2,1,0:T(8,128)}, u32[]{:S(2)}) copy-start(f32[2,128,1024]{2,1,0:T(8,128)} %get-tuple-element.14) | copy-start | bytes 3145732
  42.9 6.9 %collective-permute-start.8 = (bf16[32,1024]{1,0:T(8,128)(2,1)S(1)}, bf16[32,1024]{1,0:T(8,128)(2,1)S(1)}, u32[]{:S(2)}, u32[]{:S(2)}) collective-permute-start(bf16[32,1024]{1,0:T(8,128)(2,1)S(1)} %get-tuple-element.22), channel_id=1, source_target_pairs={{0,2},{1,3},{2,0},{3,1},{4,6},{5,7},{6,4},{7,5},{8,10},{9,11},{10,... | collective-permute-start | bytes 196616 | tf_op jit(solution)/shard_map/ppermute | solution.py:115
  44.3 6.3 %collective-permute-start.9 = (bf16[32,1024]{1,0:T(8,128)(2,1)S(1)}, bf16[32,1024]{1,0:T(8,128)(2,1)S(1)}, u32[]{:S(2)}, u32[]{:S(2)}) collective-permute-start(bf16[32,1024]{1,0:T(8,128)(2,1)S(1)} %get-tuple-element.21), channel_id=1, source_target_pairs={{0,1},{1,2},{2,3},{3,0},{4,5},{5,6},{6,7},{7,4},{8,9},{9,10},{10,1... | collective-permute-start | bytes 196616 | tf_op jit(solution)/shard_map/ppermute | solution.py:115
  45.1 6.2 %collective-permute-start.7 = (bf16[32,1024]{1,0:T(8,128)(2,1)S(1)}, bf16[32,1024]{1,0:T(8,128)(2,1)S(1)}, u32[]{:S(2)}, u32[]{:S(2)}) collective-permute-start(bf16[32,1024]{1,0:T(8,128)(2,1)S(1)} %get-tuple-element.23), channel_id=1, source_target_pairs={{0,3},{1,0},{2,1},{3,2},{4,7},{5,4},{6,5},{7,6},{8,11},{9,8},{10,9... | collective-permute-start | bytes 196616 | tf_op jit(solution)/shard_map/ppermute | solution.py:115

commit v9 on v8

--- a/solution.py
+++ b/solution.py
@@ -14,7 +14,7 @@
 NEGATIVE = -1e30
 EPSILON = 1e-06
 LOOKAHEAD = 3
-STATS_SUM = "xor"
+STATS_SUM = "perm"
 NG_MODE = "perm"
 OUT_MODE = "perm"
 

time: 55.6 us -> 53.9 us (0.969)
  waiting for transfers between devices: 15.3 us -> 10.6 us
  starting transfers between devices: 22.4 us -> 25 us
    ppermute x2 -> x3, waiting for transfers between devices: 6.64 us -> 1.64 us  [tp_sum(): lax.ppermute(stats, 'tp', [(i, (i + shift) % peers) for i in range(peers)])]
    ppermute x2 -> x3, starting transfers between devices: 1.51 us -> 4.33 us  [tp_sum(): lax.ppermute(stats, 'tp', [(i, (i + shift) % peers) for i in range(peers)])]
    ppermute x3, waiting for transfers between devices: 3.14 us -> 4.12 us  [heads_to_tiles(): chunk = lax.ppermute(chunk, 'tp', [(i, (i + shift) % n) for i in range(n)])]
    ppermute x4, waiting for transfers between devices: 1.87 us -> 1.15 us  [passed_along(): return lax.ppermute(x, axis, pairs)]
  transfers between devices with their start and end apart: 12 -> 13, of which waited for: 8 -> 8; matrix products, arithmetic and copies ran while one was open for 5% -> 5% of each run, Pallas kernels for 0% -> 0%
where the time goes in v9:
time: 53.9 us; the launch traced here: 53.2 us
  starting transfers between devices  25 us (46%)
  waiting for transfers between devices  10.6 us (20%)
  Pallas kernels  8.01 us (15%)
  local copies, waits for them, and re-layouts  6.43 us (12%)
  other arithmetic  2.2 us (4%)
  between operations  0.92 us (2%)
    ppermute x4, starting transfers between devices, passed_along(): return lax.ppermute(x, axis, pairs)  11.2 us
    ppermute x3, starting transfers between devices, heads_to_tiles(): chunk = lax.ppermute(chunk, 'tp', [(i, (i + shift) % n) for i in range(n)])  4.81 us
    ppermute x3, starting transfers between devices, tiles_to_heads(): chunk = lax.ppermute(chunk, 'tp', [(i, (i + shift) % n) for i in range(n)])  4.67 us
    pallas_call x1, Pallas kernels, attend_backward(): pl.pallas_call(functools.partial(_backward_kernel, heads=group, scale=HSZ...  4.52 us
    ppermute x3, starting transfers between devices, tp_sum(): lax.ppermute(stats, 'tp', [(i, (i + shift) % peers) for i in range(peers)])  4.33 us
    ppermute x3, waiting for transfers between devices, heads_to_tiles(): chunk = lax.ppermute(chunk, 'tp', [(i, (i + shift) % n) for i in range(n)])  4.12 us
    ppermute x3, waiting for transfers between devices, tiles_to_heads(): chunk = lax.ppermute(chunk, 'tp', [(i, (i + shift) % n) for i in range(n)])  3.67 us
    pallas_call x1, Pallas kernels, attend_forward(): pl.pallas_call(functools.partial(_forward_kernel, heads=group, scale=HSZ...  3.49 us
  transfers between devices with their start and end apart: 13, of which 8 were waited for; matrix products, arithmetic and copies ran while one was open for 5% of the time, Pallas kernels for 0%

profile of v9, /device:TPU:4, one launch (start us, length us, event | category | flops | bytes accessed | tf_op | source)
XLA Modules:
  0.0 53.2 jit_solution(5624121852703471947)
XLA Ops:
  0.7 1.0 %constant_dynamic-update-slice_fusion.1 = bf16[128,2048]{1,0:T(8,128)(2,1)S(1)} fusion(bf16[128,1024]{1,0:T(8,128)(2,1)} %k_ref.3), kind=kLoop, calls=%fused_computation.51 | loop fusion | bytes 524288
  1.7 2.1 %collective-permute-start = (bf16[128,2048]{1,0:T(8,128)(2,1)S(1)}, bf16[128,2048]{1,0:T(8,128)(2,1)S(1)}, u32[]{:S(2)}, u32[]{:S(2)}) collective-permute-start(bf16[128,2048]{1,0:T(8,128)(2,1)S(1)} %constant_dynamic-update-slice_fusion), channel_id=1, source_target_pairs={{0,4},{4,8},{8,12},{12,16},{16,20},{20,24},{24,28},{1,5},{5,9},{9,... | collective-permute-start | bytes 1572872 | tf_op jit(solution)/shard_map/ppermute | solution.py:25
  3.8 4.5 %collective-permute-start.1 = (bf16[128,2048]{1,0:T(8,128)(2,1)S(1)}, bf16[128,2048]{1,0:T(8,128)(2,1)S(1)}, u32[]{:S(2)}, u32[]{:S(2)}) collective-permute-start(bf16[128,2048]{1,0:T(8,128)(2,1)S(1)} %constant_dynamic-update-slice_fusion), channel_id=1, source_target_pairs={{4,0},{8,4},{12,8},{16,12},{20,16},{24,20},{28,24},{5,1},{9,5},{13... | collective-permute-start | bytes 1572872 | tf_op jit(solution)/shard_map/ppermute | solution.py:25
  8.4 3.7 %collective-permute-start.2 = (bf16[32,1024]{1,0:T(8,128)(2,1)S(1)}, bf16[32,1024]{1,0:T(8,128)(2,1)S(1)}, u32[]{:S(2)}, u32[]{:S(2)}) collective-permute-start(bf16[32,1024]{1,0:T(8,128)(2,1)S(1)} %get-tuple-element.26), channel_id=1, source_target_pairs={{0,3},{1,0},{2,1},{3,2},{4,7},{5,4},{6,5},{7,6},{8,11},{9,8},{10,9... | collective-permute-start | bytes 196616 | tf_op jit(solution)/shard_map/ppermute | solution.py:96
  12.1 1.0 %collective-permute-start.4 = (bf16[32,1024]{1,0:T(8,128)(2,1)S(1)}, bf16[32,1024]{1,0:T(8,128)(2,1)S(1)}, u32[]{:S(2)}, u32[]{:S(2)}) collective-permute-start(bf16[32,1024]{1,0:T(8,128)(2,1)S(1)} %get-tuple-element.25), channel_id=1, source_target_pairs={{0,1},{1,2},{2,3},{3,0},{4,5},{5,6},{6,7},{7,4},{8,9},{9,10},{10,1... | collective-permute-start | bytes 196616 | tf_op jit(solution)/shard_map/ppermute | solution.py:96
  14.5 2.8 %collective-permute-done.3 = bf16[32,1024]{1,0:T(8,128)(2,1)S(1)} collective-permute-done((bf16[32,1024]{1,0:T(8,128)(2,1)S(1)}, bf16[32,1024]{1,0:T(8,128)(2,1)S(1)}, u32[]{:S(2)}, u32[]{:S(2)}) %collective-permute-start.3) | collective-permute-done | bytes 65568 | tf_op jit(solution)/shard_map/ppermute | solution.py:96
  17.3 0.9 %collective-permute-done.4 = bf16[32,1024]{1,0:T(8,128)(2,1)S(1)} collective-permute-done((bf16[32,1024]{1,0:T(8,128)(2,1)S(1)}, bf16[32,1024]{1,0:T(8,128)(2,1)S(1)}, u32[]{:S(2)}, u32[]{:S(2)}) %collective-permute-start.4) | collective-permute-done | bytes 65568 | tf_op jit(solution)/shard_map/ppermute | solution.py:96
  18.5 0.8 %copy-done.1 = bf16[128,2048]{1,0:T(8,128)(2,1)} copy-done((bf16[128,2048]{1,0:T(8,128)(2,1)}, bf16[128,2048]{1,0:T(8,128)(2,1)S(1)}, u32[]{:S(2)}) %copy-start.1) | copy-done | bytes 524312
  19.4 0.8 %copy-done.2 = bf16[128,2048]{1,0:T(8,128)(2,1)} copy-done((bf16[128,2048]{1,0:T(8,128)(2,1)}, bf16[128,2048]{1,0:T(8,128)(2,1)S(1)}, u32[]{:S(2)}) %copy-start.2) | copy-done | bytes 524312
  20.2 3.5 %shard_map.93 = (bf16[128,1024]{1,0:T(8,128)(2,1)}, f32[2,4,128]{2,1,0:T(4,128)}) custom-call(s32[3]{0:T(128)} %fusion.19.mask_ref, bf16[128,1024]{1,0:T(8,128)(2,1)} %q_ref.3, bf16[128,1024]{1,0:T(8,128)(2,1)} %k_ref.3, bf16[128,1024]{1,0:T(8,128)(2,1)} %v_ref.3, bf16[128,2048]{1,0:T(8,128)(2,1)} %copy-done.1, bf16[128,2048]{1,0:T(8,128)(2,1)} %copy-done.1, ...), custom_call_target="tpu_custom_call" | custom-call | flops 201326592 | bytes 2097152 | tf_op jit(solution)/shard_map/pallas_call | solution.py:195
  23.7 1.2 %fusion = (f32[128]{0:T(128)S(1)}, f32[128]{0:T(128)S(1)}) fusion(bf16[128,1024]{1,0:T(8,128)(2,1)} %get-tuple-element.11.o_ref, f32[1024]{0:T(1024)S(1)} %dynamic_slice.38, bf16[4,32,1024]{2,1,0:T(8,128)(2,1)S(1)} %fusion.15), kind=kLoop, calls=%fused_computation.4 | loop fusion | flops 917248 | bytes 529408 | tf_op jit(solution)/shard_map/reduce_sum | solution.py:291
  24.9 2.1 %collective-permute-start.6 = (f32[128,2]{0,1:T(2,128)S(1)}, f32[128,2]{0,1:T(2,128)S(1)}, u32[]{:S(2)}, u32[]{:S(2)}) collective-permute-start(f32[128,2]{0,1:T(2,128)S(1)} %pad_maximum_fusion), channel_id=1, source_target_pairs={{0,2},{1,3},{2,0},{3,1},{4,6},{5,7},{6,4},{7,5},{8,10},{9,11},{10,... | collective-permute-start | bytes 3080 | tf_op jit(solution)/shard_map/ppermute | solution.py:72
  27.0 2.2 %collective-permute-start.7 = (f32[128,2]{0,1:T(2,128)S(1)}, f32[128,2]{0,1:T(2,128)S(1)}, u32[]{:S(2)}, u32[]{:S(2)}) collective-permute-start(f32[128,2]{0,1:T(2,128)S(1)} %pad_maximum_fusion), channel_id=1, source_target_pairs={{0,3},{1,0},{2,1},{3,2},{4,7},{5,4},{6,5},{7,6},{8,11},{9,8},{10,9... | collective-permute-start | bytes 3080 | tf_op jit(solution)/shard_map/ppermute | solution.py:72
  29.2 1.1 %collective-permute-done.5 = f32[128,2]{0,1:T(2,128)S(1)} collective-permute-done((f32[128,2]{0,1:T(2,128)S(1)}, f32[128,2]{0,1:T(2,128)S(1)}, u32[]{:S(2)}, u32[]{:S(2)}) %collective-permute-start.5) | collective-permute-done | bytes 1056 | tf_op jit(solution)/shard_map/ppermute | solution.py:72
  30.9 0.7 %copy.16.norm_ref = f32[128,2]{1,0:T(8,128)} copy(f32[128,2]{0,1:T(2,128)S(1)} %pad_maximum_fusion.1) | data formatting | bytes 2048 | tf_op jit(solution)/shard_map/concatenate | solution.py:298
  31.6 4.5 %shard_map.94 = (bf16[128,1024]{1,0:T(8,128)(2,1)}, bf16[2,128,1024]{2,1,0:T(8,128)(2,1)}, bf16[2,128,1024]{2,1,0:T(8,128)(2,1)}, f32[2,128,1024]{2,1,0:T(8,128)}) custom-call(s32[3]{0:T(128)} %fusion.19.mask_ref, bf16[128,1024]{1,0:T(8,128)(2,1)} %q_ref.3, bf16[128,1024]{1,0:T(8,128)(2,1)} %k_ref.3, bf16[128,1024]{1,0:T(8,128)(2,1)} %v_ref.3, ...), custom_call_target="tpu_custom_call" | custom-call | flops 503316480 | bytes 4718592 | tf_op jit(solution)/shard_map/pallas_call | solution.py:257
  36.1 2.7 %collective-permute-start.11 = (bf16[2,128,1024]{2,1,0:T(8,128)(2,1)}, bf16[2,128,1024]{2,1,0:T(8,128)(2,1)S(1)}, u32[]{:S(2)}, u32[]{:S(2)}) collective-permute-start(bf16[2,128,1024]{2,1,0:T(8,128)(2,1)} %get-tuple-element.15), channel_id=1, source_target_pairs={{4,0},{8,4},{12,8},{16,12},{20,16},{24,20},{28,24},{5,1},{9,5},{13... | collective-permute-start | bytes 1572872 | tf_op jit(solution)/shard_map/ppermute | solution.py:25
  38.8 1.9 %collective-permute-start.12 = (bf16[2,128,1024]{2,1,0:T(8,128)(2,1)}, bf16[2,128,1024]{2,1,0:T(8,128)(2,1)S(1)}, u32[]{:S(2)}, u32[]{:S(2)}) collective-permute-start(bf16[2,128,1024]{2,1,0:T(8,128)(2,1)} %get-tuple-element.16), channel_id=1, source_target_pairs={{0,4},{4,8},{8,12},{12,16},{16,20},{20,24},{24,28},{1,5},{5,9},{9,... | collective-permute-start | bytes 1572872 | tf_op jit(solution)/shard_map/ppermute | solution.py:25
  41.0 1.0 %collective-permute-start.9 = (bf16[32,1024]{1,0:T(8,128)(2,1)S(1)}, bf16[32,1024]{1,0:T(8,128)(2,1)S(1)}, u32[]{:S(2)}, u32[]{:S(2)}) collective-permute-start(bf16[32,1024]{1,0:T(8,128)(2,1)S(1)} %get-tuple-element.22), channel_id=1, source_target_pairs={{0,2},{1,3},{2,0},{3,1},{4,6},{5,7},{6,4},{7,5},{8,10},{9,11},{10,... | collective-permute-start | bytes 196616 | tf_op jit(solution)/shard_map/ppermute | solution.py:115
  42.0 3.1 %collective-permute-start.10 = (bf16[32,1024]{1,0:T(8,128)(2,1)S(1)}, bf16[32,1024]{1,0:T(8,128)(2,1)S(1)}, u32[]{:S(2)}, u32[]{:S(2)}) collective-permute-start(bf16[32,1024]{1,0:T(8,128)(2,1)S(1)} %get-tuple-element.21), channel_id=1, source_target_pairs={{0,1},{1,2},{2,3},{3,0},{4,5},{5,6},{6,7},{7,4},{8,9},{9,10},{10,1... | collective-permute-start | bytes 196616 | tf_op jit(solution)/shard_map/ppermute | solution.py:115
  45.0 0.8 %collective-permute-start.8 = (bf16[32,1024]{1,0:T(8,128)(2,1)S(1)}, bf16[32,1024]{1,0:T(8,128)(2,1)S(1)}, u32[]{:S(2)}, u32[]{:S(2)}) collective-permute-start(bf16[32,1024]{1,0:T(8,128)(2,1)S(1)} %get-tuple-element.23), channel_id=1, source_target_pairs={{0,3},{1,0},{2,1},{3,2},{4,7},{5,4},{6,5},{7,6},{8,11},{9,8},{10,9... | collective-permute-start | bytes 196616 | tf_op jit(solution)/shard_map/ppermute | solution.py:115
  45.8 3.1 %collective-permute-done.9 = bf16[32,1024]{1,0:T(8,128)(2,1)S(1)} collective-permute-done((bf16[32,1024]{1,0:T(8,128)(2,1)S(1)}, bf16[32,1024]{1,0:T(8,128)(2,1)S(1)}, u32[]{:S(2)}, u32[]{:S(2)}) %collective-permute-start.9) | collective-permute-done | bytes 65568 | tf_op jit(solution)/shard_map/ppermute | solution.py:115
  51.0 1.1 %collective-permute-done.12 = bf16[2,128,1024]{2,1,0:T(8,128)(2,1)S(1)} collective-permute-done((bf16[2,128,1024]{2,1,0:T(8,128)(2,1)}, bf16[2,128,1024]{2,1,0:T(8,128)(2,1)S(1)}, u32[]{:S(2)}, u32[]{:S(2)}) %collective-permute-start.12) | collective-permute-done | bytes 524320 | tf_op jit(solution)/shard_map/ppermute | solution.py:25
  52.3 0.8 %slice_bitcast_fusion = (bf16[128,1024]{1,0:T(8,128)(2,1)}, bf16[128,1024]{1,0:T(8,128)(2,1)}) fusion(bf16[2,128,1024]{2,1,0:T(8,128)(2,1)S(1)} %add_convert_fusion), kind=kLoop, calls=%fused_computation.39 | loop fusion | bytes 1048576 | tf_op jit(solution)/shard_map/squeeze | solution.py:305
  (42 shorter events, 5.0 us)
Async XLA Ops:
  0.6 13.2 %copy-start = (s32[8,3]{0,1:T(4,128)S(1)}, s32[8,3]{0,1:T(4,128)}, u32[]{:S(2)}) copy-start(s32[8,3]{0,1:T(4,128)} %param.11) | copy-start | bytes 292
  0.6 1.0 %copy-start.3 = (bf16[128,1024]{1,0:T(8,128)(2,1)S(1)}, bf16[128,1024]{1,0:T(8,128)(2,1)}, u32[]{:S(2)}) copy-start(bf16[128,1024]{1,0:T(8,128)(2,1)} %v_ref.3) | copy-start | bytes 786436
  1.7 6.7 %copy-start.7 = (bf16[32,4096]{1,0:T(8,128)(2,1)S(1)}, bf16[32,4096]{1,0:T(8,128)(2,1)}, u32[]{:S(2)}) copy-start(bf16[32,4096]{1,0:T(8,128)(2,1)} %param.13) | copy-start | bytes 786436
  1.7 16.8 %collective-permute-start = (bf16[128,2048]{1,0:T(8,128)(2,1)S(1)}, bf16[128,2048]{1,0:T(8,128)(2,1)S(1)}, u32[]{:S(2)}, u32[]{:S(2)}) collective-permute-start(bf16[128,2048]{1,0:T(8,128)(2,1)S(1)} %constant_dynamic-update-slice_fusion), channel_id=1, source_target_pairs={{0,4},{4,8},{8,12},{12,16},{16,20},{20,24},{24,28},{1,5},{5,9},{9,... | collective-permute-start | bytes 1572872 | tf_op jit(solution)/shard_map/ppermute | solution.py:25
  3.8 14.7 %collective-permute-start.1 = (bf16[128,2048]{1,0:T(8,128)(2,1)S(1)}, bf16[128,2048]{1,0:T(8,128)(2,1)S(1)}, u32[]{:S(2)}, u32[]{:S(2)}) collective-permute-start(bf16[128,2048]{1,0:T(8,128)(2,1)S(1)} %constant_dynamic-update-slice_fusion), channel_id=1, source_target_pairs={{4,0},{8,4},{12,8},{16,12},{20,16},{24,20},{28,24},{5,1},{9,5},{13... | collective-permute-start | bytes 1572872 | tf_op jit(solution)/shard_map/ppermute | solution.py:25
  8.4 6.1 %collective-permute-start.2 = (bf16[32,1024]{1,0:T(8,128)(2,1)S(1)}, bf16[32,1024]{1,0:T(8,128)(2,1)S(1)}, u32[]{:S(2)}, u32[]{:S(2)}) collective-permute-start(bf16[32,1024]{1,0:T(8,128)(2,1)S(1)} %get-tuple-element.26), channel_id=1, source_target_pairs={{0,3},{1,0},{2,1},{3,2},{4,7},{5,4},{6,5},{7,6},{8,11},{9,8},{10,9... | collective-permute-start | bytes 196616 | tf_op jit(solution)/shard_map/ppermute | solution.py:96
  12.1 5.2 %collective-permute-start.3 = (bf16[32,1024]{1,0:T(8,128)(2,1)S(1)}, bf16[32,1024]{1,0:T(8,128)(2,1)S(1)}, u32[]{:S(2)}, u32[]{:S(2)}) collective-permute-start(bf16[32,1024]{1,0:T(8,128)(2,1)S(1)} %get-tuple-element.28), channel_id=1, source_target_pairs={{0,2},{1,3},{2,0},{3,1},{4,6},{5,7},{6,4},{7,5},{8,10},{9,11},{10,... | collective-permute-start | bytes 196616 | tf_op jit(solution)/shard_map/ppermute | solution.py:96
  12.1 6.1 %collective-permute-start.4 = (bf16[32,1024]{1,0:T(8,128)(2,1)S(1)}, bf16[32,1024]{1,0:T(8,128)(2,1)S(1)}, u32[]{:S(2)}, u32[]{:S(2)}) collective-permute-start(bf16[32,1024]{1,0:T(8,128)(2,1)S(1)} %get-tuple-element.25), channel_id=1, source_target_pairs={{0,1},{1,2},{2,3},{3,0},{4,5},{5,6},{6,7},{7,4},{8,9},{9,10},{10,1... | collective-permute-start | bytes 196616 | tf_op jit(solution)/shard_map/ppermute | solution.py:96
  13.8 9.9 %copy-start.8 = (f32[1024]{0:T(1024)}, f32[1024]{0:T(1024)S(1)}, u32[]{:S(2)}) copy-start(f32[1024]{0:T(1024)S(1)} %dynamic_slice.38) | copy-start | bytes 12292
  18.5 5.2 %copy-start.4 = (bf16[4,32,1024]{2,1,0:T(8,128)(2,1)}, bf16[4,32,1024]{2,1,0:T(8,128)(2,1)S(1)}, u32[]{:S(2)}) copy-start(bf16[4,32,1024]{2,1,0:T(8,128)(2,1)S(1)} %fusion.15) | copy-start | bytes 786436
  18.5 0.9 %copy-start.1 = (bf16[128,2048]{1,0:T(8,128)(2,1)}, bf16[128,2048]{1,0:T(8,128)(2,1)S(1)}, u32[]{:S(2)}) copy-start(bf16[128,2048]{1,0:T(8,128)(2,1)S(1)} %collective-permute-done.kp_ref.vp_ref) | copy-start | bytes 1572868
  19.4 0.8 %copy-start.2 = (bf16[128,2048]{1,0:T(8,128)(2,1)}, bf16[128,2048]{1,0:T(8,128)(2,1)S(1)}, u32[]{:S(2)}) copy-start(bf16[128,2048]{1,0:T(8,128)(2,1)S(1)} %collective-permute-done.1.kn_ref.vn_ref) | copy-start | bytes 1572868
  24.8 5.4 %collective-permute-start.5 = (f32[128,2]{0,1:T(2,128)S(1)}, f32[128,2]{0,1:T(2,128)S(1)}, u32[]{:S(2)}, u32[]{:S(2)}) collective-permute-start(f32[128,2]{0,1:T(2,128)S(1)} %pad_maximum_fusion), channel_id=1, source_target_pairs={{0,1},{1,2},{2,3},{3,0},{4,5},{5,6},{6,7},{7,4},{8,9},{9,10},{10,1... | collective-permute-start | bytes 3080 | tf_op jit(solution)/shard_map/ppermute | solution.py:72
  24.9 5.4 %collective-permute-start.6 = (f32[128,2]{0,1:T(2,128)S(1)}, f32[128,2]{0,1:T(2,128)S(1)}, u32[]{:S(2)}, u32[]{:S(2)}) collective-permute-start(f32[128,2]{0,1:T(2,128)S(1)} %pad_maximum_fusion), channel_id=1, source_target_pairs={{0,2},{1,3},{2,0},{3,1},{4,6},{5,7},{6,4},{7,5},{8,10},{9,11},{10,... | collective-permute-start | bytes 3080 | tf_op jit(solution)/shard_map/ppermute | solution.py:72
  27.0 3.8 %collective-permute-start.7 = (f32[128,2]{0,1:T(2,128)S(1)}, f32[128,2]{0,1:T(2,128)S(1)}, u32[]{:S(2)}, u32[]{:S(2)}) collective-permute-start(f32[128,2]{0,1:T(2,128)S(1)} %pad_maximum_fusion), channel_id=1, source_target_pairs={{0,3},{1,0},{2,1},{3,2},{4,7},{5,4},{6,5},{7,6},{8,11},{9,8},{10,9... | collective-permute-start | bytes 3080 | tf_op jit(solution)/shard_map/ppermute | solution.py:72
  31.6 9.2 %copy-start.5 = (bf16[128,1024]{1,0:T(8,128)(2,1)S(1)}, bf16[128,1024]{1,0:T(8,128)(2,1)}, u32[]{:S(2)}) copy-start(bf16[128,1024]{1,0:T(8,128)(2,1)} %get-tuple-element.11.o_ref) | copy-start | bytes 786436
  36.1 4.7 %copy-start.9 = (f32[1024]{0:T(1024)S(1)}, f32[1024]{0:T(1024)}, u32[]{:S(2)}) copy-start(f32[1024]{0:T(1024)} %copy-done.8) | copy-start | bytes 12292
  36.1 14.8 %collective-permute-start.11 = (bf16[2,128,1024]{2,1,0:T(8,128)(2,1)}, bf16[2,128,1024]{2,1,0:T(8,128)(2,1)S(1)}, u32[]{:S(2)}, u32[]{:S(2)}) collective-permute-start(bf16[2,128,1024]{2,1,0:T(8,128)(2,1)} %get-tuple-element.15), channel_id=1, source_target_pairs={{4,0},{8,4},{12,8},{16,12},{20,16},{24,20},{28,24},{5,1},{9,5},{13... | collective-permute-start | bytes 1572872 | tf_op jit(solution)/shard_map/ppermute | solution.py:25
  38.8 13.3 %collective-permute-start.12 = (bf16[2,128,1024]{2,1,0:T(8,128)(2,1)}, bf16[2,128,1024]{2,1,0:T(8,128)(2,1)S(1)}, u32[]{:S(2)}, u32[]{:S(2)}) collective-permute-start(bf16[2,128,1024]{2,1,0:T(8,128)(2,1)} %get-tuple-element.16), channel_id=1, source_target_pairs={{0,4},{4,8},{8,12},{12,16},{16,20},{20,24},{24,28},{1,5},{5,9},{9,... | collective-permute-start | bytes 1572872 | tf_op jit(solution)/shard_map/ppermute | solution.py:25
  40.8 11.3 %copy-start.6 = (f32[2,128,1024]{2,1,0:T(8,128)S(1)}, f32[2,128,1024]{2,1,0:T(8,128)}, u32[]{:S(2)}) copy-start(f32[2,128,1024]{2,1,0:T(8,128)} %get-tuple-element.14) | copy-start | bytes 3145732
  41.0 7.9 %collective-permute-start.9 = (bf16[32,1024]{1,0:T(8,128)(2,1)S(1)}, bf16[32,1024]{1,0:T(8,128)(2,1)S(1)}, u32[]{:S(2)}, u32[]{:S(2)}) collective-permute-start(bf16[32,1024]{1,0:T(8,128)(2,1)S(1)} %get-tuple-element.22), channel_id=1, source_target_pairs={{0,2},{1,3},{2,0},{3,1},{4,6},{5,7},{6,4},{7,5},{8,10},{9,11},{10,... | collective-permute-start | bytes 196616 | tf_op jit(solution)/shard_map/ppermute | solution.py:115
  42.0 7.5 %collective-permute-start.10 = (bf16[32,1024]{1,0:T(8,128)(2,1)S(1)}, bf16[32,1024]{1,0:T(8,128)(2,1)S(1)}, u32[]{:S(2)}, u32[]{:S(2)}) collective-permute-start(bf16[32,1024]{1,0:T(8,128)(2,1)S(1)} %get-tuple-element.21), channel_id=1, source_target_pairs={{0,1},{1,2},{2,3},{3,0},{4,5},{5,6},{6,7},{7,4},{8,9},{9,10},{10,1... | collective-permute-start | bytes 196616 | tf_op jit(solution)/shard_map/ppermute | solution.py:115
  45.0 4.9 %collective-permute-start.8 = (bf16[32,1024]{1,0:T(8,128)(2,1)S(1)}, bf16[32,1024]{1,0:T(8,128)(2,1)S(1)}, u32[]{:S(2)}, u32[]{:S(2)}) collective-permute-start(bf16[32,1024]{1,0:T(8,128)(2,1)S(1)} %get-tuple-element.23), channel_id=1, source_target_pairs={{0,3},{1,0},{2,1},{3,2},{4,7},{5,4},{6,5},{7,6},{8,11},{9,8},{10,9... | collective-permute-start | bytes 196616 | tf_op jit(solution)/shard_map/ppermute | solution.py:115
